TPU v7x, 32 devices: a whole 2x2x4 slice. The times are simulated.
32 devices in a mesh: dp: 8 (over y, x, core), tensor: 4 (over z).
Axes of the slice: x: 2, y: 2, z: 4, core: 2. Of those that a mesh axis runs over, the one named last changes fastest.
Arguments:
- acts: bfloat16 [4096, 2048], P('dp', 'tensor'), may hold values from -6 to 6
- out_grads: bfloat16 [4096, 8192], P('dp', 'tensor'), may hold values from -6 to 6
- basis_out: bfloat16 [8192, 8192], P('tensor'), may hold values from -0.0625 to 0.0625
- basis_in: bfloat16 [2048, 2048], P('tensor'), may hold values from -0.125 to 0.125
- slot_sequence: int32 [16], replicated, may hold values from 0 to 15, each once
- seq_lengths: int32 [16], replicated, may hold values from 1 to 256, 2560 in all
Outputs:
- eigenvalues: float32 [8192, 2048], P('tensor', 'dp')
Inputs may be any that keep to these rules, and one draw needn't show every extreme that they name: `slot_sequence`: every sequence number appears exactly once. `seq_lengths`: the largest count is exactly 256.
All inputs are finite; a program needn't handle non-finite values.
Results may differ from a plain program's by a relative error of at most 0.0018.
Values may be sent and summed in bfloat16 or wider, within the bound.
No kernel may reach another device: no remote copies, remote signals or barrier semaphores. Data moves between devices by JAX's collectives and lax.ppermute only.
A program may use at most 128 MiB of HBM per device.

v0:
```python
import jax
import jax.numpy as jnp
from jax import lax
from jax.sharding import PartitionSpec as P

LEN = 256


def shards(acts, out_grads, basis_out, basis_in, slot_sequence, seq_lengths):
    tok_rows = acts.shape[0]
    local_seqs = tok_rows // LEN
    seq_total = seq_lengths.shape[0]
    group_index = lax.axis_index("dp")
    slot_ids = group_index * local_seqs + jnp.arange(local_seqs, dtype=jnp.int32)
    seq_numbers = jnp.arange(seq_total, dtype=jnp.int32)
    which_seq = jnp.sum(
        jnp.where(slot_ids[:, None] == seq_numbers[None, :], slot_sequence[None, :], 0), axis=1
    )
    slot_counts = jnp.sum(
        jnp.where(which_seq[:, None] == seq_numbers[None, :], seq_lengths[None, :], 0), axis=1
    )
    row_counts = jnp.repeat(slot_counts, LEN)
    positions = jnp.arange(tok_rows, dtype=jnp.int32) % LEN
    valid_mask = positions < row_counts
    masked = jnp.where(valid_mask[:, None], out_grads, jnp.zeros_like(out_grads))
    rot_sums = lax.psum_scatter(
        jnp.einsum("oi,to->it", basis_out, masked, preferred_element_type=jnp.float32),
        "tensor",
        scatter_dimension=0,
        tiled=True,
    )
    rot_grads = rot_sums.astype(jnp.bfloat16)
    whole_acts = lax.all_gather(acts, "tensor", axis=1, tiled=True)
    rot_acts = jnp.dot(
        whole_acts,
        lax.all_gather(basis_in, "tensor", axis=0, tiled=True),
        preferred_element_type=jnp.float32,
    ).astype(jnp.bfloat16)
    squares = jnp.zeros((rot_grads.shape[0], rot_acts.shape[1]), jnp.float32)
    for slot_pos in range(local_seqs):
        grad_slot = rot_grads[:, slot_pos * LEN : (slot_pos + 1) * LEN]
        act_slot = rot_acts[slot_pos * LEN : (slot_pos + 1) * LEN]
        rotated = jnp.dot(grad_slot, act_slot, preferred_element_type=jnp.float32)
        squares = squares + rotated * rotated
    summed = lax.psum_scatter(squares, "dp", scatter_dimension=1, tiled=True)
    return summed / (seq_total * LEN)


def solution(mesh):
    return jax.shard_map(
        shards,
        mesh=mesh,
        in_specs=(
            P("dp", "tensor"),
            P("dp", "tensor"),
            P("tensor", None),
            P("tensor", None),
            P(),
            P(),
        ),
        out_specs=P("tensor", "dp"),
        check_vma=False,
    )
```

profile of v0, /device:TPU:0, one launch (start us, length us, event | category | flops | bytes accessed | tf_op | source)
XLA Modules:
  0.0 628.3 jit_solution(10822918368611207636)
XLA Ops:
  6.5 0.0 copy-start.2
  6.5 0.0 copy-start.3
  6.5 0.0 copy-start.1
  6.5 0.0 all-gather.3.cloned.1.call-start
  6.5 0.7 all-gather.3.cloned.1.call-update
  7.3 0.0 all-gather.5.cloned.1.call-start
  7.3 0.7 all-gather.5.cloned.1.call-update
  8.0 0.0 reduce-scatter.3.cloned.1.call-start
  8.1 0.0 copy-done.2
  8.1 0.2 fusion.12
  8.3 0.0 copy-done.3
  8.3 0.2 fusion.13
  8.5 0.1 broadcast_bitcast_fusion
  8.5 0.0 copy-done.1
  8.5 26.9 %convolution_bitcast_fusion = f32[8192,512]{0,1:T(8,128)} fusion(bf16[2048,8192]{1,0:T(8,128)(2,1)} %param.8, bf16[512,2048]{1,0:T(8,128)(2,1)S(1)} %copy-done.1, pred[512]{0:T(512)(128)(4,1)S(1)} %fusion.8), kind=kOutput, calls=%fused_computation.1 | convolution fusion | flops 17180917760 | bytes 52429312 | tf_op jit(solution)/shard_map/oi,to->it/dot_general | solution.py:27
  35.4 0.0 reduce-scatter.3.cloned.1.call-update
  35.5 0.2 reduce-scatter.5.cloned.1.call-start
  35.7 21.6 %all-gather.3.cloned.1.call-done = bf16[512,2048]{1,0:T(8,128)(2,1)} async-done(((bf16[512,512]{1,0:T(8,128)(2,1)}), bf16[512,2048]{1,0:T(8,128)(2,1)}) %all-gather.3.cloned.1.call-update) | async-done | bytes 2097168 | tf_op jit(solution)/shard_map/all_gather | solution.py:33
  57.3 150.0 %all-gather.5.cloned.1.call-done = bf16[2048,2048]{1,0:T(8,128)(2,1)} async-done(((bf16[512,2048]{1,0:T(8,128)(2,1)}), bf16[2048,2048]{1,0:T(8,128)(2,1)}) %all-gather.5.cloned.1.call-update) | async-done | bytes 8388624 | tf_op jit(solution)/shard_map/all_gather | solution.py:36
  207.3 9.8 %convolution_convert_fusion = bf16[512,2048]{1,0:T(8,128)(2,1)} fusion(bf16[512,2048]{1,0:T(8,128)(2,1)} %all-gather.3.cloned.1.call-done, bf16[2048,2048]{1,0:T(8,128)(2,1)} %all-gather.5.cloned.1.call-done), kind=kOutput, calls=%fused_computation.2 | convolution fusion | flops 4296015872 | bytes 12582912 | tf_op jit(solution)/shard_map/dot_general | solution.py:34
  217.2 271.2 %reduce-scatter.3.cloned.1.call-done = f32[2048,512]{0,1:T(8,128)} async-done(((f32[8192,512]{0,1:T(8,128)}), f32[2048,512]{0,1:T(8,128)}) %reduce-scatter.3.cloned.1.call-update) | async-done | bytes 4194320 | tf_op jit(solution)/shard_map/reduce_scatter | solution.py:26
  488.4 0.0 copy-start
  488.4 2.6 convert_element_type.6
  491.0 0.2 copy-done
  491.2 2.4 fusion.4
  493.6 8.3 %multiply_add_fusion = f32[2048,2048]{1,0:T(8,128)} fusion(f32[2048,2048]{1,0:T(8,128)S(1)} %fusion.4, bf16[512,2048]{1,0:T(8,128)(2,1)} %convolution_convert_fusion, bf16[2048,512]{0,1:T(8,128)(2,1)S(1)} %convert_element_type.6), kind=kOutput, calls=%fused_computation | convolution fusion | flops 2160066560 | bytes 35651584 | tf_op jit(solution)/shard_map/dot_general | solution.py:43
  501.9 0.0 reduce-scatter.5.cloned.1.call-update
  501.9 116.8 %reduce-scatter.5.cloned.1.call-done = f32[2048,256]{1,0:T(8,128)} async-done(((f32[2048,2048]{1,0:T(8,128)}), f32[2048,256]{1,0:T(8,128)}) %reduce-scatter.5.cloned.1.call-update) | async-done | bytes 2097168 | tf_op jit(solution)/shard_map/reduce_scatter | solution.py:45
  618.7 3.0 broadcast_multiply_fusion
  (3 shorter events, 0.0 us)
Async XLA Ops:
  6.5 1.5 copy-start.2
  6.5 1.7 copy-start.3
  6.5 2.0 copy-start.1
  6.5 50.8 %all-gather.3.cloned.1.call-start = ((), (), s32[]{:S(2)}) async-start(), calls=%async_computation.3 | async-start | bytes 2621440 | tf_op jit(solution)/shard_map/all_gather | solution.py:33
  7.3 200.1 %all-gather.5.cloned.1.call-start = ((), (), s32[]{:S(2)}) async-start(), calls=%async_computation.4 | async-start | bytes 10485760 | tf_op jit(solution)/shard_map/all_gather | solution.py:36
  8.0 480.3 %reduce-scatter.3.cloned.1.call-start = ((), (), s32[]{:S(2)}) async-start(), calls=%async_computation.2 | async-start | bytes 20971520 | tf_op jit(solution)/shard_map/reduce_scatter | solution.py:26
  35.5 583.3 %reduce-scatter.5.cloned.1.call-start = ((), (), s32[]{:S(2)}) async-start(), calls=%async_computation.5 | async-start | bytes 18874368 | tf_op jit(solution)/shard_map/reduce_scatter | solution.py:45
  488.4 2.9 copy-start
Sparse Core Ops, SparseCore 0:
  8.9 48.3 all-gather.2
  58.9 148.4 all-gather.4
  209.7 278.6 reduce-scatter.2
  502.1 116.6 reduce-scatter.4
where the time goes:
time: 628 us
  waiting for transfers between devices  561 us (89%)
  matrix products  47.4 us (8%)
  between operations  13.2 us (2%)
    reduce_scatter x1, waiting for transfers between devices, shards(): lax.psum_scatter(jnp.einsum('oi,to->it', basis_out, masked, preferred_ele...  271 us
    all_gather x1, waiting for transfers between devices, shards(): lax.all_gather(basis_in, 'tensor', axis=0, tiled=True)  150 us
    reduce_scatter x1, waiting for transfers between devices, shards(): summed = lax.psum_scatter(squares, 'dp', scatter_dimension=1, tiled=True)  117 us
    dot_general x1, matrix products, shards(): jnp.einsum('oi,to->it', basis_out, masked, preferred_element_type=jnp.flo...  26.9 us
    all_gather x1, waiting for transfers between devices, shards(): whole_acts = lax.all_gather(acts, 'tensor', axis=1, tiled=True)  21.6 us
  transfers between devices with their start and end apart: 4, of which 4 were waited for; matrix products, arithmetic and copies ran while one was open for 6% of the time, Pallas kernels for 0%

commit v1 on v0

v1 whole, which is shorter than its diff:
```python
import jax
import jax.numpy as jnp
from jax import lax
from jax.sharding import PartitionSpec as P

LEN = 256
VALID_NUM, VALID_DEN = 5, 8


def redistribute(x, dp):
    slots = x.shape[0] // LEN
    width = x.shape[1]
    x = x.reshape(slots, LEN // dp, dp, width).transpose(2, 0, 1, 3).reshape(-1, width)
    return lax.all_to_all(x, "dp", 0, 0, tiled=True)


def shards(acts, out_grads, basis_out, basis_in, slot_sequence, seq_lengths, *, dp):
    tok_rows = acts.shape[0]
    local_slots = tok_rows // LEN
    nseq = seq_lengths.shape[0]
    per = LEN // dp
    total = nseq * LEN * VALID_NUM // VALID_DEN
    cap = -(-(total + nseq * (dp - 1)) // dp)
    cap = -(-cap // 16) * 16
    group = lax.axis_index("dp")

    counts = seq_lengths[slot_sequence]
    groups = jnp.arange(dp, dtype=jnp.int32)
    kept = jnp.clip((counts[:, None] - groups[None, :] + dp - 1) // dp, 0, per)
    ends = jnp.cumsum(kept, axis=0)
    starts = ends - kept

    my_ends = ends[:, group]
    my_starts = starts[:, group]
    rows = jnp.arange(cap, dtype=jnp.int32)
    slot_of = jnp.sum((my_ends[None, :] <= rows[:, None]).astype(jnp.int32), axis=1)
    in_use = slot_of < nseq
    slot_c = jnp.minimum(slot_of, nseq - 1)
    src = jnp.clip(slot_c * per + rows - my_starts[slot_c], 0, nseq * per - 1)

    grads_r = redistribute(out_grads, dp)
    grads_p = jnp.take(grads_r, src, axis=0, mode="clip")
    grads_p = jnp.where(in_use[:, None], grads_p, jnp.zeros_like(grads_p))
    acts_r = redistribute(acts, dp)
    acts_p = jnp.take(acts_r, src, axis=0, mode="clip")

    act_part = jnp.dot(acts_p, basis_in, preferred_element_type=jnp.float32)
    in_cols = act_part.shape[1] // dp
    act_part = act_part.reshape(cap, dp, in_cols).transpose(1, 0, 2).reshape(-1, in_cols)
    act_part = lax.all_to_all(act_part, "dp", 0, 0, tiled=True)
    rot_acts = lax.psum(act_part, "tensor").astype(jnp.bfloat16)

    grad_part = jnp.dot(grads_p, basis_out, preferred_element_type=jnp.float32)
    rot_grads = lax.psum_scatter(grad_part, "tensor", scatter_dimension=1, tiled=True)
    rot_grads = rot_grads.astype(jnp.bfloat16)
    all_grads = lax.all_gather(rot_grads, "dp", axis=0, tiled=True)

    js = jnp.arange(per, dtype=jnp.int32)
    pick = groups[None, :, None] * cap + starts[:, :, None] + js[None, None, :]
    live = js[None, None, :] < kept[:, :, None]
    pick = jnp.where(live, pick, 0).reshape(-1)
    live = live.reshape(-1)
    grads_u = jnp.take(all_grads, pick, axis=0, mode="clip")
    acts_u = jnp.take(rot_acts, pick, axis=0, mode="clip")
    acts_u = jnp.where(live[:, None], acts_u, jnp.zeros_like(acts_u))

    squares = jnp.zeros((all_grads.shape[1], rot_acts.shape[1]), jnp.float32)
    for slot in range(nseq):
        g = grads_u[slot * LEN : (slot + 1) * LEN]
        a = acts_u[slot * LEN : (slot + 1) * LEN]
        rotated = lax.dot_general(g, a, (((0,), (0,)), ((), ())), preferred_element_type=jnp.float32)
        squares = squares + rotated * rotated
    return squares / (nseq * LEN)


def solution(mesh):
    dp = mesh.shape["dp"]

    def body(*args):
        return shards(*args, dp=dp)

    return jax.shard_map(
        body,
        mesh=mesh,
        in_specs=(
            P("dp", "tensor"),
            P("dp", "tensor"),
            P("tensor", None),
            P("tensor", None),
            P(),
            P(),
        ),
        out_specs=P("tensor", "dp"),
        check_vma=False,
    )
```

time: 628 us -> 520 us (0.83)
  waiting for transfers between devices: 561 us -> 249 us
  blocking collectives: 0 us -> 110 us
  local copies, waits for them, and re-layouts: 0.29 us -> 70.9 us
  starting transfers between devices: 0.3 us -> 9.8 us
  other arithmetic: 6.06 us -> 15.5 us
    reduce_scatter x2 -> x1, waiting for transfers between devices: 388 us -> 186 us  [shards(): lax.psum_scatter(grad_part, 'tensor', scatter_dimension=1, tiled=True)]
    all_gather x2 -> x1, waiting for transfers between devices: 172 us -> 0.02 us  [shards(): all_grads = lax.all_gather(rot_grads, 'dp', axis=0, tiled=True)]
    psum x0 -> x1, blocking collectives: none -> 96.5 us  [shards(): rot_acts = lax.psum(act_part, 'tensor').astype(jnp.bfloat16)]
    gather x0 -> x6, local copies, waits for them, and re-layouts: none -> 64.3 us  [the longest x1 37.6 us: shards(): grads_u = jnp.take(all_grads, pick, axis=0, mode='clip')]
    all_to_all x0 -> x2, waiting for transfers between devices: none -> 62.1 us  [the longest x1 47.5 us: shards(): act_part = lax.all_to_all(act_part, 'dp', 0, 0, tiled=True)]
    all_to_all x0 -> x1, blocking collectives: none -> 13.8 us  [redistribute(): return lax.all_to_all(x, 'dp', 0, 0, tiled=True)]
    gather x0 -> x6, other arithmetic: none -> 10 us  [the longest x3 10 us: shards(): src = jnp.clip(slot_c * per + rows - my_starts[slot_c], 0, nseq * per - 1)]
    all_to_all x0 -> x2, starting transfers between devices: none -> 9.72 us  [the longest x1 5.33 us: redistribute(): return lax.all_to_all(x, 'dp', 0, 0, tiled=True)]
  transfers between devices with their start and end apart: 4 -> 4, of which waited for: 4 -> 3; matrix products, arithmetic and copies ran while one was open for 6% -> 7% of each run, Pallas kernels for 0% -> 0%
where the time goes in v1:
time: 520 us
  waiting for transfers between devices  249 us (48%)
  blocking collectives  110 us (21%)
  local copies, waits for them, and re-layouts  70.9 us (14%)
  matrix products  50.8 us (10%)
  other arithmetic  15.5 us (3%)
  between operations  13.7 us (3%)
  starting transfers between devices  9.8 us (2%)
    reduce_scatter x1, waiting for transfers between devices, shards(): lax.psum_scatter(grad_part, 'tensor', scatter_dimension=1, tiled=True)  186 us
    psum x1, blocking collectives, shards(): rot_acts = lax.psum(act_part, 'tensor').astype(jnp.bfloat16)  96.5 us
    all_to_all x1, waiting for transfers between devices, shards(): act_part = lax.all_to_all(act_part, 'dp', 0, 0, tiled=True)  47.5 us
    gather x1, local copies, waits for them, and re-layouts, shards(): grads_u = jnp.take(all_grads, pick, axis=0, mode='clip')  37.6 us
    dot_general x16, matrix products, shards(): lax.dot_general(g, a, (((0,), (0,)), ((), ())), preferred_element_type=jn...  29.8 us
    dot_general x1, matrix products, shards(): grad_part = jnp.dot(grads_p, basis_out, preferred_element_type=jnp.float32)  20.1 us
    gather x1, local copies, waits for them, and re-layouts, shards(): acts_u = jnp.take(rot_acts, pick, axis=0, mode='clip')  17 us
    all_to_all x1, waiting for transfers between devices, redistribute(): return lax.all_to_all(x, 'dp', 0, 0, tiled=True)  14.6 us
  transfers between devices with their start and end apart: 4, of which 3 were waited for; matrix products, arithmetic and copies ran while one was open for 7% of the time, Pallas kernels for 0%

profile of v1, /device:TPU:0, one launch (start us, length us, event | category | flops | bytes accessed | tf_op | source)
XLA Modules:
  0.0 519.7 jit_solution(9904804231336584999)
XLA Ops:
  6.5 4.2 copy.16
  10.8 5.3 %all-to-all-start = ((bf16[8,64,2048]{2,1,0:T(8,128)(2,1)}), bf16[8,64,2048]{2,1,0:T(8,128)(2,1)}, u32[]{:S(2)}, u32[]{:S(2)}) async-start(bf16[8,64,2048]{2,1,0:T(8,128)(2,1)} %bitcast.40), calls=%async_computation | async-start | bytes 4194304 | tf_op jit(solution)/shard_map/all_to_all | solution.py:14
  16.2 0.7 gather_fusion
  17.3 0.8 fusion.60
  18.1 4.3 fusion.57
  22.4 5.7 %select_select_fusion = s32[336]{0:T(512)S(1)} fusion(pred[336]{0:T(512)(128)(4,1)S(1)} %get-tuple-element.13, pred[336]{0:T(512)(128)(4,1)S(1)} %get-tuple-element.12, pred[336]{0:T(512)(128)(4,1)S(1)} %get-tuple-element.11, pred[336]{0:T(512)(128)(4,1)S(1)} %get-tuple-element.10, pred[336]{0:T(512)(128)(4,1)S(1)} %get-tuple-element.9, ...), kind=kLoop, calls=%fused_computation.112 | loop fusion | flops 3024 | bytes 5748 | tf_op jit(solution)/shard_map/gather | solution.py:39
  28.2 14.6 %all-to-all-done = bf16[8,64,2048]{2,1,0:T(8,128)(2,1)} async-done(((bf16[8,64,2048]{2,1,0:T(8,128)(2,1)}), bf16[8,64,2048]{2,1,0:T(8,128)(2,1)}, u32[]{:S(2)}, u32[]{:S(2)}) %all-to-all-start) | async-done | bytes 2097184 | tf_op jit(solution)/shard_map/all_to_all | solution.py:14
  42.8 6.2 %gather_fusion.1 = bf16[336,2048]{1,0:T(8,128)(2,1)S(1)} fusion(bf16[512,2048]{1,0:T(8,128)(2,1)} %bitcast.3, s32[1024]{0:T(1024)S(1)} %pad_clamp_fusion), kind=kCustom, calls=%fused_computation.1 | custom fusion | bytes 2753856 | tf_op jit(solution)/shard_map/jit(_take)/gather | solution.py:42
  49.1 20.1 %fusion.16 = f32[336,8192]{1,0:T(8,128)} fusion(bf16[2048,8192]{1,0:T(8,128)(2,1)} %param.8, bf16[336,2048]{1,0:T(8,128)(2,1)S(1)} %gather_fusion.1, pred[336]{0:T(512)(128)(4,1)S(1)} %broadcast_compare_fusion), kind=kOutput, calls=%fused_computation.39 | convolution fusion | flops 11274977280 | bytes 45941072 | tf_op jit(solution)/shard_map/dot_general | solution.py:53
  69.2 186.5 %reduce-scatter.2.cloned.1.call-done = f32[336,2048]{1,0:T(8,128)} async-done(((f32[336,8192]{1,0:T(8,128)}), f32[336,2048]{1,0:T(8,128)}) %reduce-scatter.2.cloned.1.call-update) | async-done | bytes 2752528 | tf_op jit(solution)/shard_map/reduce_scatter | solution.py:54
  255.7 3.1 convert_element_type.10
  259.0 13.8 %all_to_all.33 = bf16[8,64,512]{2,1,0:T(8,128)(2,1)S(1)} all-to-all(bf16[8,64,512]{2,1,0:T(8,128)(2,1)S(1)} %bitcast.42), channel_id=1, replica_groups=mesh['dp'=8,'tensor'=4] {'dp'}, dimensions={0} | all-to-all | bytes 1048576 | tf_op jit(solution)/shard_map/all_to_all | solution.py:14
  272.8 2.0 gather_fusion.3
  274.9 0.9 fusion.61
  275.7 1.8 copy.21
  277.6 4.4 all-to-all-start.2
  282.4 47.5 %all-to-all-done.2 = f32[8,336,256]{2,1,0:T(8,128)} async-done(((f32[8,336,256]{2,1,0:T(8,128)}), f32[8,336,256]{2,1,0:T(8,128)}, u32[]{:S(2)}, u32[]{:S(2)}) %all-to-all-start.2) | async-done | bytes 2752544 | tf_op jit(solution)/shard_map/all_to_all | solution.py:50
  329.8 96.5 %all-reduce.1 = bf16[2688,256]{1,0:T(8,128)(2,1)S(1)} all-reduce(f32[2688,256]{1,0:T(8,128)} %bitcast.25), channel_id=1, replica_groups=mesh['dp'=8,'tensor'=4] {'tensor'}, use_global_device_ids=true, to_apply=%region_3.4 | all-reduce | flops 688128 | bytes 4128768 | tf_op jit(solution)/shard_map/psum | solution.py:51
  426.3 17.0 %gather_fusion.4 = bf16[4096,256]{1,0:T(8,128)(2,1)} fusion(bf16[2688,256]{1,0:T(8,128)(2,1)S(1)} %all-reduce.1, s32[4096]{0:T(1024)S(1)} %broadcast_clamp_fusion), kind=kCustom, calls=%fused_computation.4 | custom fusion | bytes 4210688 | tf_op jit(solution)/shard_map/jit(_take)/gather | solution.py:64
  443.3 1.9 broadcast_select_fusion
  445.3 37.6 %gather_fusion.2 = bf16[4096,2048]{1,0:T(8,128)(2,1)} fusion(bf16[2688,2048]{1,0:T(8,128)(2,1)} %all-gather.2.cloned.1.call-done, s32[4096]{0:T(1024)S(1)} %broadcast_clamp_fusion), kind=kCustom, calls=%fused_computation.2 | custom fusion | bytes 33570816 | tf_op jit(solution)/shard_map/jit(_take)/gather | solution.py:63
  482.9 1.9 convolution_multiply_fusion.10
  484.8 2.1 convolution_multiply_fusion.11
  486.9 3.6 convolution_multiply_fusion.12
  490.5 3.1 convolution_multiply_fusion.13
  493.6 3.0 convolution_multiply_fusion.14
  496.6 1.7 convolution_multiply_fusion.5
  499.8 0.5 convolution_multiply_fusion.2
  500.3 0.5 convolution_multiply_fusion.3
  501.8 5.2 %fusion.4 = f32[2048,256]{1,0:T(8,128)} fusion(f32[2048,256]{1,0:T(8,128)S(1)} %convolution_multiply_fusion.10, f32[2048,256]{1,0:T(8,128)S(1)} %convolution_multiply_fusion.11, f32[2048,256]{1,0:T(8,128)} %convolution_multiply_fusion.12, f32[2048,256]{1,0:T(8,128)} %convolution_multiply_fusion.13, f32[2048,256]{1,0:T(8,128)} %convolution_multiply_fusion.14, ...), kind=kOutput, calls=%fused_computation.26 | convolution fusion | flops 271581184 | bytes 13762560 | tf_op jit(solution)/shard_map/dot_general | solution.py:71
  507.0 2.6 fusion.9
  509.6 3.3 fusion.15
  (43 shorter events, 3.7 us)
Async XLA Ops:
  6.5 268.3 %copy-start = (bf16[512,2048]{1,0:T(8,128)(2,1)S(1)}, bf16[512,2048]{1,0:T(8,128)(2,1)}, u32[]{:S(2)}) copy-start(bf16[512,2048]{1,0:T(8,128)(2,1)} %param.9) | copy-start | bytes 6291460
  10.7 5.4 %copy-start.6 = (s32[16]{0:T(128)S(1)}, s32[16]{0:T(128)}, u32[]{:S(2)}) copy-start(s32[16]{0:T(128)} %param.10) | copy-start | bytes 196
  10.8 5.4 %copy-start.2 = (s32[16]{0:T(128)S(1)}, s32[16]{0:T(128)}, u32[]{:S(2)}) copy-start(s32[16]{0:T(128)} %param.11) | copy-start | bytes 196
  10.8 32.0 %all-to-all-start = ((bf16[8,64,2048]{2,1,0:T(8,128)(2,1)}), bf16[8,64,2048]{2,1,0:T(8,128)(2,1)}, u32[]{:S(2)}, u32[]{:S(2)}) async-start(bf16[8,64,2048]{2,1,0:T(8,128)(2,1)} %bitcast.40), calls=%async_computation | async-start | bytes 4194304 | tf_op jit(solution)/shard_map/all_to_all | solution.py:14
  16.1 239.6 %reduce-scatter.2.cloned.1.call-start = ((), (), s32[]{:S(2)}) async-start(), calls=%async_computation.4 | async-start | bytes 13762560 | tf_op jit(solution)/shard_map/reduce_scatter | solution.py:54
  69.2 189.6 %copy-start.5 = (bf16[512,512]{1,0:T(8,128)(2,1)S(1)}, bf16[512,512]{1,0:T(8,128)(2,1)}, u32[]{:S(2)}) copy-start(bf16[512,512]{1,0:T(8,128)(2,1)} %param.6) | copy-start | bytes 1572868
  69.2 376.1 %all-gather.2.cloned.1.call-start = ((), (), s32[]{:S(2)}) async-start(), calls=%async_computation.5 | async-start | bytes 12386304 | tf_op jit(solution)/shard_map/all_gather | solution.py:56
  277.6 52.3 %all-to-all-start.2 = ((f32[8,336,256]{2,1,0:T(8,128)}), f32[8,336,256]{2,1,0:T(8,128)}, u32[]{:S(2)}, u32[]{:S(2)}) async-start(f32[8,336,256]{2,1,0:T(8,128)} %bitcast.39), calls=%async_computation.3 | async-start | bytes 5505024 | tf_op jit(solution)/shard_map/all_to_all | solution.py:50
  445.3 61.7 %copy-start.4 = (bf16[4096,256]{1,0:T(8,128)(2,1)}, bf16[4096,256]{1,0:T(8,128)(2,1)S(1)}, u32[]{:S(2)}) copy-start(bf16[4096,256]{1,0:T(8,128)(2,1)S(1)} %broadcast_select_fusion) | copy-start | bytes 6291460
  482.9 15.4 %copy-start.3 = (bf16[4096,2048]{1,0:T(8,128)(2,1)S(1)}, bf16[4096,2048]{1,0:T(8,128)(2,1)}, u32[]{:S(2)}) copy-start(bf16[4096,2048]{1,0:T(8,128)(2,1)} %gather_fusion.2) | copy-start | bytes 50331652
  509.6 3.3 copy-start.1
Sparse Core Ops, SparseCore 0:
  69.3 186.3 reduce-scatter.1
  258.9 88.7 all-gather.1

commit v2 on v1

v2 whole, which is shorter than its diff:
```python
import jax
import jax.numpy as jnp
from jax import lax
from jax.sharding import PartitionSpec as P

LEN = 256
VALID_NUM, VALID_DEN = 5, 8
CHUNKS = 4


def redistribute(x, dp):
    slots = x.shape[0] // LEN
    width = x.shape[1]
    x = x.reshape(slots, LEN // dp, dp, width).transpose(2, 0, 1, 3).reshape(-1, width)
    return lax.all_to_all(x, "dp", 0, 0, tiled=True)


def shards(acts, out_grads, basis_out, basis_in, slot_sequence, seq_lengths, *, dp, tp):
    tok_rows = acts.shape[0]
    nseq = seq_lengths.shape[0]
    per = LEN // dp
    total = nseq * LEN * VALID_NUM // VALID_DEN
    cap = -(-(total + nseq * (dp - 1)) // dp)
    cap = -(-cap // 16) * 16
    rows_all = dp * cap
    group = lax.axis_index("dp")

    counts = seq_lengths[slot_sequence]
    groups = jnp.arange(dp, dtype=jnp.int32)
    kept = jnp.clip((counts[:, None] - groups[None, :] + dp - 1) // dp, 0, per)
    ends = jnp.cumsum(kept, axis=0)
    starts = ends - kept

    my_ends = ends[:, group]
    my_starts = starts[:, group]
    rows = jnp.arange(cap, dtype=jnp.int32)
    slot_of = jnp.sum((my_ends[None, :] <= rows[:, None]).astype(jnp.int32), axis=1)
    in_use = slot_of < nseq
    slot_c = jnp.minimum(slot_of, nseq - 1)
    src = jnp.clip(slot_c * per + rows - my_starts[slot_c], 0, nseq * per - 1)

    grads_r = redistribute(out_grads, dp)
    grads_p = jnp.take(grads_r, src, axis=0, mode="clip")
    grads_p = jnp.where(in_use[:, None], grads_p, jnp.zeros_like(grads_p))
    acts_r = redistribute(acts, dp)
    acts_p = jnp.take(acts_r, src, axis=0, mode="clip")

    act_part = jnp.dot(acts_p, basis_in, preferred_element_type=jnp.float32)
    act_sum = lax.psum_scatter(act_part, "tensor", scatter_dimension=1, tiled=True)
    act_whole = lax.all_gather(act_sum.astype(jnp.bfloat16), "tensor", axis=1, tiled=True)
    in_cols = act_whole.shape[1] // dp
    act_whole = act_whole.reshape(cap, dp, in_cols).transpose(1, 0, 2).reshape(-1, in_cols)
    rot_acts = lax.all_to_all(act_whole, "dp", 0, 0, tiled=True)

    lo = groups[None, :] * cap + starts
    win = jnp.minimum(lo, rows_all - per)
    js = jnp.arange(per, dtype=jnp.int32)
    at = win[:, :, None] + js[None, None, :]
    live = (at >= lo[:, :, None]) & (at < (lo + kept)[:, :, None])

    def windows(rows_of, slot):
        return jnp.concatenate([lax.dynamic_slice_in_dim(rows_of, win[slot, g], per, 0) for g in range(dp)])

    units = cap // 16
    bounds = [16 * (c * units // CHUNKS) for c in range(CHUNKS + 1)]
    pieces = []
    for c in range(CHUNKS):
        if c == 1:
            grads_p, rot_acts = lax.optimization_barrier((grads_p, rot_acts))
        block = grads_p[bounds[c] : bounds[c + 1]]
        grad_part = jnp.dot(block, basis_out, preferred_element_type=jnp.float32)
        rot_grads = lax.psum_scatter(grad_part, "tensor", scatter_dimension=1, tiled=True)
        rot_grads = rot_grads.astype(jnp.bfloat16)
        sent = jnp.broadcast_to(rot_grads[None], (dp,) + rot_grads.shape).reshape(-1, rot_grads.shape[1])
        got = lax.all_to_all(sent, "dp", 0, 0, tiled=True)
        pieces.append(got.reshape(dp, -1, got.shape[1]))
    all_grads = jnp.concatenate(pieces, axis=1).reshape(rows_all, -1)

    def one_slot(slot, squares):
        g_s = windows(all_grads, slot)
        a_s = windows(rot_acts, slot)
        a_s = jnp.where(live[slot].reshape(-1, 1), a_s, jnp.zeros_like(a_s))
        rotated = lax.dot_general(g_s, a_s, (((0,), (0,)), ((), ())), preferred_element_type=jnp.float32)
        return squares + rotated * rotated

    squares = jnp.zeros((all_grads.shape[1], rot_acts.shape[1]), jnp.float32)
    squares = lax.fori_loop(0, nseq, one_slot, squares)
    return squares / (nseq * LEN)


def solution(mesh):
    dp = mesh.shape["dp"]
    tp = mesh.shape["tensor"]

    def body(*args):
        return shards(*args, dp=dp, tp=tp)

    return jax.shard_map(
        body,
        mesh=mesh,
        in_specs=(
            P("dp", "tensor"),
            P("dp", "tensor"),
            P("tensor", None),
            P("tensor", None),
            P(),
            P(),
        ),
        out_specs=P("tensor", "dp"),
        check_vma=False,
    )
```

time: 520 us -> 849 us (1.63)
  loops' own time: 0 us -> 237 us
  local copies, waits for them, and re-layouts: 70.9 us -> 160 us
  blocking collectives: 110 us -> 22.3 us
  matrix products: 50.8 us -> 117 us
  starting transfers between devices: 9.8 us -> 27.4 us
  other arithmetic: 15.5 us -> 31.5 us
  waiting for transfers between devices: 249 us -> 233 us
    another operation x0 -> x1, loops' own time: none -> 237 us  [shards(): squares = lax.fori_loop(0, nseq, one_slot, squares)]
    while x0 -> x224, local copies, waits for them, and re-layouts: none -> 110 us
    psum x1 -> x0, blocking collectives: 96.5 us -> none  [shards(): rot_acts = lax.psum(act_part, 'tensor').astype(jnp.bfloat16)]
    dot_general x17 -> x20, matrix products: 49.9 us -> 115 us  [the longest x4 60.9 us: shards(): grad_part = jnp.dot(block, basis_out, preferred_element_type=jnp.float32)]
    gather x2 -> x0, local copies, waits for them, and re-layouts: 54.6 us -> none  [the longest x1 37.6 us: shards(): grads_u = jnp.take(all_grads, pick, axis=0, mode='clip')]
    reduce_scatter x1 -> x4, waiting for transfers between devices: 186 us -> 132 us  [shards(): lax.psum_scatter(grad_part, 'tensor', scatter_dimension=1, tiled=True)]
    reduce_scatter x0 -> x1, waiting for transfers between devices: none -> 18.9 us  [shards(): lax.psum_scatter(act_part, 'tensor', scatter_dimension=1, tiled=True)]
    all_gather x1, waiting for transfers between devices: 0.02 us -> 17.7 us  [shards(): lax.all_gather(act_sum.astype(jnp.bfloat16), 'tensor', axis=1, tiled=True)]
  transfers between devices with their start and end apart: 4 -> 12, of which waited for: 3 -> 7; matrix products, arithmetic and copies ran while one was open for 7% -> 11% of each run, Pallas kernels for 0% -> 0%
where the time goes in v2:
time: 849 us; the launch traced here: 841 us
  loops' own time  237 us (28%)
  waiting for transfers between devices  233 us (27%)
  local copies, waits for them, and re-layouts  160 us (19%)
  matrix products  117 us (14%)
  other arithmetic  31.5 us (4%)
  starting transfers between devices  27.4 us (3%)
  blocking collectives  22.3 us (3%)
  between operations  13.7 us (2%)
    another operation x1, loops' own time, shards(): squares = lax.fori_loop(0, nseq, one_slot, squares)  237 us
    reduce_scatter x4, waiting for transfers between devices, shards(): lax.psum_scatter(grad_part, 'tensor', scatter_dimension=1, tiled=True)  132 us
    while x224, local copies, waits for them, and re-layouts  110 us
    dot_general x4, matrix products, shards(): grad_part = jnp.dot(block, basis_out, preferred_element_type=jnp.float32)  60.9 us
    dot_general x16, matrix products, one_slot(): lax.dot_general(g_s, a_s, (((0,), (0,)), ((), ())), preferred_element_typ...  53.7 us
    all_to_all x4, waiting for transfers between devices, shards(): got = lax.all_to_all(sent, 'dp', 0, 0, tiled=True)  37.7 us
    all_to_all x2, waiting for transfers between devices, redistribute(): return lax.all_to_all(x, 'dp', 0, 0, tiled=True)  26.6 us
    all_to_all x1, blocking collectives, shards(): rot_acts = lax.all_to_all(act_whole, 'dp', 0, 0, tiled=True)  22.3 us
  transfers between devices with their start and end apart: 12, of which 7 were waited for; matrix products, arithmetic and copies ran while one was open for 11% of the time, Pallas kernels for 0%

profile of v2, /device:TPU:0, one launch (start us, length us, event | category | flops | bytes accessed | tf_op | source)
XLA Modules:
  0.0 841.4 jit_solution(1465902554699397482)
XLA Ops:
  8.7 5.2 all-to-all-start.2
  17.2 4.3 fusion.22
  21.5 5.7 select_select_fusion
  35.8 4.1 all-to-all-start
  40.0 26.6 %all-to-all-done = bf16[8,64,2048]{2,1,0:T(8,128)(2,1)S(1)} async-done(((bf16[8,64,2048]{2,1,0:T(8,128)(2,1)}), bf16[8,64,2048]{2,1,0:T(8,128)(2,1)S(1)}, u32[]{:S(2)}, u32[]{:S(2)}) %all-to-all-start) | async-done | bytes 2097184 | tf_op jit(solution)/shard_map/all_to_all | solution.py:15
  69.0 18.9 %reduce-scatter.8.cloned.1.call-done = f32[336,512]{1,0:T(8,128)} async-done(((f32[336,2048]{1,0:T(8,128)}), f32[336,512]{1,0:T(8,128)}) %reduce-scatter.8.cloned.1.call-update) | async-done | bytes 688144 | tf_op jit(solution)/shard_map/reduce_scatter | solution.py:49
  90.0 15.4 %fusion.7 = f32[80,8192]{1,0:T(8,128)} fusion(bf16[2048,8192]{1,0:T(8,128)(2,1)} %param.10, bf16[336,2048]{1,0:T(8,128)(2,1)S(1)} %broadcast_select_fusion), kind=kOutput, calls=%fused_computation.40 | convolution fusion | flops 2684354560 | bytes 36503552 | tf_op jit(solution)/shard_map/dot_general | solution.py:71
  105.5 17.7 %all-gather.2.cloned.1.call-done = bf16[336,2048]{1,0:T(8,128)(2,1)} async-done(((bf16[336,512]{1,0:T(8,128)(2,1)}), bf16[336,2048]{1,0:T(8,128)(2,1)}) %all-gather.2.cloned.1.call-update) | async-done | bytes 1376272 | tf_op jit(solution)/shard_map/all_gather | solution.py:50
  124.7 22.3 %all_to_all.57 = bf16[8,336,256]{2,1,0:T(8,128)(2,1)S(1)} all-to-all(bf16[8,336,256]{2,1,0:T(8,128)(2,1)S(1)} %bitcast.72), channel_id=1, replica_groups=mesh['dp'=8,'tensor'=4] {'dp'}, dimensions={0} | all-to-all | bytes 2752512 | tf_op jit(solution)/shard_map/all_to_all | solution.py:53
  147.0 15.2 %fusion.11 = f32[80,8192]{1,0:T(8,128)} fusion(bf16[2048,8192]{1,0:T(8,128)(2,1)} %param.10, bf16[336,2048]{1,0:T(8,128)(2,1)S(1)} %broadcast_select_fusion), kind=kOutput, calls=%fused_computation.44 | convolution fusion | flops 2684354560 | bytes 36503552 | tf_op jit(solution)/shard_map/dot_general | solution.py:71
  162.5 15.2 %fusion.9 = f32[80,8192]{1,0:T(8,128)} fusion(bf16[2048,8192]{1,0:T(8,128)(2,1)} %param.10, bf16[336,2048]{1,0:T(8,128)(2,1)S(1)} %broadcast_select_fusion), kind=kOutput, calls=%fused_computation.42 | convolution fusion | flops 2684354560 | bytes 36503552 | tf_op jit(solution)/shard_map/dot_general | solution.py:71
  180.7 4.4 all-to-all-start.1
  185.2 15.1 %fusion.5 = f32[96,8192]{1,0:T(8,128)} fusion(bf16[2048,8192]{1,0:T(8,128)(2,1)} %param.10, bf16[336,2048]{1,0:T(8,128)(2,1)S(1)} %broadcast_select_fusion), kind=kOutput, calls=%fused_computation.38 | convolution fusion | flops 3221225472 | bytes 37093376 | tf_op jit(solution)/shard_map/dot_general | solution.py:71
  200.3 30.6 %reduce-scatter.10.cloned.1.call-done = f32[80,2048]{1,0:T(8,128)} async-done(((f32[80,8192]{1,0:T(8,128)}), f32[80,2048]{1,0:T(8,128)}) %reduce-scatter.10.cloned.1.call-update) | async-done | bytes 655376 | tf_op jit(solution)/shard_map/reduce_scatter | solution.py:72
  233.9 4.4 all-to-all-start.4
  238.2 46.6 %reduce-scatter.12.cloned.1.call-done = f32[80,2048]{1,0:T(8,128)} async-done(((f32[80,8192]{1,0:T(8,128)}), f32[80,2048]{1,0:T(8,128)}) %reduce-scatter.12.cloned.1.call-update) | async-done | bytes 655376 | tf_op jit(solution)/shard_map/reduce_scatter | solution.py:72
  287.9 4.4 all-to-all-start.5
  292.3 54.7 %reduce-scatter.14.cloned.1.call-done = f32[96,2048]{1,0:T(8,128)} async-done(((f32[96,8192]{1,0:T(8,128)}), f32[96,2048]{1,0:T(8,128)}) %reduce-scatter.14.cloned.1.call-update) | async-done | bytes 786448 | tf_op jit(solution)/shard_map/reduce_scatter | solution.py:72
  350.3 4.5 all-to-all-start.6
  354.9 37.6 %all-to-all-done.6 = bf16[8,96,2048]{2,1,0:T(8,128)(2,1)} async-done(((bf16[8,96,2048]{2,1,0:T(8,128)(2,1)}), bf16[8,96,2048]{2,1,0:T(8,128)(2,1)}, u32[]{:S(2)}, u32[]{:S(2)}) %all-to-all-start.6) | async-done | bytes 3145760 | tf_op jit(solution)/shard_map/all_to_all | solution.py:75
  392.6 10.6 %pad_maximum_fusion = bf16[8,336,2048]{2,1,0:T(8,128)(2,1)} fusion(bf16[8,96,2048]{2,1,0:T(8,128)(2,1)} %all-to-all-done.6, bf16[8,80,2048]{2,1,0:T(8,128)(2,1)} %all-to-all-done.5, bf16[8,80,2048]{2,1,0:T(8,128)(2,1)} %all-to-all-done.4, bf16[8,80,2048]{2,1,0:T(8,128)(2,1)} %all-to-all-done.1), kind=kLoop, calls=%fused_computation.34 | loop fusion | flops 44040192 | bytes 22020096 | tf_op jit(solution)/shard_map/concatenate | solution.py:77
  403.2 428.2 %while.14 = (s32[]{:T(128)}, f32[2048,256]{1,0:T(8,128)}, s32[16,8]{0,1:T(8,128)S(1)}, bf16[2688,2048]{1,0:T(8,128)(2,1)}, pred[16,8,32]{2,1,0:T(8,128)(4,1)S(1)...) while((s32[]{:T(128)}, f32[2048,256]{1,0:T(8,128)}, ...), condition=%wide.region_8.9_spmd.clone, body=%wide.region_7.8_spmd.clone.sunk | while | flops 270073888 | bytes 7735039 | solution.py:87
  478.7 3.5 fusion.38
  505.6 3.5 fusion.38
  532.4 3.5 fusion.38
  559.3 3.5 fusion.38
  586.2 3.5 fusion.38
  613.0 3.5 fusion.38
  639.9 3.5 fusion.38
  666.7 3.5 fusion.38
  693.6 3.5 fusion.38
  827.9 3.5 fusion.38
  (369 shorter events, 192.8 us)
Async XLA Ops:
  6.5 22.8 %copy-start = (bf16[512,2048]{1,0:T(8,128)(2,1)S(1)}, bf16[512,2048]{1,0:T(8,128)(2,1)}, u32[]{:S(2)}) copy-start(bf16[512,2048]{1,0:T(8,128)(2,1)} %param.11) | copy-start | bytes 6291460
  8.7 18.6 %all-to-all-start.2 = ((bf16[8,64,512]{2,1,0:T(8,128)(2,1)}), bf16[8,64,512]{2,1,0:T(8,128)(2,1)S(1)}, u32[]{:S(2)}, u32[]{:S(2)}) async-start(bf16[8,64,512]{2,1,0:T(8,128)(2,1)} %bitcast.22), calls=%async_computation.3 | async-start | bytes 1048576 | tf_op jit(solution)/shard_map/all_to_all | solution.py:15
  13.9 74.0 %reduce-scatter.8.cloned.1.call-start = ((), (), s32[]{:S(2)}) async-start(), calls=%async_computation.13 | async-start | bytes 3440640 | tf_op jit(solution)/shard_map/reduce_scatter | solution.py:49
  31.8 1.6 copy-start.2
  35.8 30.8 %all-to-all-start = ((bf16[8,64,2048]{2,1,0:T(8,128)(2,1)}), bf16[8,64,2048]{2,1,0:T(8,128)(2,1)S(1)}, u32[]{:S(2)}, u32[]{:S(2)}) async-start(bf16[8,64,2048]{2,1,0:T(8,128)(2,1)} %bitcast.71), calls=%async_computation | async-start | bytes 4194304 | tf_op jit(solution)/shard_map/all_to_all | solution.py:15
  40.0 83.3 %all-gather.2.cloned.1.call-start = ((), (), s32[]{:S(2)}) async-start(), calls=%async_computation.14 | async-start | bytes 1720320 | tf_op jit(solution)/shard_map/all_gather | solution.py:50
  89.8 87.9 %reduce-scatter.6.cloned.1.call-start = ((), (), s32[]{:S(2)}) async-start(), calls=%async_computation.12 | async-start | bytes 3276800 | tf_op jit(solution)/shard_map/reduce_scatter | solution.py:72
  105.5 125.4 %reduce-scatter.10.cloned.1.call-start = ((), (), s32[]{:S(2)}) async-start(), calls=%async_computation.15 | async-start | bytes 3276800 | tf_op jit(solution)/shard_map/reduce_scatter | solution.py:72
  162.2 122.7 %reduce-scatter.12.cloned.1.call-start = ((), (), s32[]{:S(2)}) async-start(), calls=%async_computation.16 | async-start | bytes 3276800 | tf_op jit(solution)/shard_map/reduce_scatter | solution.py:72
  180.7 51.3 %all-to-all-start.1 = ((bf16[8,80,2048]{2,1,0:T(8,128)(2,1)}), bf16[8,80,2048]{2,1,0:T(8,128)(2,1)}, u32[]{:S(2)}, u32[]{:S(2)}) async-start(bf16[8,80,2048]{2,1,0:T(8,128)(2,1)} %broadcast_in_dim.79), calls=%async_computation.2 | async-start | bytes 5242880 | tf_op jit(solution)/shard_map/all_to_all | solution.py:75
  185.2 161.9 %reduce-scatter.14.cloned.1.call-start = ((), (), s32[]{:S(2)}) async-start(), calls=%async_computation.17 | async-start | bytes 3932160 | tf_op jit(solution)/shard_map/reduce_scatter | solution.py:72
  233.9 52.2 %all-to-all-start.4 = ((bf16[8,80,2048]{2,1,0:T(8,128)(2,1)}), bf16[8,80,2048]{2,1,0:T(8,128)(2,1)}, u32[]{:S(2)}, u32[]{:S(2)}) async-start(bf16[8,80,2048]{2,1,0:T(8,128)(2,1)} %broadcast_in_dim.80), calls=%async_computation.7 | async-start | bytes 5242880 | tf_op jit(solution)/shard_map/all_to_all | solution.py:75
  287.9 60.3 %all-to-all-start.5 = ((bf16[8,80,2048]{2,1,0:T(8,128)(2,1)}), bf16[8,80,2048]{2,1,0:T(8,128)(2,1)}, u32[]{:S(2)}, u32[]{:S(2)}) async-start(bf16[8,80,2048]{2,1,0:T(8,128)(2,1)} %broadcast_in_dim.81), calls=%async_computation.9 | async-start | bytes 5242880 | tf_op jit(solution)/shard_map/all_to_all | solution.py:75
  350.3 42.3 %all-to-all-start.6 = ((bf16[8,96,2048]{2,1,0:T(8,128)(2,1)}), bf16[8,96,2048]{2,1,0:T(8,128)(2,1)}, u32[]{:S(2)}, u32[]{:S(2)}) async-start(bf16[8,96,2048]{2,1,0:T(8,128)(2,1)} %broadcast_in_dim.82), calls=%async_computation.11 | async-start | bytes 6291456 | tf_op jit(solution)/shard_map/all_to_all | solution.py:75
  831.4 3.2 copy-start.1
Sparse Core Ops, SparseCore 0:
  31.9 55.9 reduce-scatter.7
  89.9 33.2 all-gather.1
  125.6 51.2 reduce-scatter.5
  179.1 51.7 reduce-scatter.9
  233.0 51.7 reduce-scatter.11
  287.0 59.9 reduce-scatter.13

commit v3 on v1

--- a/solution.py
+++ b/solution.py
@@ -45,10 +45,11 @@
     acts_p = jnp.take(acts_r, src, axis=0, mode="clip")
 
     act_part = jnp.dot(acts_p, basis_in, preferred_element_type=jnp.float32)
-    in_cols = act_part.shape[1] // dp
-    act_part = act_part.reshape(cap, dp, in_cols).transpose(1, 0, 2).reshape(-1, in_cols)
-    act_part = lax.all_to_all(act_part, "dp", 0, 0, tiled=True)
-    rot_acts = lax.psum(act_part, "tensor").astype(jnp.bfloat16)
+    act_sum = lax.psum_scatter(act_part, "tensor", scatter_dimension=1, tiled=True)
+    act_whole = lax.all_gather(act_sum.astype(jnp.bfloat16), "tensor", axis=1, tiled=True)
+    in_cols = act_whole.shape[1] // dp
+    act_whole = act_whole.reshape(cap, dp, in_cols).transpose(1, 0, 2).reshape(-1, in_cols)
+    rot_acts = lax.all_to_all(act_whole, "dp", 0, 0, tiled=True)
 
     grad_part = jnp.dot(grads_p, basis_out, preferred_element_type=jnp.float32)
     rot_grads = lax.psum_scatter(grad_part, "tensor", scatter_dimension=1, tiled=True)

time: 520 us -> 462 us (0.89)
  blocking collectives: 110 us -> 0 us
  waiting for transfers between devices: 249 us -> 296 us
    psum x1 -> x0, blocking collectives: 96.5 us -> none  [shards(): rot_acts = lax.psum(act_part, 'tensor').astype(jnp.bfloat16)]
    all_gather x0 -> x1, waiting for transfers between devices: none -> 33.2 us  [shards(): lax.all_gather(act_sum.astype(jnp.bfloat16), 'tensor', axis=1, tiled=True)]
    all_gather x1, waiting for transfers between devices: 0.02 us -> 19.3 us  [shards(): all_grads = lax.all_gather(rot_grads, 'dp', axis=0, tiled=True)]
    all_to_all x1, waiting for transfers between devices: 47.5 us -> 31.3 us  [shards(): rot_acts = lax.all_to_all(act_whole, 'dp', 0, 0, tiled=True)]
    all_to_all x1 -> x0, blocking collectives: 13.8 us -> none  [redistribute(): return lax.all_to_all(x, 'dp', 0, 0, tiled=True)]
    all_to_all x1 -> x2, waiting for transfers between devices: 14.6 us -> 26.6 us  [redistribute(): return lax.all_to_all(x, 'dp', 0, 0, tiled=True)]
  transfers between devices with their start and end apart: 4 -> 7, of which waited for: 3 -> 5; matrix products, arithmetic and copies ran while one was open for 7% -> 14% of each run, Pallas kernels for 0% -> 0%
where the time goes in v3:
time: 462 us; the launch traced here: 461 us
  waiting for transfers between devices  296 us (64%)
  local copies, waits for them, and re-layouts  68.9 us (15%)
  matrix products  52.3 us (11%)
  other arithmetic  17.4 us (4%)
  between operations  13.4 us (3%)
  starting transfers between devices  13.3 us (3%)
    reduce_scatter x1, waiting for transfers between devices, shards(): lax.psum_scatter(grad_part, 'tensor', scatter_dimension=1, tiled=True)  185 us
    gather x1, local copies, waits for them, and re-layouts, shards(): grads_u = jnp.take(all_grads, pick, axis=0, mode='clip')  36.9 us
    all_gather x1, waiting for transfers between devices, shards(): lax.all_gather(act_sum.astype(jnp.bfloat16), 'tensor', axis=1, tiled=True)  33.2 us
    all_to_all x1, waiting for transfers between devices, shards(): rot_acts = lax.all_to_all(act_whole, 'dp', 0, 0, tiled=True)  31.3 us
    dot_general x16, matrix products, shards(): lax.dot_general(g, a, (((0,), (0,)), ((), ())), preferred_element_type=jn...  29.8 us
    all_to_all x2, waiting for transfers between devices, redistribute(): return lax.all_to_all(x, 'dp', 0, 0, tiled=True)  26.6 us
    dot_general x1, matrix products, shards(): grad_part = jnp.dot(grads_p, basis_out, preferred_element_type=jnp.float32)  20.1 us
    all_gather x1, waiting for transfers between devices, shards(): all_grads = lax.all_gather(rot_grads, 'dp', axis=0, tiled=True)  19.3 us
  transfers between devices with their start and end apart: 7, of which 5 were waited for; matrix products, arithmetic and copies ran while one was open for 14% of the time, Pallas kernels for 0%

profile of v3, /device:TPU:0, one launch (start us, length us, event | category | flops | bytes accessed | tf_op | source)
XLA Modules:
  0.0 461.0 jit_solution(5852510574726155238)
XLA Ops:
  6.5 2.1 copy.17
  8.7 5.2 %all-to-all-start.1 = ((bf16[8,64,512]{2,1,0:T(8,128)(2,1)}), bf16[8,64,512]{2,1,0:T(8,128)(2,1)S(1)}, u32[]{:S(2)}, u32[]{:S(2)}) async-start(bf16[8,64,512]{2,1,0:T(8,128)(2,1)} %bitcast.22), calls=%async_computation.2 | async-start | bytes 1048576 | tf_op jit(solution)/shard_map/all_to_all | solution.py:14
  15.9 4.3 fusion.57
  20.2 5.7 %select_select_fusion = s32[336]{0:T(512)S(1)} fusion(pred[336]{0:T(512)(128)(4,1)S(1)} %get-tuple-element.13, pred[336]{0:T(512)(128)(4,1)S(1)} %get-tuple-element.12, pred[336]{0:T(512)(128)(4,1)S(1)} %get-tuple-element.11, pred[336]{0:T(512)(128)(4,1)S(1)} %get-tuple-element.10, pred[336]{0:T(512)(128)(4,1)S(1)} %get-tuple-element.9, ...), kind=kLoop, calls=%fused_computation.112 | loop fusion | flops 3024 | bytes 5748 | tf_op jit(solution)/shard_map/gather | solution.py:39
  26.0 2.0 gather_fusion.3
  28.0 2.4 fusion.61
  30.5 1.6 copy-done.5
  32.0 2.5 copy.16
  34.5 4.1 all-to-all-start
  38.7 26.6 %all-to-all-done = bf16[8,64,2048]{2,1,0:T(8,128)(2,1)S(1)} async-done(((bf16[8,64,2048]{2,1,0:T(8,128)(2,1)}), bf16[8,64,2048]{2,1,0:T(8,128)(2,1)S(1)}, u32[]{:S(2)}, u32[]{:S(2)}) %all-to-all-start) | async-done | bytes 2097184 | tf_op jit(solution)/shard_map/all_to_all | solution.py:14
  65.3 2.4 gather_fusion.1
  67.7 20.1 %fusion.16 = f32[336,8192]{1,0:T(8,128)} fusion(bf16[2048,8192]{1,0:T(8,128)(2,1)} %param.8, bf16[336,2048]{1,0:T(8,128)(2,1)S(1)} %gather_fusion.1, pred[336]{0:T(512)(128)(4,1)S(1)} %broadcast_compare_fusion), kind=kOutput, calls=%fused_computation.39 | convolution fusion | flops 11274977280 | bytes 45941072 | tf_op jit(solution)/shard_map/dot_general | solution.py:54
  88.0 1.9 convert_element_type.11
  89.9 185.2 %reduce-scatter.3.cloned.1.call-done = f32[336,2048]{1,0:T(8,128)} async-done(((f32[336,8192]{1,0:T(8,128)}), f32[336,2048]{1,0:T(8,128)}) %reduce-scatter.3.cloned.1.call-update) | async-done | bytes 2752528 | tf_op jit(solution)/shard_map/reduce_scatter | solution.py:55
  275.1 3.1 convert_element_type.10
  278.2 33.2 %all-gather.5.cloned.1.call-done = bf16[336,2048]{1,0:T(8,128)(2,1)} async-done(((bf16[336,512]{1,0:T(8,128)(2,1)}), bf16[336,2048]{1,0:T(8,128)(2,1)}) %all-gather.5.cloned.1.call-update) | async-done | bytes 1376272 | tf_op jit(solution)/shard_map/all_gather | solution.py:49
  311.4 2.5 copy.21
  313.9 3.8 all-to-all-start.2
  318.1 31.3 %all-to-all-done.2 = bf16[8,336,256]{2,1,0:T(8,128)(2,1)S(1)} async-done(((bf16[8,336,256]{2,1,0:T(8,128)(2,1)}), bf16[8,336,256]{2,1,0:T(8,128)(2,1)S(1)}, u32[]{:S(2)}, u32[]{:S(2)}) %all-to-all-start.2) | async-done | bytes 1376288 | tf_op jit(solution)/shard_map/all_to_all | solution.py:52
  349.4 17.0 %gather_fusion.4 = bf16[4096,256]{1,0:T(8,128)(2,1)} fusion(bf16[2688,256]{1,0:T(8,128)(2,1)S(1)} %bitcast.37, s32[4096]{0:T(1024)S(1)} %broadcast_clamp_fusion), kind=kCustom, calls=%fused_computation.4 | custom fusion | bytes 4210688 | tf_op jit(solution)/shard_map/jit(_take)/gather | solution.py:65
  366.4 1.9 broadcast_select_fusion
  368.3 19.3 %all-gather.3.cloned.1.call-done = bf16[2688,2048]{1,0:T(8,128)(2,1)} async-done(((bf16[336,2048]{1,0:T(8,128)(2,1)}), bf16[2688,2048]{1,0:T(8,128)(2,1)}) %all-gather.3.cloned.1.call-update) | async-done | bytes 11010064 | tf_op jit(solution)/shard_map/all_gather | solution.py:57
  387.7 36.9 %gather_fusion.2 = bf16[4096,2048]{1,0:T(8,128)(2,1)} fusion(bf16[2688,2048]{1,0:T(8,128)(2,1)} %all-gather.3.cloned.1.call-done, s32[4096]{0:T(1024)S(1)} %broadcast_clamp_fusion), kind=kCustom, calls=%fused_computation.2 | custom fusion | bytes 33570816 | tf_op jit(solution)/shard_map/jit(_take)/gather | solution.py:64
  424.6 1.9 convolution_multiply_fusion.10
  426.4 2.1 convolution_multiply_fusion.11
  428.6 3.6 convolution_multiply_fusion.12
  432.2 3.1 convolution_multiply_fusion.13
  435.2 3.0 convolution_multiply_fusion.14
  438.2 1.7 convolution_multiply_fusion.5
  443.4 5.2 %fusion.4 = f32[2048,256]{1,0:T(8,128)} fusion(f32[2048,256]{1,0:T(8,128)S(1)} %convolution_multiply_fusion.10, f32[2048,256]{1,0:T(8,128)S(1)} %convolution_multiply_fusion.11, f32[2048,256]{1,0:T(8,128)} %convolution_multiply_fusion.12, f32[2048,256]{1,0:T(8,128)} %convolution_multiply_fusion.13, f32[2048,256]{1,0:T(8,128)} %convolution_multiply_fusion.14, ...), kind=kOutput, calls=%fused_computation.25 | convolution fusion | flops 271581184 | bytes 13762560 | tf_op jit(solution)/shard_map/dot_general | solution.py:72
  448.6 2.6 fusion.9
  451.2 3.3 fusion.15
  (50 shorter events, 6.0 us)
Async XLA Ops:
  6.5 21.5 %copy-start = (bf16[512,2048]{1,0:T(8,128)(2,1)S(1)}, bf16[512,2048]{1,0:T(8,128)(2,1)}, u32[]{:S(2)}) copy-start(bf16[512,2048]{1,0:T(8,128)(2,1)} %param.9) | copy-start | bytes 6291460
  6.5 7.4 %copy-start.6 = (s32[16]{0:T(128)S(1)}, s32[16]{0:T(128)}, u32[]{:S(2)}) copy-start(s32[16]{0:T(128)} %param.10) | copy-start | bytes 196
  6.5 7.4 %copy-start.2 = (s32[16]{0:T(128)S(1)}, s32[16]{0:T(128)}, u32[]{:S(2)}) copy-start(s32[16]{0:T(128)} %param.11) | copy-start | bytes 196
  8.7 17.3 %all-to-all-start.1 = ((bf16[8,64,512]{2,1,0:T(8,128)(2,1)}), bf16[8,64,512]{2,1,0:T(8,128)(2,1)S(1)}, u32[]{:S(2)}, u32[]{:S(2)}) async-start(bf16[8,64,512]{2,1,0:T(8,128)(2,1)} %bitcast.22), calls=%async_computation.2 | async-start | bytes 1048576 | tf_op jit(solution)/shard_map/all_to_all | solution.py:14
  13.9 74.1 %reduce-scatter.5.cloned.1.call-start = ((), (), s32[]{:S(2)}) async-start(), calls=%async_computation.7 | async-start | bytes 3440640 | tf_op jit(solution)/shard_map/reduce_scatter | solution.py:48
  30.4 1.6 copy-start.5
  34.5 30.8 %all-to-all-start = ((bf16[8,64,2048]{2,1,0:T(8,128)(2,1)}), bf16[8,64,2048]{2,1,0:T(8,128)(2,1)S(1)}, u32[]{:S(2)}, u32[]{:S(2)}) async-start(bf16[8,64,2048]{2,1,0:T(8,128)(2,1)} %bitcast.40), calls=%async_computation | async-start | bytes 4194304 | tf_op jit(solution)/shard_map/all_to_all | solution.py:14
  38.7 236.5 %reduce-scatter.3.cloned.1.call-start = ((), (), s32[]{:S(2)}) async-start(), calls=%async_computation.5 | async-start | bytes 13762560 | tf_op jit(solution)/shard_map/reduce_scatter | solution.py:55
  87.9 223.5 %all-gather.5.cloned.1.call-start = ((), (), s32[]{:S(2)}) async-start(), calls=%async_computation.8 | async-start | bytes 1720320 | tf_op jit(solution)/shard_map/all_gather | solution.py:49
  89.9 297.8 %all-gather.3.cloned.1.call-start = ((), (), s32[]{:S(2)}) async-start(), calls=%async_computation.6 | async-start | bytes 12386304 | tf_op jit(solution)/shard_map/all_gather | solution.py:57
  313.9 35.4 %all-to-all-start.2 = ((bf16[8,336,256]{2,1,0:T(8,128)(2,1)}), bf16[8,336,256]{2,1,0:T(8,128)(2,1)S(1)}, u32[]{:S(2)}, u32[]{:S(2)}) async-start(bf16[8,336,256]{2,1,0:T(8,128)(2,1)} %bitcast.36), calls=%async_computation.4 | async-start | bytes 2752512 | tf_op jit(solution)/shard_map/all_to_all | solution.py:52
  368.3 80.3 %copy-start.4 = (bf16[4096,256]{1,0:T(8,128)(2,1)}, bf16[4096,256]{1,0:T(8,128)(2,1)S(1)}, u32[]{:S(2)}) copy-start(bf16[4096,256]{1,0:T(8,128)(2,1)S(1)} %broadcast_select_fusion) | copy-start | bytes 6291460
  424.6 15.4 %copy-start.3 = (bf16[4096,2048]{1,0:T(8,128)(2,1)S(1)}, bf16[4096,2048]{1,0:T(8,128)(2,1)}, u32[]{:S(2)}) copy-start(bf16[4096,2048]{1,0:T(8,128)(2,1)} %gather_fusion.2) | copy-start | bytes 50331652
  451.2 3.3 copy-start.1
Sparse Core Ops, SparseCore 0:
  30.6 55.9 reduce-scatter.4
  88.9 186.1 reduce-scatter.2
  276.7 34.6 all-gather.4
  313.1 74.4 all-gather.2

commit v4 on v3

--- a/solution.py
+++ b/solution.py
@@ -1,6 +1,10 @@
+import functools
+
 import jax
 import jax.numpy as jnp
 from jax import lax
+from jax.experimental import pallas as pl
+from jax.experimental.pallas import tpu as pltpu
 from jax.sharding import PartitionSpec as P
 
 LEN = 256
@@ -12,6 +16,39 @@
     width = x.shape[1]
     x = x.reshape(slots, LEN // dp, dp, width).transpose(2, 0, 1, 3).reshape(-1, width)
     return lax.all_to_all(x, "dp", 0, 0, tiled=True)
+
+
+def slot_squares(win_ref, lo_ref, hi_ref, grads_hbm, acts_hbm, out_ref, gbuf, abuf, sems, *, dp, per, scale):
+    s = pl.program_id(0)
+    copies = []
+    for g in range(dp):
+        w = pl.multiple_of(win_ref[s * dp + g], 16)
+        cg = pltpu.make_async_copy(grads_hbm.at[pl.ds(w, per)], gbuf.at[pl.ds(g * per, per)], sems.at[0, g])
+        ca = pltpu.make_async_copy(acts_hbm.at[pl.ds(w, per)], abuf.at[pl.ds(g * per, per)], sems.at[1, g])
+        cg.start()
+        ca.start()
+        copies += [cg, ca]
+    for c in copies:
+        c.wait()
+
+    @pl.when(s == 0)
+    def _():
+        out_ref[...] = jnp.zeros_like(out_ref)
+
+    for g in range(dp):
+        w = win_ref[s * dp + g]
+        row = w + lax.broadcasted_iota(jnp.int32, (per, 1), 0)
+        keep = (row >= lo_ref[s * dp + g]) & (row < hi_ref[s * dp + g])
+        a = abuf[pl.ds(g * per, per), :].astype(jnp.float32)
+        abuf[pl.ds(g * per, per), :] = jnp.where(keep, a, 0.0).astype(jnp.bfloat16)
+    rotated = lax.dot_general(
+        gbuf[...], abuf[...], (((0,), (0,)), ((), ())), preferred_element_type=jnp.float32
+    )
+    out_ref[...] += rotated * rotated
+
+    @pl.when(s == pl.num_programs(0) - 1)
+    def _():
+        out_ref[...] = out_ref[...] * scale
 
 
 def shards(acts, out_grads, basis_out, basis_in, slot_sequence, seq_lengths, *, dp):
@@ -47,6 +84,7 @@
     act_part = jnp.dot(acts_p, basis_in, preferred_element_type=jnp.float32)
     act_sum = lax.psum_scatter(act_part, "tensor", scatter_dimension=1, tiled=True)
     act_whole = lax.all_gather(act_sum.astype(jnp.bfloat16), "tensor", axis=1, tiled=True)
+    grads_p, act_whole = lax.optimization_barrier((grads_p, act_whole))
     in_cols = act_whole.shape[1] // dp
     act_whole = act_whole.reshape(cap, dp, in_cols).transpose(1, 0, 2).reshape(-1, in_cols)
     rot_acts = lax.all_to_all(act_whole, "dp", 0, 0, tiled=True)
@@ -56,22 +94,27 @@
     rot_grads = rot_grads.astype(jnp.bfloat16)
     all_grads = lax.all_gather(rot_grads, "dp", axis=0, tiled=True)
 
-    js = jnp.arange(per, dtype=jnp.int32)
-    pick = groups[None, :, None] * cap + starts[:, :, None] + js[None, None, :]
-    live = js[None, None, :] < kept[:, :, None]
-    pick = jnp.where(live, pick, 0).reshape(-1)
-    live = live.reshape(-1)
-    grads_u = jnp.take(all_grads, pick, axis=0, mode="clip")
-    acts_u = jnp.take(rot_acts, pick, axis=0, mode="clip")
-    acts_u = jnp.where(live[:, None], acts_u, jnp.zeros_like(acts_u))
-
-    squares = jnp.zeros((all_grads.shape[1], rot_acts.shape[1]), jnp.float32)
-    for slot in range(nseq):
-        g = grads_u[slot * LEN : (slot + 1) * LEN]
-        a = acts_u[slot * LEN : (slot + 1) * LEN]
-        rotated = lax.dot_general(g, a, (((0,), (0,)), ((), ())), preferred_element_type=jnp.float32)
-        squares = squares + rotated * rotated
-    return squares / (nseq * LEN)
+    span = per + 16
+    lo = groups[None, :] * cap + starts
+    win = jnp.minimum((lo // 16) * 16, dp * cap - span)
+    out_rows, in_cols = all_grads.shape[1], rot_acts.shape[1]
+    kernel = functools.partial(slot_squares, dp=dp, per=span, scale=1.0 / (nseq * LEN))
+    return pl.pallas_call(
+        kernel,
+        out_shape=jax.ShapeDtypeStruct((out_rows, in_cols), jnp.float32),
+        grid_spec=pltpu.PrefetchScalarGridSpec(
+            num_scalar_prefetch=3,
+            grid=(nseq,),
+            in_specs=[pl.BlockSpec(memory_space=pl.ANY), pl.BlockSpec(memory_space=pl.ANY)],
+            out_specs=pl.BlockSpec((out_rows, in_cols), lambda s, *_: (0, 0)),
+            scratch_shapes=[
+                pltpu.VMEM((dp * span, out_rows), jnp.bfloat16),
+                pltpu.VMEM((dp * span, in_cols), jnp.bfloat16),
+                pltpu.SemaphoreType.DMA((2, dp)),
+            ],
+        ),
+        compiler_params=pltpu.CompilerParams(dimension_semantics=("arbitrary",)),
+    )(win.reshape(-1), lo.reshape(-1), (lo + kept).reshape(-1), all_grads, rot_acts)
 
 
 def solution(mesh):

time: 462 us -> 455 us (0.985)
  local copies, waits for them, and re-layouts: 68.9 us -> 13.4 us
  Pallas kernels: 0 us -> 39.9 us
  waiting for transfers between devices: 296 us -> 335 us
  matrix products: 52.3 us -> 22.4 us
    gather x2 -> x0, local copies, waits for them, and re-layouts: 53.9 us -> none  [the longest x1 36.9 us: shards(): grads_u = jnp.take(all_grads, pick, axis=0, mode='clip')]
    reduce_scatter x1, waiting for transfers between devices: 0.02 us -> 47.9 us  [shards(): lax.psum_scatter(act_part, 'tensor', scatter_dimension=1, tiled=True)]
    pallas_call x0 -> x1, Pallas kernels: none -> 39.9 us  [shards(): pl.pallas_call(kernel, out_shape=jax.ShapeDtypeStruct((out_rows, in_cols)...]
    dot_general x16 -> x0, matrix products: 29.8 us -> none  [shards(): lax.dot_general(g, a, (((0,), (0,)), ((), ())), preferred_element_type=jn...]
    all_to_all x2, waiting for transfers between devices: 26.6 us -> 0.01 us  [redistribute(): return lax.all_to_all(x, 'dp', 0, 0, tiled=True)]
    all_gather x1, waiting for transfers between devices: 19.3 us -> 42 us  [shards(): all_grads = lax.all_gather(rot_grads, 'dp', axis=0, tiled=True)]
  transfers between devices with their start and end apart: 7 -> 7, of which waited for: 5 -> 5; matrix products, arithmetic and copies ran while one was open for 14% -> 5% of each run, Pallas kernels for 0% -> 0%
where the time goes in v4:
time: 455 us; the launch traced here: 454 us
  waiting for transfers between devices  335 us (74%)
  Pallas kernels  39.9 us (9%)
  matrix products  22.4 us (5%)
  other arithmetic  16.6 us (4%)
  local copies, waits for them, and re-layouts  13.4 us (3%)
  between operations  13.3 us (3%)
  starting transfers between devices  13.2 us (3%)
    reduce_scatter x1, waiting for transfers between devices, shards(): lax.psum_scatter(grad_part, 'tensor', scatter_dimension=1, tiled=True)  186 us
    reduce_scatter x1, waiting for transfers between devices, shards(): lax.psum_scatter(act_part, 'tensor', scatter_dimension=1, tiled=True)  47.9 us
    all_gather x1, waiting for transfers between devices, shards(): all_grads = lax.all_gather(rot_grads, 'dp', axis=0, tiled=True)  42 us
    pallas_call x1, Pallas kernels, shards(): pl.pallas_call(kernel, out_shape=jax.ShapeDtypeStruct((out_rows, in_cols)...  39.9 us
    all_gather x1, waiting for transfers between devices, shards(): lax.all_gather(act_sum.astype(jnp.bfloat16), 'tensor', axis=1, tiled=True)  30.8 us
    all_to_all x1, waiting for transfers between devices, shards(): rot_acts = lax.all_to_all(act_whole, 'dp', 0, 0, tiled=True)  28.7 us
    dot_general x1, matrix products, shards(): grad_part = jnp.dot(grads_p, basis_out, preferred_element_type=jnp.float32)  19.9 us
    gather x3, other arithmetic, shards(): src = jnp.clip(slot_c * per + rows - my_starts[slot_c], 0, nseq * per - 1)  10 us
  transfers between devices with their start and end apart: 7, of which 5 were waited for; matrix products, arithmetic and copies ran while one was open for 5% of the time, Pallas kernels for 0%

profile of v4, /device:TPU:0, one launch (start us, length us, event | category | flops | bytes accessed | tf_op | source)
XLA Modules:
  0.0 453.9 jit_solution(4315043658798019704)
XLA Ops:
  6.5 2.1 copy.14
  8.7 5.2 %all-to-all-start.1 = ((bf16[8,64,512]{2,1,0:T(8,128)(2,1)}), bf16[8,64,512]{2,1,0:T(8,128)(2,1)S(1)}, u32[]{:S(2)}, u32[]{:S(2)}) async-start(bf16[8,64,512]{2,1,0:T(8,128)(2,1)} %bitcast.22), calls=%async_computation.1 | async-start | bytes 1048576 | tf_op jit(solution)/shard_map/all_to_all | solution.py:18
  14.0 0.7 gather_fusion
  14.6 0.1 fusion.1
  14.8 0.2 dynamic-slice_reduce_fusion
  14.9 0.1 convert_reduce_fusion
  15.1 0.6 fusion.7
  15.7 4.3 fusion.4
  20.0 5.7 %select_select_fusion = s32[336]{0:T(512)S(1)} fusion(pred[336]{0:T(512)(128)(4,1)S(1)} %get-tuple-element.17, pred[336]{0:T(512)(128)(4,1)S(1)} %get-tuple-element.16, pred[336]{0:T(512)(128)(4,1)S(1)} %get-tuple-element.15, pred[336]{0:T(512)(128)(4,1)S(1)} %get-tuple-element.14, pred[336]{0:T(512)(128)(4,1)S(1)} %get-tuple-element.13, ...), kind=kLoop, calls=%fused_computation.38 | loop fusion | flops 3024 | bytes 5748 | tf_op jit(solution)/shard_map/gather | solution.py:76
  25.8 2.0 gather_fusion.2
  27.8 2.4 fusion.8
  30.3 1.6 copy-done.4
  31.9 2.5 copy.13
  34.3 4.1 all-to-all-start
  38.5 47.9 %reduce-scatter.3.cloned.1.call-done = f32[336,512]{1,0:T(8,128)} async-done(((f32[336,2048]{1,0:T(8,128)}), f32[336,512]{1,0:T(8,128)}) %reduce-scatter.3.cloned.1.call-update) | async-done | bytes 688144 | tf_op jit(solution)/shard_map/reduce_scatter | solution.py:85
  86.4 1.9 convert_element_type.10
  88.4 2.4 gather_fusion.1
  90.8 0.2 broadcast_select_fusion
  91.0 30.8 %all-gather.3.cloned.1.call-done = bf16[336,2048]{1,0:T(8,128)(2,1)} async-done(((bf16[336,512]{1,0:T(8,128)(2,1)}), bf16[336,2048]{1,0:T(8,128)(2,1)}) %all-gather.3.cloned.1.call-update) | async-done | bytes 1376272 | tf_op jit(solution)/shard_map/all_gather | solution.py:86
  121.8 19.9 %fusion.9 = f32[336,8192]{1,0:T(8,128)} fusion(bf16[336,2048]{1,0:T(8,128)(2,1)S(1)} %broadcast_select_fusion, bf16[2048,8192]{1,0:T(8,128)(2,1)} %param.8), kind=kOutput, calls=%fused_computation.58 | convolution fusion | flops 11274289152 | bytes 45940736 | tf_op jit(solution)/shard_map/dot_general | solution.py:92
  141.8 185.6 %reduce-scatter.5.cloned.1.call-done = f32[336,2048]{1,0:T(8,128)} async-done(((f32[336,8192]{1,0:T(8,128)}), f32[336,2048]{1,0:T(8,128)}) %reduce-scatter.5.cloned.1.call-update) | async-done | bytes 2752528 | tf_op jit(solution)/shard_map/reduce_scatter | solution.py:93
  327.4 3.1 convert_element_type.11
  330.5 1.2 copy.18
  331.6 3.7 all-to-all-start.2
  335.3 0.1 reduce_window_sum.14
  335.4 0.1 add.69
  335.5 0.1 sub.63
  335.6 0.6 fusion.6
  336.2 0.5 multiply_minimum_fusion.win_ref
  336.7 28.7 %all-to-all-done.2 = bf16[8,336,256]{2,1,0:T(8,128)(2,1)S(1)} async-done(((bf16[8,336,256]{2,1,0:T(8,128)(2,1)}), bf16[8,336,256]{2,1,0:T(8,128)(2,1)S(1)}, u32[]{:S(2)}, u32[]{:S(2)}) %all-to-all-start.2) | async-done | bytes 1376288 | tf_op jit(solution)/shard_map/all_to_all | solution.py:90
  365.4 42.0 %all-gather.5.cloned.1.call-done.grads_hbm = bf16[2688,2048]{1,0:T(8,128)(2,1)} async-done(((bf16[336,2048]{1,0:T(8,128)(2,1)}), bf16[2688,2048]{1,0:T(8,128)(2,1)}) %all-gather.5.cloned.1.call-update) | async-done | bytes 11010064 | tf_op jit(solution)/shard_map/all_gather | solution.py:95
  407.4 39.9 %shard_map.64 = f32[2048,256]{1,0:T(8,128)} custom-call(s32[128]{0:T(128)} %multiply_minimum_fusion.win_ref, s32[128]{0:T(128)} %copy-done.6, s32[128]{0:T(128)} %get-tuple-element.20.hi_ref, bf16[2688,2048]{1,0:T(8,128)(2,1)} %all-gather.5.cloned.1.call-done.grads_hbm, bf16[2688,256]{1,0:T(8,128)(2,1)} %bitcast.41), custom_call_target="tpu_custom_call" | custom-call | tf_op jit(solution)/shard_map/pallas_call | solution.py:102
  (35 shorter events, 0.4 us)
Async XLA Ops:
  6.5 21.3 %copy-start = (bf16[512,2048]{1,0:T(8,128)(2,1)S(1)}, bf16[512,2048]{1,0:T(8,128)(2,1)}, u32[]{:S(2)}) copy-start(bf16[512,2048]{1,0:T(8,128)(2,1)} %param.9) | copy-start | bytes 6291460
  6.5 7.4 %copy-start.7 = (s32[16]{0:T(128)S(1)}, s32[16]{0:T(128)}, u32[]{:S(2)}) copy-start(s32[16]{0:T(128)} %param.10) | copy-start | bytes 196
  6.5 7.4 %copy-start.2 = (s32[16]{0:T(128)S(1)}, s32[16]{0:T(128)}, u32[]{:S(2)}) copy-start(s32[16]{0:T(128)} %param.11) | copy-start | bytes 196
  8.7 17.1 %all-to-all-start.1 = ((bf16[8,64,512]{2,1,0:T(8,128)(2,1)}), bf16[8,64,512]{2,1,0:T(8,128)(2,1)S(1)}, u32[]{:S(2)}, u32[]{:S(2)}) async-start(bf16[8,64,512]{2,1,0:T(8,128)(2,1)} %bitcast.22), calls=%async_computation.1 | async-start | bytes 1048576 | tf_op jit(solution)/shard_map/all_to_all | solution.py:18
  13.9 72.5 %reduce-scatter.3.cloned.1.call-start = ((), (), s32[]{:S(2)}) async-start(), calls=%async_computation.5 | async-start | bytes 3440640 | tf_op jit(solution)/shard_map/reduce_scatter | solution.py:85
  30.3 1.6 copy-start.4
  34.3 54.0 %all-to-all-start = ((bf16[8,64,2048]{2,1,0:T(8,128)(2,1)}), bf16[8,64,2048]{2,1,0:T(8,128)(2,1)S(1)}, u32[]{:S(2)}, u32[]{:S(2)}) async-start(bf16[8,64,2048]{2,1,0:T(8,128)(2,1)} %bitcast.40), calls=%async_computation | async-start | bytes 4194304 | tf_op jit(solution)/shard_map/all_to_all | solution.py:18
  38.5 83.3 %all-gather.3.cloned.1.call-start = ((), (), s32[]{:S(2)}) async-start(), calls=%async_computation.6 | async-start | bytes 1720320 | tf_op jit(solution)/shard_map/all_gather | solution.py:86
  88.3 239.1 %reduce-scatter.5.cloned.1.call-start = ((), (), s32[]{:S(2)}) async-start(), calls=%async_computation.7 | async-start | bytes 13762560 | tf_op jit(solution)/shard_map/reduce_scatter | solution.py:93
  141.7 188.8 %copy-start.5 = (bf16[336,2048]{1,0:T(8,128)(2,1)S(1)}, bf16[336,2048]{1,0:T(8,128)(2,1)}, u32[]{:S(2)}) copy-start(bf16[336,2048]{1,0:T(8,128)(2,1)} %all-gather.3.cloned.1.call-done) | copy-start | bytes 4128772
  141.7 265.7 %all-gather.5.cloned.1.call-start = ((), (), s32[]{:S(2)}) async-start(), calls=%async_computation.8 | async-start | bytes 12386304 | tf_op jit(solution)/shard_map/all_gather | solution.py:95
  331.6 33.8 %all-to-all-start.2 = ((bf16[8,336,256]{2,1,0:T(8,128)(2,1)}), bf16[8,336,256]{2,1,0:T(8,128)(2,1)S(1)}, u32[]{:S(2)}, u32[]{:S(2)}) async-start(bf16[8,336,256]{2,1,0:T(8,128)(2,1)} %bitcast.37), calls=%async_computation.4 | async-start | bytes 2752512 | tf_op jit(solution)/shard_map/all_to_all | solution.py:90
  336.2 71.2 %copy-start.6 = (s32[128]{0:T(128)}, s32[128]{0:T(128)S(1)}, u32[]{:S(2)}) copy-start(s32[128]{0:T(128)S(1)} %get-tuple-element.21.lo_ref) | copy-start | bytes 1540
  365.4 42.0 %copy-start.3 = (bf16[8,336,256]{2,1,0:T(8,128)(2,1)}, bf16[8,336,256]{2,1,0:T(8,128)(2,1)S(1)}, u32[]{:S(2)}) copy-start(bf16[8,336,256]{2,1,0:T(8,128)(2,1)S(1)} %all-to-all-done.2) | copy-start | bytes 4128772
  407.4 40.0 %copy-start.1 = (bf16[512,2048]{1,0:T(8,128)(2,1)S(1)}, bf16[512,2048]{1,0:T(8,128)(2,1)}, u32[]{:S(2)}) copy-start(bf16[512,2048]{1,0:T(8,128)(2,1)} %param.9) | copy-start | bytes 6291460
Sparse Core Ops, SparseCore 0:
  30.4 55.9 reduce-scatter.2
  88.4 33.2 all-gather.2
  141.8 185.5 reduce-scatter.4
  330.6 76.7 all-gather.4

commit v5 on v4

--- a/solution.py
+++ b/solution.py
@@ -18,35 +18,54 @@
     return lax.all_to_all(x, "dp", 0, 0, tiled=True)
 
 
-def slot_squares(win_ref, lo_ref, hi_ref, grads_hbm, acts_hbm, out_ref, gbuf, abuf, sems, *, dp, per, scale):
+def slot_squares(win_ref, lo_ref, hi_ref, grads_hbm, acts_hbm, out_ref, gbuf, abuf, sems, *, dp, per, pair, scale):
     s = pl.program_id(0)
-    copies = []
-    for g in range(dp):
-        w = pl.multiple_of(win_ref[s * dp + g], 16)
-        cg = pltpu.make_async_copy(grads_hbm.at[pl.ds(w, per)], gbuf.at[pl.ds(g * per, per)], sems.at[0, g])
-        ca = pltpu.make_async_copy(acts_hbm.at[pl.ds(w, per)], abuf.at[pl.ds(g * per, per)], sems.at[1, g])
-        cg.start()
-        ca.start()
-        copies += [cg, ca]
-    for c in copies:
+    n = pl.num_programs(0)
+
+    def copies(step, b):
+        out = []
+        for q in range(pair):
+            for g in range(dp):
+                w = pl.multiple_of(win_ref[(step * pair + q) * dp + g], 16)
+                rows = pl.ds(g * per, per)
+                out.append(pltpu.make_async_copy(grads_hbm.at[pl.ds(w, per)], gbuf.at[b, q, rows], sems.at[b, q, 0, g]))
+                out.append(pltpu.make_async_copy(acts_hbm.at[pl.ds(w, per)], abuf.at[b, q, rows], sems.at[b, q, 1, g]))
+        return out
+
+    b = s % 2
+
+    @pl.when(s == 0)
+    def _():
+        for c in copies(0, 0):
+            c.start()
+
+    @pl.when(s + 1 < n)
+    def _():
+        for c in copies(s + 1, 1 - b):
+            c.start()
+
+    for c in copies(s, b):
         c.wait()
 
     @pl.when(s == 0)
     def _():
         out_ref[...] = jnp.zeros_like(out_ref)
 
-    for g in range(dp):
-        w = win_ref[s * dp + g]
-        row = w + lax.broadcasted_iota(jnp.int32, (per, 1), 0)
-        keep = (row >= lo_ref[s * dp + g]) & (row < hi_ref[s * dp + g])
-        a = abuf[pl.ds(g * per, per), :].astype(jnp.float32)
-        abuf[pl.ds(g * per, per), :] = jnp.where(keep, a, 0.0).astype(jnp.bfloat16)
-    rotated = lax.dot_general(
-        gbuf[...], abuf[...], (((0,), (0,)), ((), ())), preferred_element_type=jnp.float32
-    )
-    out_ref[...] += rotated * rotated
+    acc = None
+    for q in range(pair):
+        slot = s * pair + q
+        for g in range(dp):
+            row = win_ref[slot * dp + g] + lax.broadcasted_iota(jnp.int32, (per, 1), 0)
+            keep = (row >= lo_ref[slot * dp + g]) & (row < hi_ref[slot * dp + g])
+            a = abuf[b, q, pl.ds(g * per, per), :].astype(jnp.float32)
+            abuf[b, q, pl.ds(g * per, per), :] = jnp.where(keep, a, 0.0).astype(jnp.bfloat16)
+        rotated = lax.dot_general(
+            gbuf[b, q], abuf[b, q], (((0,), (0,)), ((), ())), preferred_element_type=jnp.float32
+        )
+        acc = rotated * rotated if acc is None else acc + rotated * rotated
+    out_ref[...] += acc
 
-    @pl.when(s == pl.num_programs(0) - 1)
+    @pl.when(s == n - 1)
     def _():
         out_ref[...] = out_ref[...] * scale
 
@@ -84,12 +103,12 @@
     act_part = jnp.dot(acts_p, basis_in, preferred_element_type=jnp.float32)
     act_sum = lax.psum_scatter(act_part, "tensor", scatter_dimension=1, tiled=True)
     act_whole = lax.all_gather(act_sum.astype(jnp.bfloat16), "tensor", axis=1, tiled=True)
-    grads_p, act_whole = lax.optimization_barrier((grads_p, act_whole))
+    grad_part = jnp.dot(grads_p, basis_out, preferred_element_type=jnp.float32)
+    grad_part, act_whole = lax.optimization_barrier((grad_part, act_whole))
     in_cols = act_whole.shape[1] // dp
     act_whole = act_whole.reshape(cap, dp, in_cols).transpose(1, 0, 2).reshape(-1, in_cols)
     rot_acts = lax.all_to_all(act_whole, "dp", 0, 0, tiled=True)
 
-    grad_part = jnp.dot(grads_p, basis_out, preferred_element_type=jnp.float32)
     rot_grads = lax.psum_scatter(grad_part, "tensor", scatter_dimension=1, tiled=True)
     rot_grads = rot_grads.astype(jnp.bfloat16)
     all_grads = lax.all_gather(rot_grads, "dp", axis=0, tiled=True)
@@ -98,19 +117,20 @@
     lo = groups[None, :] * cap + starts
     win = jnp.minimum((lo // 16) * 16, dp * cap - span)
     out_rows, in_cols = all_grads.shape[1], rot_acts.shape[1]
-    kernel = functools.partial(slot_squares, dp=dp, per=span, scale=1.0 / (nseq * LEN))
+    pair = 2 if nseq % 2 == 0 else 1
+    kernel = functools.partial(slot_squares, dp=dp, per=span, pair=pair, scale=1.0 / (nseq * LEN))
     return pl.pallas_call(
         kernel,
         out_shape=jax.ShapeDtypeStruct((out_rows, in_cols), jnp.float32),
         grid_spec=pltpu.PrefetchScalarGridSpec(
             num_scalar_prefetch=3,
-            grid=(nseq,),
+            grid=(nseq // pair,),
             in_specs=[pl.BlockSpec(memory_space=pl.ANY), pl.BlockSpec(memory_space=pl.ANY)],
             out_specs=pl.BlockSpec((out_rows, in_cols), lambda s, *_: (0, 0)),
             scratch_shapes=[
-                pltpu.VMEM((dp * span, out_rows), jnp.bfloat16),
-                pltpu.VMEM((dp * span, in_cols), jnp.bfloat16),
-                pltpu.SemaphoreType.DMA((2, dp)),
+                pltpu.VMEM((2, pair, dp * span, out_rows), jnp.bfloat16),
+                pltpu.VMEM((2, pair, dp * span, in_cols), jnp.bfloat16),
+                pltpu.SemaphoreType.DMA((2, pair, 2, dp)),
             ],
         ),
         compiler_params=pltpu.CompilerParams(dimension_semantics=("arbitrary",)),

time: 455 us -> 417 us (0.916)
  Pallas kernels: 39.9 us -> 19.9 us
  waiting for transfers between devices: 335 us -> 317 us
    reduce_scatter x1, waiting for transfers between devices: 47.9 us -> 18.9 us  [shards(): lax.psum_scatter(act_part, 'tensor', scatter_dimension=1, tiled=True)]
    all_to_all x2, waiting for transfers between devices: 0.01 us -> 26.6 us  [redistribute(): return lax.all_to_all(x, 'dp', 0, 0, tiled=True)]
    pallas_call x1, Pallas kernels: 39.9 us -> 19.9 us  [shards(): pl.pallas_call(kernel, out_shape=jax.ShapeDtypeStruct((out_rows, in_cols)...]
    all_gather x1, waiting for transfers between devices: 30.8 us -> 13.3 us  [shards(): lax.all_gather(act_sum.astype(jnp.bfloat16), 'tensor', axis=1, tiled=True)]
  transfers between devices with their start and end apart: 7 -> 7, of which waited for: 5 -> 6; matrix products, arithmetic and copies ran while one was open for 5% -> 9% of each run, Pallas kernels for 0% -> 0%
where the time goes in v5:
time: 417 us; the launch traced here: 416 us
  waiting for transfers between devices  317 us (76%)
  matrix products  22.5 us (5%)
  Pallas kernels  19.9 us (5%)
  other arithmetic  16.5 us (4%)
  local copies, waits for them, and re-layouts  13.4 us (3%)
  between operations  13.3 us (3%)
  starting transfers between devices  13.2 us (3%)
    reduce_scatter x1, waiting for transfers between devices, shards(): lax.psum_scatter(grad_part, 'tensor', scatter_dimension=1, tiled=True)  188 us
    all_gather x1, waiting for transfers between devices, shards(): all_grads = lax.all_gather(rot_grads, 'dp', axis=0, tiled=True)  42 us
    all_to_all x1, waiting for transfers between devices, shards(): rot_acts = lax.all_to_all(act_whole, 'dp', 0, 0, tiled=True)  28.7 us
    all_to_all x2, waiting for transfers between devices, redistribute(): return lax.all_to_all(x, 'dp', 0, 0, tiled=True)  26.6 us
    dot_general x1, matrix products, shards(): grad_part = jnp.dot(grads_p, basis_out, preferred_element_type=jnp.float32)  20.1 us
    pallas_call x1, Pallas kernels, shards(): pl.pallas_call(kernel, out_shape=jax.ShapeDtypeStruct((out_rows, in_cols)...  19.9 us
    reduce_scatter x1, waiting for transfers between devices, shards(): lax.psum_scatter(act_part, 'tensor', scatter_dimension=1, tiled=True)  18.9 us
    all_gather x1, waiting for transfers between devices, shards(): lax.all_gather(act_sum.astype(jnp.bfloat16), 'tensor', axis=1, tiled=True)  13.3 us
  transfers between devices with their start and end apart: 7, of which 6 were waited for; matrix products, arithmetic and copies ran while one was open for 9% of the time, Pallas kernels for 0%

profile of v5, /device:TPU:0, one launch (start us, length us, event | category | flops | bytes accessed | tf_op | source)
XLA Modules:
  0.0 416.2 jit_solution(858863250826972206)
XLA Ops:
  6.5 2.1 copy.14
  8.7 5.2 %all-to-all-start.1 = ((bf16[8,64,512]{2,1,0:T(8,128)(2,1)}), bf16[8,64,512]{2,1,0:T(8,128)(2,1)S(1)}, u32[]{:S(2)}, u32[]{:S(2)}) async-start(bf16[8,64,512]{2,1,0:T(8,128)(2,1)} %bitcast.22), calls=%async_computation.1 | async-start | bytes 1048576 | tf_op jit(solution)/shard_map/all_to_all | solution.py:18
  14.0 0.7 gather_fusion
  14.6 0.1 fusion.5
  14.8 0.2 dynamic-slice_reduce_fusion
  14.9 0.1 convert_reduce_fusion
  15.1 0.6 fusion.12
  15.7 4.3 %fusion.8 = (s32[336]{0:T(512)S(1)}, s32[336,1]{0,1:T(1,128)S(1)}) fusion(s32[]{:T(128)} %bitcast.13, s32[]{:T(128)} %bitcast.14, s32[]{:T(128)} %bitcast.15, s32[]{:T(128)} %bitcast.16, s32[]{:T(128)} %bitcast.17, s32[]{:T(128)} %bitcast.19, s32[]{:T(128)} %bitcast.18, s32[336]{0:T(512)S(1)} %broadcast_minimum_fusion), kind=kLoop, calls=%fused_computation.44 | loop fusion | flops 5040 | bytes 4060 | tf_op jit(solution)/shard_map/gather | solution.py:95
  20.0 5.7 %select_select_fusion = s32[336]{0:T(512)S(1)} fusion(pred[336]{0:T(512)(128)(4,1)S(1)} %get-tuple-element.17, pred[336]{0:T(512)(128)(4,1)S(1)} %get-tuple-element.16, pred[336]{0:T(512)(128)(4,1)S(1)} %get-tuple-element.15, pred[336]{0:T(512)(128)(4,1)S(1)} %get-tuple-element.14, pred[336]{0:T(512)(128)(4,1)S(1)} %get-tuple-element.13, ...), kind=kLoop, calls=%fused_computation.41 | loop fusion | flops 3024 | bytes 5748 | tf_op jit(solution)/shard_map/gather | solution.py:95
  25.8 2.0 gather_fusion.2
  27.8 2.4 fusion.13
  30.3 1.6 copy-done.4
  31.9 2.5 copy.13
  34.3 4.1 all-to-all-start
  38.5 26.6 %all-to-all-done = bf16[8,64,2048]{2,1,0:T(8,128)(2,1)S(1)} async-done(((bf16[8,64,2048]{2,1,0:T(8,128)(2,1)}), bf16[8,64,2048]{2,1,0:T(8,128)(2,1)S(1)}, u32[]{:S(2)}, u32[]{:S(2)}) %all-to-all-start) | async-done | bytes 2097184 | tf_op jit(solution)/shard_map/all_to_all | solution.py:18
  65.1 2.4 gather_fusion.1
  67.5 18.9 %reduce-scatter.3.cloned.1.call-done = f32[336,512]{1,0:T(8,128)} async-done(((f32[336,2048]{1,0:T(8,128)}), f32[336,512]{1,0:T(8,128)}) %reduce-scatter.3.cloned.1.call-update) | async-done | bytes 688144 | tf_op jit(solution)/shard_map/reduce_scatter | solution.py:104
  86.4 1.9 convert_element_type.10
  88.4 20.1 %fusion = f32[336,8192]{1,0:T(8,128)} fusion(bf16[2048,8192]{1,0:T(8,128)(2,1)} %param.8, bf16[336,2048]{1,0:T(8,128)(2,1)S(1)} %gather_fusion.1, pred[336]{0:T(512)(128)(4,1)S(1)} %broadcast_compare_fusion), kind=kOutput, calls=%fused_computation.4 | convolution fusion | flops 11274977280 | bytes 45941072 | tf_op jit(solution)/shard_map/dot_general | solution.py:106
  108.5 13.3 %all-gather.3.cloned.1.call-done = bf16[336,2048]{1,0:T(8,128)(2,1)} async-done(((bf16[336,512]{1,0:T(8,128)(2,1)}), bf16[336,2048]{1,0:T(8,128)(2,1)}) %all-gather.3.cloned.1.call-update) | async-done | bytes 1376272 | tf_op jit(solution)/shard_map/all_gather | solution.py:105
  121.8 187.8 %reduce-scatter.5.cloned.1.call-done = f32[336,2048]{1,0:T(8,128)} async-done(((f32[336,8192]{1,0:T(8,128)}), f32[336,2048]{1,0:T(8,128)}) %reduce-scatter.5.cloned.1.call-update) | async-done | bytes 2752528 | tf_op jit(solution)/shard_map/reduce_scatter | solution.py:112
  309.7 3.1 convert_element_type.11
  312.8 1.2 copy.18
  313.9 3.7 all-to-all-start.2
  317.6 0.1 reduce_window_sum.14
  317.7 0.1 add.69
  317.8 0.1 sub.63
  317.9 0.6 fusion.11
  318.5 0.5 multiply_minimum_fusion.win_ref
  319.0 28.7 %all-to-all-done.2 = bf16[8,336,256]{2,1,0:T(8,128)(2,1)S(1)} async-done(((bf16[8,336,256]{2,1,0:T(8,128)(2,1)}), bf16[8,336,256]{2,1,0:T(8,128)(2,1)S(1)}, u32[]{:S(2)}, u32[]{:S(2)}) %all-to-all-start.2) | async-done | bytes 1376288 | tf_op jit(solution)/shard_map/all_to_all | solution.py:110
  347.7 42.0 %all-gather.5.cloned.1.call-done.grads_hbm = bf16[2688,2048]{1,0:T(8,128)(2,1)} async-done(((bf16[336,2048]{1,0:T(8,128)(2,1)}), bf16[2688,2048]{1,0:T(8,128)(2,1)}) %all-gather.5.cloned.1.call-update) | async-done | bytes 11010064 | tf_op jit(solution)/shard_map/all_gather | solution.py:114
  389.7 19.9 %shard_map.64 = f32[2048,256]{1,0:T(8,128)} custom-call(s32[128]{0:T(128)} %multiply_minimum_fusion.win_ref, s32[128]{0:T(128)} %copy-done.6, s32[128]{0:T(128)} %get-tuple-element.20.hi_ref, bf16[2688,2048]{1,0:T(8,128)(2,1)} %all-gather.5.cloned.1.call-done.grads_hbm, bf16[2688,256]{1,0:T(8,128)(2,1)} %bitcast.40), custom_call_target="tpu_custom_call" | custom-call | tf_op jit(solution)/shard_map/pallas_call | solution.py:122
  (34 shorter events, 0.4 us)
Async XLA Ops:
  6.5 21.3 %copy-start = (bf16[512,2048]{1,0:T(8,128)(2,1)S(1)}, bf16[512,2048]{1,0:T(8,128)(2,1)}, u32[]{:S(2)}) copy-start(bf16[512,2048]{1,0:T(8,128)(2,1)} %param.9) | copy-start | bytes 6291460
  6.5 7.4 %copy-start.7 = (s32[16]{0:T(128)S(1)}, s32[16]{0:T(128)}, u32[]{:S(2)}) copy-start(s32[16]{0:T(128)} %param.10) | copy-start | bytes 196
  6.5 7.4 %copy-start.2 = (s32[16]{0:T(128)S(1)}, s32[16]{0:T(128)}, u32[]{:S(2)}) copy-start(s32[16]{0:T(128)} %param.11) | copy-start | bytes 196
  8.7 17.1 %all-to-all-start.1 = ((bf16[8,64,512]{2,1,0:T(8,128)(2,1)}), bf16[8,64,512]{2,1,0:T(8,128)(2,1)S(1)}, u32[]{:S(2)}, u32[]{:S(2)}) async-start(bf16[8,64,512]{2,1,0:T(8,128)(2,1)} %bitcast.22), calls=%async_computation.1 | async-start | bytes 1048576 | tf_op jit(solution)/shard_map/all_to_all | solution.py:18
  13.9 72.5 %reduce-scatter.3.cloned.1.call-start = ((), (), s32[]{:S(2)}) async-start(), calls=%async_computation.5 | async-start | bytes 3440640 | tf_op jit(solution)/shard_map/reduce_scatter | solution.py:104
  30.3 1.6 copy-start.4
  34.3 30.8 %all-to-all-start = ((bf16[8,64,2048]{2,1,0:T(8,128)(2,1)}), bf16[8,64,2048]{2,1,0:T(8,128)(2,1)S(1)}, u32[]{:S(2)}, u32[]{:S(2)}) async-start(bf16[8,64,2048]{2,1,0:T(8,128)(2,1)} %bitcast.39), calls=%async_computation | async-start | bytes 4194304 | tf_op jit(solution)/shard_map/all_to_all | solution.py:18
  38.5 83.3 %all-gather.3.cloned.1.call-start = ((), (), s32[]{:S(2)}) async-start(), calls=%async_computation.6 | async-start | bytes 1720320 | tf_op jit(solution)/shard_map/all_gather | solution.py:105
  88.3 221.4 %reduce-scatter.5.cloned.1.call-start = ((), (), s32[]{:S(2)}) async-start(), calls=%async_computation.7 | async-start | bytes 13762560 | tf_op jit(solution)/shard_map/reduce_scatter | solution.py:112
  121.8 191.0 %copy-start.5 = (bf16[336,2048]{1,0:T(8,128)(2,1)S(1)}, bf16[336,2048]{1,0:T(8,128)(2,1)}, u32[]{:S(2)}) copy-start(bf16[336,2048]{1,0:T(8,128)(2,1)} %all-gather.3.cloned.1.call-done) | copy-start | bytes 4128772
  121.8 267.9 %all-gather.5.cloned.1.call-start = ((), (), s32[]{:S(2)}) async-start(), calls=%async_computation.8 | async-start | bytes 12386304 | tf_op jit(solution)/shard_map/all_gather | solution.py:114
  313.9 33.8 %all-to-all-start.2 = ((bf16[8,336,256]{2,1,0:T(8,128)(2,1)}), bf16[8,336,256]{2,1,0:T(8,128)(2,1)S(1)}, u32[]{:S(2)}, u32[]{:S(2)}) async-start(bf16[8,336,256]{2,1,0:T(8,128)(2,1)} %bitcast.36), calls=%async_computation.4 | async-start | bytes 2752512 | tf_op jit(solution)/shard_map/all_to_all | solution.py:110
  318.5 71.2 %copy-start.6 = (s32[128]{0:T(128)}, s32[128]{0:T(128)S(1)}, u32[]{:S(2)}) copy-start(s32[128]{0:T(128)S(1)} %get-tuple-element.21.lo_ref) | copy-start | bytes 1540
  347.7 42.0 %copy-start.3 = (bf16[8,336,256]{2,1,0:T(8,128)(2,1)}, bf16[8,336,256]{2,1,0:T(8,128)(2,1)S(1)}, u32[]{:S(2)}) copy-start(bf16[8,336,256]{2,1,0:T(8,128)(2,1)S(1)} %all-to-all-done.2) | copy-start | bytes 4128772
  389.7 20.0 %copy-start.1 = (bf16[512,2048]{1,0:T(8,128)(2,1)S(1)}, bf16[512,2048]{1,0:T(8,128)(2,1)}, u32[]{:S(2)}) copy-start(bf16[512,2048]{1,0:T(8,128)(2,1)} %param.9) | copy-start | bytes 6291460
Sparse Core Ops, SparseCore 0:
  30.4 55.9 reduce-scatter.2
  88.4 33.2 all-gather.2
  124.1 185.5 reduce-scatter.4
  312.9 76.7 all-gather.4

commit v6 on v5

--- a/solution.py
+++ b/solution.py
@@ -110,6 +110,7 @@
     rot_acts = lax.all_to_all(act_whole, "dp", 0, 0, tiled=True)
 
     rot_grads = lax.psum_scatter(grad_part, "tensor", scatter_dimension=1, tiled=True)
+    rot_grads, rot_acts = lax.optimization_barrier((rot_grads, rot_acts))
     rot_grads = rot_grads.astype(jnp.bfloat16)
     all_grads = lax.all_gather(rot_grads, "dp", axis=0, tiled=True)
 

time: 417 us -> 406 us (0.974)
  waiting for transfers between devices: 317 us -> 287 us
  blocking collectives: 0 us -> 22.4 us
    all_to_all x1 -> x0, waiting for transfers between devices: 28.7 us -> none  [shards(): rot_acts = lax.all_to_all(act_whole, 'dp', 0, 0, tiled=True)]
    reduce_scatter x1, waiting for transfers between devices: 188 us -> 164 us  [shards(): lax.psum_scatter(grad_part, 'tensor', scatter_dimension=1, tiled=True)]
    all_gather x1, waiting for transfers between devices: 42 us -> 65.2 us  [shards(): all_grads = lax.all_gather(rot_grads, 'dp', axis=0, tiled=True)]
    all_to_all x0 -> x1, blocking collectives: none -> 22.4 us  [shards(): rot_acts = lax.all_to_all(act_whole, 'dp', 0, 0, tiled=True)]
  transfers between devices with their start and end apart: 7 -> 6, of which waited for: 6 -> 5; matrix products, arithmetic and copies ran while one was open for 9% -> 10% of each run, Pallas kernels for 0% -> 0%
where the time goes in v6:
time: 406 us; the launch traced here: 405 us
  waiting for transfers between devices  287 us (71%)
  matrix products  22.9 us (6%)
  blocking collectives  22.4 us (6%)
  Pallas kernels  19.6 us (5%)
  other arithmetic  16.4 us (4%)
  local copies, waits for them, and re-layouts  14.3 us (4%)
  between operations  13.3 us (3%)
  starting transfers between devices  9.5 us (2%)
    reduce_scatter x1, waiting for transfers between devices, shards(): lax.psum_scatter(grad_part, 'tensor', scatter_dimension=1, tiled=True)  164 us
    all_gather x1, waiting for transfers between devices, shards(): all_grads = lax.all_gather(rot_grads, 'dp', axis=0, tiled=True)  65.2 us
    all_to_all x2, waiting for transfers between devices, redistribute(): return lax.all_to_all(x, 'dp', 0, 0, tiled=True)  26.6 us
    all_to_all x1, blocking collectives, shards(): rot_acts = lax.all_to_all(act_whole, 'dp', 0, 0, tiled=True)  22.4 us
    dot_general x1, matrix products, shards(): grad_part = jnp.dot(grads_p, basis_out, preferred_element_type=jnp.float32)  20.5 us
    pallas_call x1, Pallas kernels, shards(): pl.pallas_call(kernel, out_shape=jax.ShapeDtypeStruct((out_rows, in_cols)...  19.6 us
    reduce_scatter x1, waiting for transfers between devices, shards(): lax.psum_scatter(act_part, 'tensor', scatter_dimension=1, tiled=True)  18.3 us
    all_gather x1, waiting for transfers between devices, shards(): lax.all_gather(act_sum.astype(jnp.bfloat16), 'tensor', axis=1, tiled=True)  12.9 us
  transfers between devices with their start and end apart: 6, of which 5 were waited for; matrix products, arithmetic and copies ran while one was open for 10% of the time, Pallas kernels for 0%

profile of v6, /device:TPU:0, one launch (start us, length us, event | category | flops | bytes accessed | tf_op | source)
XLA Modules:
  0.0 405.5 jit_solution(14457768366759974681)
XLA Ops:
  6.5 2.1 copy.14
  8.7 5.2 %all-to-all-start.1 = ((bf16[8,64,512]{2,1,0:T(8,128)(2,1)}), bf16[8,64,512]{2,1,0:T(8,128)(2,1)S(1)}, u32[]{:S(2)}, u32[]{:S(2)}) async-start(bf16[8,64,512]{2,1,0:T(8,128)(2,1)} %bitcast.22), calls=%async_computation.1 | async-start | bytes 1048576 | tf_op jit(solution)/shard_map/all_to_all | solution.py:18
  14.0 0.7 gather_fusion
  14.6 0.1 fusion.5
  14.8 0.2 dynamic-slice_reduce_fusion
  14.9 0.1 convert_reduce_fusion
  15.1 0.6 fusion.12
  15.7 4.3 %fusion.8 = (s32[336]{0:T(512)S(1)}, s32[336,1]{0,1:T(1,128)S(1)}) fusion(s32[]{:T(128)} %bitcast.13, s32[]{:T(128)} %bitcast.14, s32[]{:T(128)} %bitcast.15, s32[]{:T(128)} %bitcast.16, s32[]{:T(128)} %bitcast.17, s32[]{:T(128)} %bitcast.19, s32[]{:T(128)} %bitcast.18, s32[336]{0:T(512)S(1)} %broadcast_minimum_fusion), kind=kLoop, calls=%fused_computation.44 | loop fusion | flops 5040 | bytes 4060 | tf_op jit(solution)/shard_map/gather | solution.py:95
  20.0 0.1 compare_reduce_fusion.8
  20.0 5.7 %select_select_fusion = s32[336]{0:T(512)S(1)} fusion(pred[336]{0:T(512)(128)(4,1)S(1)} %get-tuple-element.21, pred[336]{0:T(512)(128)(4,1)S(1)} %get-tuple-element.20, pred[336]{0:T(512)(128)(4,1)S(1)} %get-tuple-element.19, pred[336]{0:T(512)(128)(4,1)S(1)} %get-tuple-element.18, pred[336]{0:T(512)(128)(4,1)S(1)} %get-tuple-element.17, ...), kind=kLoop, calls=%fused_computation.41 | loop fusion | flops 3024 | bytes 5748 | tf_op jit(solution)/shard_map/gather | solution.py:95
  25.8 2.0 gather_fusion.2
  27.8 2.4 fusion.13
  30.3 1.6 copy-done.3
  31.9 2.5 copy.13
  34.3 4.1 %all-to-all-start = ((bf16[8,64,2048]{2,1,0:T(8,128)(2,1)}), bf16[8,64,2048]{2,1,0:T(8,128)(2,1)S(1)}, u32[]{:S(2)}, u32[]{:S(2)}) async-start(bf16[8,64,2048]{2,1,0:T(8,128)(2,1)} %bitcast.39), calls=%async_computation | async-start | bytes 4194304 | tf_op jit(solution)/shard_map/all_to_all | solution.py:18
  38.5 26.6 %all-to-all-done = bf16[8,64,2048]{2,1,0:T(8,128)(2,1)S(1)} async-done(((bf16[8,64,2048]{2,1,0:T(8,128)(2,1)}), bf16[8,64,2048]{2,1,0:T(8,128)(2,1)S(1)}, u32[]{:S(2)}, u32[]{:S(2)}) %all-to-all-start) | async-done | bytes 2097184 | tf_op jit(solution)/shard_map/all_to_all | solution.py:18
  65.1 3.0 gather_fusion.1
  68.1 18.3 %reduce-scatter.3.cloned.1.call-done = f32[336,512]{1,0:T(8,128)} async-done(((f32[336,2048]{1,0:T(8,128)}), f32[336,512]{1,0:T(8,128)}) %reduce-scatter.3.cloned.1.call-update) | async-done | bytes 688144 | tf_op jit(solution)/shard_map/reduce_scatter | solution.py:104
  86.4 1.9 convert_element_type.10
  88.4 20.5 %fusion = f32[336,8192]{1,0:T(8,128)} fusion(bf16[2048,8192]{1,0:T(8,128)(2,1)} %param.8, bf16[336,2048]{1,0:T(8,128)(2,1)} %gather_fusion.1, pred[336]{0:T(512)(128)(4,1)S(1)} %broadcast_compare_fusion), kind=kOutput, calls=%fused_computation.4 | convolution fusion | flops 11274977280 | bytes 45941072 | tf_op jit(solution)/shard_map/dot_general | solution.py:106
  108.9 12.9 %all-gather.3.cloned.1.call-done = bf16[336,2048]{1,0:T(8,128)(2,1)} async-done(((bf16[336,512]{1,0:T(8,128)(2,1)}), bf16[336,2048]{1,0:T(8,128)(2,1)}) %all-gather.3.cloned.1.call-update) | async-done | bytes 1376272 | tf_op jit(solution)/shard_map/all_gather | solution.py:105
  121.8 1.4 copy.18
  123.3 22.4 %all_to_all.33 = bf16[8,336,256]{2,1,0:T(8,128)(2,1)} all-to-all(bf16[8,336,256]{2,1,0:T(8,128)(2,1)S(1)} %bitcast.41), channel_id=1, replica_groups=mesh['dp'=8,'tensor'=4] {'dp'}, dimensions={0} | all-to-all | bytes 2752512 | tf_op jit(solution)/shard_map/all_to_all | solution.py:110
  145.7 164.0 %reduce-scatter.5.cloned.1.call-done = f32[336,2048]{1,0:T(8,128)} async-done(((f32[336,8192]{1,0:T(8,128)}), f32[336,2048]{1,0:T(8,128)}) %reduce-scatter.5.cloned.1.call-update) | async-done | bytes 2752528 | tf_op jit(solution)/shard_map/reduce_scatter | solution.py:112
  309.7 3.1 convert_element_type.11
  312.8 0.1 reduce_window_sum.14
  312.9 0.1 add.69
  313.0 0.1 sub.63
  313.1 0.5 fusion.11
  313.6 0.5 multiply_minimum_fusion.win_ref
  314.1 65.2 %all-gather.5.cloned.1.call-done.grads_hbm = bf16[2688,2048]{1,0:T(8,128)(2,1)} async-done(((bf16[336,2048]{1,0:T(8,128)(2,1)}), bf16[2688,2048]{1,0:T(8,128)(2,1)}) %all-gather.5.cloned.1.call-update) | async-done | bytes 11010064 | tf_op jit(solution)/shard_map/all_gather | solution.py:115
  379.3 19.6 %shard_map.64 = f32[2048,256]{1,0:T(8,128)} custom-call(s32[128]{0:T(128)} %multiply_minimum_fusion.win_ref, s32[128]{0:T(128)} %copy-done.4, s32[128]{0:T(128)} %get-tuple-element.24.hi_ref, bf16[2688,2048]{1,0:T(8,128)(2,1)} %all-gather.5.cloned.1.call-done.grads_hbm, bf16[2688,256]{1,0:T(8,128)(2,1)} %bitcast.40), custom_call_target="tpu_custom_call" | custom-call | tf_op jit(solution)/shard_map/pallas_call | solution.py:123
  (29 shorter events, 0.3 us)
Async XLA Ops:
  6.5 21.3 %copy-start = (bf16[512,2048]{1,0:T(8,128)(2,1)S(1)}, bf16[512,2048]{1,0:T(8,128)(2,1)}, u32[]{:S(2)}) copy-start(bf16[512,2048]{1,0:T(8,128)(2,1)} %param.9) | copy-start | bytes 6291460
  6.5 7.4 %copy-start.5 = (s32[16]{0:T(128)S(1)}, s32[16]{0:T(128)}, u32[]{:S(2)}) copy-start(s32[16]{0:T(128)} %param.10) | copy-start | bytes 196
  6.5 7.4 %copy-start.2 = (s32[16]{0:T(128)S(1)}, s32[16]{0:T(128)}, u32[]{:S(2)}) copy-start(s32[16]{0:T(128)} %param.11) | copy-start | bytes 196
  8.7 17.1 %all-to-all-start.1 = ((bf16[8,64,512]{2,1,0:T(8,128)(2,1)}), bf16[8,64,512]{2,1,0:T(8,128)(2,1)S(1)}, u32[]{:S(2)}, u32[]{:S(2)}) async-start(bf16[8,64,512]{2,1,0:T(8,128)(2,1)} %bitcast.22), calls=%async_computation.1 | async-start | bytes 1048576 | tf_op jit(solution)/shard_map/all_to_all | solution.py:18
  13.9 72.5 %reduce-scatter.3.cloned.1.call-start = ((), (), s32[]{:S(2)}) async-start(), calls=%async_computation.5 | async-start | bytes 3440640 | tf_op jit(solution)/shard_map/reduce_scatter | solution.py:104
  30.3 1.6 copy-start.3
  34.3 30.8 %all-to-all-start = ((bf16[8,64,2048]{2,1,0:T(8,128)(2,1)}), bf16[8,64,2048]{2,1,0:T(8,128)(2,1)S(1)}, u32[]{:S(2)}, u32[]{:S(2)}) async-start(bf16[8,64,2048]{2,1,0:T(8,128)(2,1)} %bitcast.39), calls=%async_computation | async-start | bytes 4194304 | tf_op jit(solution)/shard_map/all_to_all | solution.py:18
  38.5 83.3 %all-gather.3.cloned.1.call-start = ((), (), s32[]{:S(2)}) async-start(), calls=%async_computation.6 | async-start | bytes 1720320 | tf_op jit(solution)/shard_map/all_gather | solution.py:105
  88.3 221.4 %reduce-scatter.5.cloned.1.call-start = ((), (), s32[]{:S(2)}) async-start(), calls=%async_computation.7 | async-start | bytes 13762560 | tf_op jit(solution)/shard_map/reduce_scatter | solution.py:112
  121.8 257.5 %all-gather.5.cloned.1.call-start = ((), (), s32[]{:S(2)}) async-start(), calls=%async_computation.8 | async-start | bytes 12386304 | tf_op jit(solution)/shard_map/all_gather | solution.py:115
  313.6 65.8 %copy-start.4 = (s32[128]{0:T(128)}, s32[128]{0:T(128)S(1)}, u32[]{:S(2)}) copy-start(s32[128]{0:T(128)S(1)} %get-tuple-element.25.lo_ref) | copy-start | bytes 1540
  379.3 19.6 %copy-start.1 = (bf16[512,2048]{1,0:T(8,128)(2,1)S(1)}, bf16[512,2048]{1,0:T(8,128)(2,1)}, u32[]{:S(2)}) copy-start(bf16[512,2048]{1,0:T(8,128)(2,1)} %param.9) | copy-start | bytes 6291460
Sparse Core Ops, SparseCore 0:
  30.4 55.9 reduce-scatter.2
  88.4 33.2 all-gather.2
  124.1 185.5 reduce-scatter.4
  312.9 66.3 all-gather.4

commit v7 on v6

--- a/solution.py
+++ b/solution.py
@@ -70,7 +70,7 @@
         out_ref[...] = out_ref[...] * scale
 
 
-def shards(acts, out_grads, basis_out, basis_in, slot_sequence, seq_lengths, *, dp):
+def shards(acts, out_grads, basis_out, basis_in, slot_sequence, seq_lengths, *, dp, tp):
     tok_rows = acts.shape[0]
     local_slots = tok_rows // LEN
     nseq = seq_lengths.shape[0]
@@ -101,10 +101,14 @@
     acts_p = jnp.take(acts_r, src, axis=0, mode="clip")
 
     act_part = jnp.dot(acts_p, basis_in, preferred_element_type=jnp.float32)
-    act_sum = lax.psum_scatter(act_part, "tensor", scatter_dimension=1, tiled=True)
-    act_whole = lax.all_gather(act_sum.astype(jnp.bfloat16), "tensor", axis=1, tiled=True)
+    quarter = act_part.shape[1] // tp
+    blocks = act_part.reshape(cap, tp, quarter).transpose(1, 0, 2).reshape(-1, quarter)
+    act_sum = jnp.sum(lax.all_to_all(blocks, "tensor", 0, 0, tiled=True).reshape(tp, cap, quarter), axis=0)
+    act_sum = act_sum.astype(jnp.bfloat16)
+    sent = jnp.broadcast_to(act_sum[None], (tp,) + act_sum.shape).reshape(-1, quarter)
+    act_whole = lax.all_to_all(sent, "tensor", 0, 0, tiled=True).reshape(tp, cap, quarter)
+    act_whole = act_whole.transpose(1, 0, 2).reshape(cap, tp * quarter)
     grad_part = jnp.dot(grads_p, basis_out, preferred_element_type=jnp.float32)
-    grad_part, act_whole = lax.optimization_barrier((grad_part, act_whole))
     in_cols = act_whole.shape[1] // dp
     act_whole = act_whole.reshape(cap, dp, in_cols).transpose(1, 0, 2).reshape(-1, in_cols)
     rot_acts = lax.all_to_all(act_whole, "dp", 0, 0, tiled=True)
@@ -140,9 +144,10 @@
 
 def solution(mesh):
     dp = mesh.shape["dp"]
+    tp = mesh.shape["tensor"]
 
     def body(*args):
-        return shards(*args, dp=dp)
+        return shards(*args, dp=dp, tp=tp)
 
     return jax.shard_map(
         body,

time: 406 us -> 439 us (1.081)
  blocking collectives: 22.4 us -> 247 us
  waiting for transfers between devices: 287 us -> 95.2 us
  local copies, waits for them, and re-layouts: 14.3 us -> 19.6 us
    all_to_all x0 -> x3, blocking collectives: none -> 225 us  [the longest x1 141 us: shards(): lax.all_to_all(blocks, 'tensor', 0, 0, tiled=True).reshape(tp, cap, quarter)]
    reduce_scatter x1, waiting for transfers between devices: 164 us -> 8.68 us  [shards(): lax.psum_scatter(grad_part, 'tensor', scatter_dimension=1, tiled=True)]
    reduce_scatter x1 -> x0, waiting for transfers between devices: 18.3 us -> none  [shards(): lax.psum_scatter(act_part, 'tensor', scatter_dimension=1, tiled=True)]
    all_gather x1 -> x0, waiting for transfers between devices: 12.9 us -> none  [shards(): lax.all_gather(act_sum.astype(jnp.bfloat16), 'tensor', axis=1, tiled=True)]
    all_to_all x2 -> x1, waiting for transfers between devices: 26.6 us -> 14.8 us  [redistribute(): return lax.all_to_all(x, 'dp', 0, 0, tiled=True)]
    all_gather x1, waiting for transfers between devices: 65.2 us -> 71.7 us  [shards(): all_grads = lax.all_gather(rot_grads, 'dp', axis=0, tiled=True)]
    all_to_all x2 -> x1, starting transfers between devices: 9.35 us -> 5.33 us  [redistribute(): return lax.all_to_all(x, 'dp', 0, 0, tiled=True)]
  transfers between devices with their start and end apart: 6 -> 3, of which waited for: 5 -> 3; matrix products, arithmetic and copies ran while one was open for 10% -> 5% of each run, Pallas kernels for 0% -> 0%
where the time goes in v7:
time: 439 us; the launch traced here: 438 us
  blocking collectives  247 us (56%)
  waiting for transfers between devices  95.2 us (22%)
  matrix products  21 us (5%)
  local copies, waits for them, and re-layouts  19.6 us (4%)
  Pallas kernels  19.2 us (4%)
  other arithmetic  16.7 us (4%)
  between operations  13.6 us (3%)
  starting transfers between devices  5.41 us (1%)
    all_to_all x1, blocking collectives, shards(): lax.all_to_all(blocks, 'tensor', 0, 0, tiled=True).reshape(tp, cap, quarter)  141 us
    all_to_all x1, blocking collectives, shards(): lax.all_to_all(sent, 'tensor', 0, 0, tiled=True).reshape(tp, cap, quarter)  72.2 us
    all_gather x1, waiting for transfers between devices, shards(): all_grads = lax.all_gather(rot_grads, 'dp', axis=0, tiled=True)  71.7 us
    all_to_all x1, blocking collectives, shards(): rot_acts = lax.all_to_all(act_whole, 'dp', 0, 0, tiled=True)  22 us
    dot_general x1, matrix products, shards(): grad_part = jnp.dot(grads_p, basis_out, preferred_element_type=jnp.float32)  20.1 us
    pallas_call x1, Pallas kernels, shards(): pl.pallas_call(kernel, out_shape=jax.ShapeDtypeStruct((out_rows, in_cols)...  19.2 us
    all_to_all x1, waiting for transfers between devices, redistribute(): return lax.all_to_all(x, 'dp', 0, 0, tiled=True)  14.8 us
    all_to_all x1, blocking collectives, redistribute(): return lax.all_to_all(x, 'dp', 0, 0, tiled=True)  12.1 us
  transfers between devices with their start and end apart: 3, of which 3 were waited for; matrix products, arithmetic and copies ran while one was open for 5% of the time, Pallas kernels for 0%

profile of v7, /device:TPU:0, one launch (start us, length us, event | category | flops | bytes accessed | tf_op | source)
XLA Modules:
  0.0 437.9 jit_solution(13996006882173773406)
XLA Ops:
  6.5 4.2 copy.17
  10.8 5.3 %all-to-all-start = ((bf16[8,64,2048]{2,1,0:T(8,128)(2,1)}), bf16[8,64,2048]{2,1,0:T(8,128)(2,1)}, u32[]{:S(2)}, u32[]{:S(2)}) async-start(bf16[8,64,2048]{2,1,0:T(8,128)(2,1)} %bitcast.42), calls=%async_computation | async-start | bytes 4194304 | tf_op jit(solution)/shard_map/all_to_all | solution.py:18
  16.2 0.7 gather_fusion
  16.8 0.1 fusion.5
  17.0 0.2 dynamic-slice_reduce_fusion
  17.2 0.6 fusion.12
  17.9 4.3 fusion.8
  22.2 5.7 %select_select_fusion = s32[336]{0:T(512)S(1)} fusion(pred[336]{0:T(512)(128)(4,1)S(1)} %get-tuple-element.17, pred[336]{0:T(512)(128)(4,1)S(1)} %get-tuple-element.16, pred[336]{0:T(512)(128)(4,1)S(1)} %get-tuple-element.15, pred[336]{0:T(512)(128)(4,1)S(1)} %get-tuple-element.14, pred[336]{0:T(512)(128)(4,1)S(1)} %get-tuple-element.13, ...), kind=kLoop, calls=%fused_computation.41 | loop fusion | flops 3024 | bytes 5748 | tf_op jit(solution)/shard_map/gather | solution.py:95
  28.0 14.8 %all-to-all-done = bf16[8,64,2048]{2,1,0:T(8,128)(2,1)} async-done(((bf16[8,64,2048]{2,1,0:T(8,128)(2,1)}), bf16[8,64,2048]{2,1,0:T(8,128)(2,1)}, u32[]{:S(2)}, u32[]{:S(2)}) %all-to-all-start) | async-done | bytes 2097184 | tf_op jit(solution)/shard_map/all_to_all | solution.py:18
  42.8 6.2 %gather_fusion.1 = bf16[336,2048]{1,0:T(8,128)(2,1)S(1)} fusion(bf16[512,2048]{1,0:T(8,128)(2,1)} %bitcast.3, s32[1024]{0:T(1024)S(1)} %pad_clamp_fusion), kind=kCustom, calls=%fused_computation.1 | custom fusion | bytes 2753856 | tf_op jit(solution)/shard_map/jit(_take)/gather | solution.py:98
  49.1 20.1 %fusion = f32[336,8192]{1,0:T(8,128)} fusion(bf16[2048,8192]{1,0:T(8,128)(2,1)} %param.8, bf16[336,2048]{1,0:T(8,128)(2,1)S(1)} %gather_fusion.1, pred[336]{0:T(512)(128)(4,1)S(1)} %broadcast_compare_fusion), kind=kOutput, calls=%fused_computation.4 | convolution fusion | flops 11274977280 | bytes 45941072 | tf_op jit(solution)/shard_map/dot_general | solution.py:111
  69.2 1.0 copy-done.2
  70.2 0.2 copy.18
  70.4 12.1 %all_to_all.45 = bf16[8,64,512]{2,1,0:T(8,128)(2,1)S(1)} all-to-all(bf16[8,64,512]{2,1,0:T(8,128)(2,1)S(1)} %bitcast.47), channel_id=1, replica_groups=mesh['dp'=8,'tensor'=4] {'dp'}, dimensions={0} | all-to-all | bytes 1048576 | tf_op jit(solution)/shard_map/all_to_all | solution.py:18
  82.5 2.0 gather_fusion.2
  84.5 0.9 fusion.13
  85.4 0.3 copy.24
  85.7 141.1 %all_to_all.46 = f32[4,336,512]{2,1,0:T(8,128)} all-to-all(f32[4,336,512]{2,1,0:T(8,128)S(1)} %bitcast.41), channel_id=1, replica_groups=mesh['dp'=8,'tensor'=4] {'tensor'}, dimensions={0} | all-to-all | bytes 5505024 | tf_op jit(solution)/shard_map/all_to_all | solution.py:106
  226.8 2.1 reduce_sum.19
  228.9 0.1 broadcast_in_dim.21
  229.0 72.2 %all_to_all.47 = bf16[4,336,512]{2,1,0:T(8,128)(2,1)S(1)} all-to-all(bf16[4,336,512]{2,1,0:T(8,128)(2,1)S(1)} %broadcast_in_dim.21), channel_id=1, replica_groups=mesh['dp'=8,'tensor'=4] {'tensor'}, dimensions={0} | all-to-all | bytes 2752512 | tf_op jit(solution)/shard_map/all_to_all | solution.py:109
  301.2 1.1 copy.20
  302.3 1.3 reshape_reshape.3
  303.5 1.6 copy.21
  305.1 22.0 %all_to_all.48 = bf16[8,336,256]{2,1,0:T(8,128)(2,1)} all-to-all(bf16[8,336,256]{2,1,0:T(8,128)(2,1)S(1)} %copy.21), channel_id=1, replica_groups=mesh['dp'=8,'tensor'=4] {'dp'}, dimensions={0} | all-to-all | bytes 2752512 | tf_op jit(solution)/shard_map/all_to_all | solution.py:114
  327.1 8.7 %reduce-scatter.2.cloned.1.call-done = f32[336,2048]{1,0:T(8,128)} async-done(((f32[336,8192]{1,0:T(8,128)}), f32[336,2048]{1,0:T(8,128)}) %reduce-scatter.2.cloned.1.call-update) | async-done | bytes 2752528 | tf_op jit(solution)/shard_map/reduce_scatter | solution.py:116
  335.8 3.1 convert_element_type.15
  339.0 0.1 sub.63
  339.2 0.5 fusion.11
  339.7 0.5 multiply_minimum_fusion.win_ref
  340.2 71.7 %all-gather.2.cloned.1.call-done.grads_hbm = bf16[2688,2048]{1,0:T(8,128)(2,1)} async-done(((bf16[336,2048]{1,0:T(8,128)(2,1)}), bf16[2688,2048]{1,0:T(8,128)(2,1)}) %all-gather.2.cloned.1.call-update) | async-done | bytes 11010064 | tf_op jit(solution)/shard_map/all_gather | solution.py:119
  411.9 19.2 %shard_map.64 = f32[2048,256]{1,0:T(8,128)} custom-call(s32[128]{0:T(128)} %multiply_minimum_fusion.win_ref, s32[128]{0:T(128)} %copy-done.3, s32[128]{0:T(128)} %get-tuple-element.20.hi_ref, bf16[2688,2048]{1,0:T(8,128)(2,1)} %all-gather.2.cloned.1.call-done.grads_hbm, bf16[2688,256]{1,0:T(8,128)(2,1)} %bitcast.43), custom_call_target="tpu_custom_call" | custom-call | tf_op jit(solution)/shard_map/pallas_call | solution.py:127
  (26 shorter events, 0.5 us)
Async XLA Ops:
  6.5 78.0 %copy-start = (bf16[512,2048]{1,0:T(8,128)(2,1)S(1)}, bf16[512,2048]{1,0:T(8,128)(2,1)}, u32[]{:S(2)}) copy-start(bf16[512,2048]{1,0:T(8,128)(2,1)} %param.9) | copy-start | bytes 6291460
  10.7 5.4 %copy-start.4 = (s32[16]{0:T(128)S(1)}, s32[16]{0:T(128)}, u32[]{:S(2)}) copy-start(s32[16]{0:T(128)} %param.10) | copy-start | bytes 196
  10.8 5.4 %copy-start.1 = (s32[16]{0:T(128)S(1)}, s32[16]{0:T(128)}, u32[]{:S(2)}) copy-start(s32[16]{0:T(128)} %param.11) | copy-start | bytes 196
  10.8 32.0 %all-to-all-start = ((bf16[8,64,2048]{2,1,0:T(8,128)(2,1)}), bf16[8,64,2048]{2,1,0:T(8,128)(2,1)}, u32[]{:S(2)}, u32[]{:S(2)}) async-start(bf16[8,64,2048]{2,1,0:T(8,128)(2,1)} %bitcast.42), calls=%async_computation | async-start | bytes 4194304 | tf_op jit(solution)/shard_map/all_to_all | solution.py:18
  16.1 319.7 %reduce-scatter.2.cloned.1.call-start = ((), (), s32[]{:S(2)}) async-start(), calls=%async_computation.6 | async-start | bytes 13762560 | tf_op jit(solution)/shard_map/reduce_scatter | solution.py:116
  69.2 1.0 copy-start.2
  69.2 342.7 %all-gather.2.cloned.1.call-start = ((), (), s32[]{:S(2)}) async-start(), calls=%async_computation.7 | async-start | bytes 12386304 | tf_op jit(solution)/shard_map/all_gather | solution.py:119
  339.7 72.2 %copy-start.3 = (s32[128]{0:T(128)}, s32[128]{0:T(128)S(1)}, u32[]{:S(2)}) copy-start(s32[128]{0:T(128)S(1)} %get-tuple-element.21.lo_ref) | copy-start | bytes 1540
Sparse Core Ops, SparseCore 0:
  69.3 266.4 reduce-scatter.1
  339.0 72.8 all-gather.1

commit v8 on v6

--- a/solution.py
+++ b/solution.py
@@ -70,7 +70,7 @@
         out_ref[...] = out_ref[...] * scale
 
 
-def shards(acts, out_grads, basis_out, basis_in, slot_sequence, seq_lengths, *, dp):
+def shards(acts, out_grads, basis_out, basis_in, slot_sequence, seq_lengths, *, dp, tp):
     tok_rows = acts.shape[0]
     local_slots = tok_rows // LEN
     nseq = seq_lengths.shape[0]
@@ -100,9 +100,12 @@
     acts_r = redistribute(acts, dp)
     acts_p = jnp.take(acts_r, src, axis=0, mode="clip")
 
-    act_part = jnp.dot(acts_p, basis_in, preferred_element_type=jnp.float32)
-    act_sum = lax.psum_scatter(act_part, "tensor", scatter_dimension=1, tiled=True)
-    act_whole = lax.all_gather(act_sum.astype(jnp.bfloat16), "tensor", axis=1, tiled=True)
+    quarter = basis_in.shape[1] // tp
+    basis_cols = basis_in.reshape(basis_in.shape[0], tp, quarter).transpose(1, 0, 2).reshape(-1, quarter)
+    basis_q = lax.all_to_all(basis_cols, "tensor", 0, 0, tiled=True)
+    acts_full = lax.all_gather(acts_p, "tensor", axis=1, tiled=True)
+    act_q = jnp.dot(acts_full, basis_q, preferred_element_type=jnp.float32).astype(jnp.bfloat16)
+    act_whole = lax.all_gather(act_q, "tensor", axis=1, tiled=True)
     grad_part = jnp.dot(grads_p, basis_out, preferred_element_type=jnp.float32)
     grad_part, act_whole = lax.optimization_barrier((grad_part, act_whole))
     in_cols = act_whole.shape[1] // dp
@@ -140,9 +143,10 @@
 
 def solution(mesh):
     dp = mesh.shape["dp"]
+    tp = mesh.shape["tensor"]
 
     def body(*args):
-        return shards(*args, dp=dp)
+        return shards(*args, dp=dp, tp=tp)
 
     return jax.shard_map(
         body,

time: 406 us -> 451 us (1.11)
  waiting for transfers between devices: 287 us -> 324 us
  local copies, waits for them, and re-layouts: 14.3 us -> 19.3 us
    all_to_all x0 -> x1, waiting for transfers between devices: none -> 51.4 us  [shards(): basis_q = lax.all_to_all(basis_cols, 'tensor', 0, 0, tiled=True)]
    reduce_scatter x1 -> x0, waiting for transfers between devices: 18.3 us -> none  [shards(): lax.psum_scatter(act_part, 'tensor', scatter_dimension=1, tiled=True)]
    all_to_all x0 -> x1, starting transfers between devices: none -> 4.87 us  [shards(): basis_q = lax.all_to_all(basis_cols, 'tensor', 0, 0, tiled=True)]
    all_gather x1 -> x2, waiting for transfers between devices: 12.9 us -> 14 us  [the longest x1 14 us: shards(): act_whole = lax.all_gather(act_q, 'tensor', axis=1, tiled=True)]
  transfers between devices with their start and end apart: 6 -> 7, of which waited for: 5 -> 6; matrix products, arithmetic and copies ran while one was open for 10% -> 11% of each run, Pallas kernels for 0% -> 0%
where the time goes in v8:
time: 451 us
  waiting for transfers between devices  324 us (72%)
  matrix products  23.1 us (5%)
  blocking collectives  22.4 us (5%)
  Pallas kernels  20.2 us (4%)
  local copies, waits for them, and re-layouts  19.3 us (4%)
  other arithmetic  14.6 us (3%)
  starting transfers between devices  13.9 us (3%)
  between operations  13.3 us (3%)
    reduce_scatter x1, waiting for transfers between devices, shards(): lax.psum_scatter(grad_part, 'tensor', scatter_dimension=1, tiled=True)  164 us
    all_gather x1, waiting for transfers between devices, shards(): all_grads = lax.all_gather(rot_grads, 'dp', axis=0, tiled=True)  65.2 us
    all_to_all x1, waiting for transfers between devices, shards(): basis_q = lax.all_to_all(basis_cols, 'tensor', 0, 0, tiled=True)  51.4 us
    all_to_all x2, waiting for transfers between devices, redistribute(): return lax.all_to_all(x, 'dp', 0, 0, tiled=True)  29 us
    all_to_all x1, blocking collectives, shards(): rot_acts = lax.all_to_all(act_whole, 'dp', 0, 0, tiled=True)  22.4 us
    pallas_call x1, Pallas kernels, shards(): pl.pallas_call(kernel, out_shape=jax.ShapeDtypeStruct((out_rows, in_cols)...  20.2 us
    dot_general x1, matrix products, shards(): grad_part = jnp.dot(grads_p, basis_out, preferred_element_type=jnp.float32)  20.1 us
    all_gather x1, waiting for transfers between devices, shards(): act_whole = lax.all_gather(act_q, 'tensor', axis=1, tiled=True)  14 us
  transfers between devices with their start and end apart: 7, of which 6 were waited for; matrix products, arithmetic and copies ran while one was open for 11% of the time, Pallas kernels for 0%

profile of v8, /device:TPU:0, one launch (start us, length us, event | category | flops | bytes accessed | tf_op | source)
XLA Modules:
  0.0 450.6 jit_solution(4200377320936052459)
XLA Ops:
  6.5 2.1 copy.19
  8.7 5.2 %all-to-all-start.1 = ((bf16[8,64,512]{2,1,0:T(8,128)(2,1)}), bf16[8,64,512]{2,1,0:T(8,128)(2,1)S(1)}, u32[]{:S(2)}, u32[]{:S(2)}) async-start(bf16[8,64,512]{2,1,0:T(8,128)(2,1)} %bitcast.22), calls=%async_computation.1 | async-start | bytes 1048576 | tf_op jit(solution)/shard_map/all_to_all | solution.py:18
  13.9 2.5 copy.18
  16.4 7.2 %all-to-all-done.1 = bf16[8,64,512]{2,1,0:T(8,128)(2,1)S(1)} async-done(((bf16[8,64,512]{2,1,0:T(8,128)(2,1)}), bf16[8,64,512]{2,1,0:T(8,128)(2,1)S(1)}, u32[]{:S(2)}, u32[]{:S(2)}) %all-to-all-start.1) | async-done | bytes 524320 | tf_op jit(solution)/shard_map/all_to_all | solution.py:18
  23.6 3.7 all-to-all-start
  27.4 0.7 gather_fusion
  28.0 0.1 fusion.5
  28.2 3.9 copy.20
  32.1 21.8 %all-to-all-done = bf16[8,64,2048]{2,1,0:T(8,128)(2,1)S(1)} async-done(((bf16[8,64,2048]{2,1,0:T(8,128)(2,1)}), bf16[8,64,2048]{2,1,0:T(8,128)(2,1)S(1)}, u32[]{:S(2)}, u32[]{:S(2)}) %all-to-all-start) | async-done | bytes 2097184 | tf_op jit(solution)/shard_map/all_to_all | solution.py:18
  53.9 4.9 %all-to-all-start.2 = ((bf16[4,512,512]{1,2,0:T(8,128)(2,1)}), bf16[4,512,512]{1,2,0:T(8,128)(2,1)}, u32[]{:S(2)}, u32[]{:S(2)}) async-start(bf16[4,512,512]{1,2,0:T(8,128)(2,1)} %bitcast.43), calls=%async_computation.2 | async-start | bytes 4194304 | tf_op jit(solution)/shard_map/all_to_all | solution.py:105
  58.8 0.2 dynamic-slice_reduce_fusion
  58.9 0.7 fusion.12
  59.6 0.1 convert_reduce_fusion
  59.7 4.4 fusion.8
  64.2 5.6 %select_select_fusion = s32[336]{0:T(512)S(1)} fusion(pred[336]{0:T(512)(128)(4,1)S(1)} %get-tuple-element.21, pred[336]{0:T(512)(128)(4,1)S(1)} %get-tuple-element.20, pred[336]{0:T(512)(128)(4,1)S(1)} %get-tuple-element.19, pred[336]{0:T(512)(128)(4,1)S(1)} %get-tuple-element.18, pred[336]{0:T(512)(128)(4,1)S(1)} %get-tuple-element.17, ...), kind=kLoop, calls=%fused_computation.42 | loop fusion | flops 3024 | bytes 5748 | tf_op jit(solution)/shard_map/gather | solution.py:95
  69.8 2.6 gather_fusion.2
  72.5 2.4 gather_fusion.1
  74.9 51.4 %all-to-all-done.2 = bf16[4,512,512]{1,2,0:T(8,128)(2,1)} async-done(((bf16[4,512,512]{1,2,0:T(8,128)(2,1)}), bf16[4,512,512]{1,2,0:T(8,128)(2,1)}, u32[]{:S(2)}, u32[]{:S(2)}) %all-to-all-start.2) | async-done | bytes 2097184 | tf_op jit(solution)/shard_map/all_to_all | solution.py:105
  126.3 2.8 copy.21
  129.2 2.9 convolution_convert_fusion
  132.2 20.1 %fusion = f32[336,8192]{1,0:T(8,128)} fusion(bf16[2048,8192]{1,0:T(8,128)(2,1)} %param.8, bf16[336,2048]{1,0:T(8,128)(2,1)S(1)} %gather_fusion.1, pred[336]{0:T(512)(128)(4,1)S(1)} %broadcast_compare_fusion), kind=kOutput, calls=%fused_computation.4 | convolution fusion | flops 11274977280 | bytes 45941072 | tf_op jit(solution)/shard_map/dot_general | solution.py:109
  152.3 14.0 %all-gather.5.cloned.1.call-done = bf16[336,2048]{1,0:T(8,128)(2,1)} async-done(((bf16[336,512]{1,0:T(8,128)(2,1)}), bf16[336,2048]{1,0:T(8,128)(2,1)}) %all-gather.5.cloned.1.call-update) | async-done | bytes 1376272 | tf_op jit(solution)/shard_map/all_gather | solution.py:108
  166.3 1.3 copy-done.3
  167.6 0.1 copy.25
  167.7 22.4 %all_to_all.42 = bf16[8,336,256]{2,1,0:T(8,128)(2,1)} all-to-all(bf16[8,336,256]{2,1,0:T(8,128)(2,1)S(1)} %bitcast.46), channel_id=1, replica_groups=mesh['dp'=8,'tensor'=4] {'dp'}, dimensions={0} | all-to-all | bytes 2752512 | tf_op jit(solution)/shard_map/all_to_all | solution.py:113
  190.1 164.1 %reduce-scatter.2.cloned.1.call-done = f32[336,2048]{1,0:T(8,128)} async-done(((f32[336,8192]{1,0:T(8,128)}), f32[336,2048]{1,0:T(8,128)}) %reduce-scatter.2.cloned.1.call-update) | async-done | bytes 2752528 | tf_op jit(solution)/shard_map/reduce_scatter | solution.py:115
  354.2 3.1 convert_element_type.11
  357.4 0.1 sub.63
  357.5 0.5 fusion.11
  358.0 0.5 multiply_minimum_fusion.win_ref
  358.6 65.2 %all-gather.7.cloned.1.call-done.grads_hbm = bf16[2688,2048]{1,0:T(8,128)(2,1)} async-done(((bf16[336,2048]{1,0:T(8,128)(2,1)}), bf16[2688,2048]{1,0:T(8,128)(2,1)}) %all-gather.7.cloned.1.call-update) | async-done | bytes 11010064 | tf_op jit(solution)/shard_map/all_gather | solution.py:118
  423.8 20.2 %shard_map.64 = f32[2048,256]{1,0:T(8,128)} custom-call(s32[128]{0:T(128)} %multiply_minimum_fusion.win_ref, s32[128]{0:T(128)} %copy-done.4, s32[128]{0:T(128)} %get-tuple-element.24.hi_ref, bf16[2688,2048]{1,0:T(8,128)(2,1)} %all-gather.7.cloned.1.call-done.grads_hbm, bf16[2688,256]{1,0:T(8,128)(2,1)} %bitcast.45), custom_call_target="tpu_custom_call" | custom-call | tf_op jit(solution)/shard_map/pallas_call | solution.py:126
  (32 shorter events, 0.6 us)
Async XLA Ops:
  6.5 20.8 %copy-start = (s32[16]{0:T(128)S(1)}, s32[16]{0:T(128)}, u32[]{:S(2)}) copy-start(s32[16]{0:T(128)} %param.11) | copy-start | bytes 196
  6.5 7.3 %copy-start.2 = (bf16[512,2048]{1,0:T(8,128)(2,1)S(1)}, bf16[512,2048]{1,0:T(8,128)(2,1)}, u32[]{:S(2)}) copy-start(bf16[512,2048]{1,0:T(8,128)(2,1)} %param.7) | copy-start | bytes 6291460
  8.7 14.9 %all-to-all-start.1 = ((bf16[8,64,512]{2,1,0:T(8,128)(2,1)}), bf16[8,64,512]{2,1,0:T(8,128)(2,1)S(1)}, u32[]{:S(2)}, u32[]{:S(2)}) async-start(bf16[8,64,512]{2,1,0:T(8,128)(2,1)} %bitcast.22), calls=%async_computation.1 | async-start | bytes 1048576 | tf_op jit(solution)/shard_map/all_to_all | solution.py:18
  23.6 3.8 copy-start.5
  23.6 30.3 %all-to-all-start = ((bf16[8,64,2048]{2,1,0:T(8,128)(2,1)}), bf16[8,64,2048]{2,1,0:T(8,128)(2,1)S(1)}, u32[]{:S(2)}, u32[]{:S(2)}) async-start(bf16[8,64,2048]{2,1,0:T(8,128)(2,1)} %bitcast.44), calls=%async_computation | async-start | bytes 4194304 | tf_op jit(solution)/shard_map/all_to_all | solution.py:18
  53.9 72.5 %all-to-all-start.2 = ((bf16[4,512,512]{1,2,0:T(8,128)(2,1)}), bf16[4,512,512]{1,2,0:T(8,128)(2,1)}, u32[]{:S(2)}, u32[]{:S(2)}) async-start(bf16[4,512,512]{1,2,0:T(8,128)(2,1)} %bitcast.43), calls=%async_computation.2 | async-start | bytes 4194304 | tf_op jit(solution)/shard_map/all_to_all | solution.py:105
  58.8 70.4 %all-gather.9.cloned.1.call-start = ((), (), s32[]{:S(2)}) async-start(), calls=%async_computation.8 | async-start | bytes 1720320 | tf_op jit(solution)/shard_map/all_gather | solution.py:106
  72.4 93.9 %all-gather.5.cloned.1.call-start = ((), (), s32[]{:S(2)}) async-start(), calls=%async_computation.5 | async-start | bytes 1720320 | tf_op jit(solution)/shard_map/all_gather | solution.py:108
  132.1 222.0 %reduce-scatter.2.cloned.1.call-start = ((), (), s32[]{:S(2)}) async-start(), calls=%async_computation.6 | async-start | bytes 13762560 | tf_op jit(solution)/shard_map/reduce_scatter | solution.py:115
  166.3 1.3 copy-start.3
  166.3 257.5 %all-gather.7.cloned.1.call-start = ((), (), s32[]{:S(2)}) async-start(), calls=%async_computation.7 | async-start | bytes 12386304 | tf_op jit(solution)/shard_map/all_gather | solution.py:118
  358.0 65.7 %copy-start.4 = (s32[128]{0:T(128)}, s32[128]{0:T(128)S(1)}, u32[]{:S(2)}) copy-start(s32[128]{0:T(128)S(1)} %get-tuple-element.25.lo_ref) | copy-start | bytes 1540
  423.8 20.3 %copy-start.1 = (s32[16]{0:T(128)S(1)}, s32[16]{0:T(128)}, u32[]{:S(2)}) copy-start(s32[16]{0:T(128)} %param.11) | copy-start | bytes 196
Sparse Core Ops, SparseCore 0:
  72.5 53.0 all-gather.8
  132.3 33.9 all-gather.4
  168.6 185.5 reduce-scatter.1
  357.4 66.3 all-gather.6

commit v9 on v7

--- a/solution.py
+++ b/solution.py
@@ -101,14 +101,13 @@
     acts_p = jnp.take(acts_r, src, axis=0, mode="clip")
 
     act_part = jnp.dot(acts_p, basis_in, preferred_element_type=jnp.float32)
-    quarter = act_part.shape[1] // tp
-    blocks = act_part.reshape(cap, tp, quarter).transpose(1, 0, 2).reshape(-1, quarter)
-    act_sum = jnp.sum(lax.all_to_all(blocks, "tensor", 0, 0, tiled=True).reshape(tp, cap, quarter), axis=0)
-    act_sum = act_sum.astype(jnp.bfloat16)
+    act_sum = lax.psum_scatter(act_part, "tensor", scatter_dimension=1, tiled=True).astype(jnp.bfloat16)
+    grad_part = jnp.dot(grads_p, basis_out, preferred_element_type=jnp.float32)
+    grad_part, act_sum = lax.optimization_barrier((grad_part, act_sum))
+    quarter = act_sum.shape[1]
     sent = jnp.broadcast_to(act_sum[None], (tp,) + act_sum.shape).reshape(-1, quarter)
     act_whole = lax.all_to_all(sent, "tensor", 0, 0, tiled=True).reshape(tp, cap, quarter)
     act_whole = act_whole.transpose(1, 0, 2).reshape(cap, tp * quarter)
-    grad_part = jnp.dot(grads_p, basis_out, preferred_element_type=jnp.float32)
     in_cols = act_whole.shape[1] // dp
     act_whole = act_whole.reshape(cap, dp, in_cols).transpose(1, 0, 2).reshape(-1, in_cols)
     rot_acts = lax.all_to_all(act_whole, "dp", 0, 0, tiled=True)

time: 439 us -> 399 us (0.909)
  blocking collectives: 247 us -> 95.2 us
  waiting for transfers between devices: 95.2 us -> 204 us
    all_to_all x2 -> x0, blocking collectives: 153 us -> none  [the longest x1 141 us: shards(): lax.all_to_all(blocks, 'tensor', 0, 0, tiled=True).reshape(tp, cap, quarter)]
    reduce_scatter x1, waiting for transfers between devices: 8.68 us -> 106 us  [shards(): lax.psum_scatter(grad_part, 'tensor', scatter_dimension=1, tiled=True)]
    all_to_all x1 -> x2, waiting for transfers between devices: 14.8 us -> 26.6 us  [redistribute(): return lax.all_to_all(x, 'dp', 0, 0, tiled=True)]
    all_to_all x1 -> x2, starting transfers between devices: 5.33 us -> 9.35 us  [redistribute(): return lax.all_to_all(x, 'dp', 0, 0, tiled=True)]
  transfers between devices with their start and end apart: 3 -> 5, of which waited for: 3 -> 3; matrix products, arithmetic and copies ran while one was open for 5% -> 11% of each run, Pallas kernels for 0% -> 0%
where the time goes in v9:
time: 399 us; the launch traced here: 398 us
  waiting for transfers between devices  204 us (51%)
  blocking collectives  95.2 us (24%)
  matrix products  23 us (6%)
  Pallas kernels  20.2 us (5%)
  local copies, waits for them, and re-layouts  16.9 us (4%)
  other arithmetic  15.7 us (4%)
  between operations  13.3 us (3%)
  starting transfers between devices  9.46 us (2%)
    reduce_scatter x1, waiting for transfers between devices, shards(): lax.psum_scatter(grad_part, 'tensor', scatter_dimension=1, tiled=True)  106 us
    all_gather x1, waiting for transfers between devices, shards(): all_grads = lax.all_gather(rot_grads, 'dp', axis=0, tiled=True)  71.8 us
    all_to_all x1, blocking collectives, shards(): lax.all_to_all(sent, 'tensor', 0, 0, tiled=True).reshape(tp, cap, quarter)  71.7 us
    all_to_all x2, waiting for transfers between devices, redistribute(): return lax.all_to_all(x, 'dp', 0, 0, tiled=True)  26.6 us
    all_to_all x1, blocking collectives, shards(): rot_acts = lax.all_to_all(act_whole, 'dp', 0, 0, tiled=True)  23.5 us
    dot_general x1, matrix products, shards(): grad_part = jnp.dot(grads_p, basis_out, preferred_element_type=jnp.float32)  20.5 us
    pallas_call x1, Pallas kernels, shards(): pl.pallas_call(kernel, out_shape=jax.ShapeDtypeStruct((out_rows, in_cols)...  20.2 us
    gather x3, other arithmetic, shards(): src = jnp.clip(slot_c * per + rows - my_starts[slot_c], 0, nseq * per - 1)  10 us
  transfers between devices with their start and end apart: 5, of which 3 were waited for; matrix products, arithmetic and copies ran while one was open for 11% of the time, Pallas kernels for 0%

profile of v9, /device:TPU:0, one launch (start us, length us, event | category | flops | bytes accessed | tf_op | source)
XLA Modules:
  0.0 397.9 jit_solution(9441914471018960641)
XLA Ops:
  6.5 2.1 copy.17
  8.7 5.2 %all-to-all-start.1 = ((bf16[8,64,512]{2,1,0:T(8,128)(2,1)}), bf16[8,64,512]{2,1,0:T(8,128)(2,1)S(1)}, u32[]{:S(2)}, u32[]{:S(2)}) async-start(bf16[8,64,512]{2,1,0:T(8,128)(2,1)} %bitcast.22), calls=%async_computation.1 | async-start | bytes 1048576 | tf_op jit(solution)/shard_map/all_to_all | solution.py:18
  14.0 0.7 gather_fusion
  14.6 0.1 fusion.5
  14.8 0.2 dynamic-slice_reduce_fusion
  14.9 0.1 convert_reduce_fusion
  15.1 0.6 fusion.12
  15.7 4.3 %fusion.8 = (s32[336]{0:T(512)S(1)}, s32[336,1]{0,1:T(1,128)S(1)}) fusion(s32[]{:T(128)} %bitcast.13, s32[]{:T(128)} %bitcast.14, s32[]{:T(128)} %bitcast.15, s32[]{:T(128)} %bitcast.16, s32[]{:T(128)} %bitcast.17, s32[]{:T(128)} %bitcast.19, s32[]{:T(128)} %bitcast.18, s32[336]{0:T(512)S(1)} %broadcast_minimum_fusion), kind=kLoop, calls=%fused_computation.43 | loop fusion | flops 5040 | bytes 4060 | tf_op jit(solution)/shard_map/gather | solution.py:95
  20.0 5.7 %select_select_fusion = s32[336]{0:T(512)S(1)} fusion(pred[336]{0:T(512)(128)(4,1)S(1)} %get-tuple-element.21, pred[336]{0:T(512)(128)(4,1)S(1)} %get-tuple-element.20, pred[336]{0:T(512)(128)(4,1)S(1)} %get-tuple-element.19, pred[336]{0:T(512)(128)(4,1)S(1)} %get-tuple-element.18, pred[336]{0:T(512)(128)(4,1)S(1)} %get-tuple-element.17, ...), kind=kLoop, calls=%fused_computation.40 | loop fusion | flops 3024 | bytes 5748 | tf_op jit(solution)/shard_map/gather | solution.py:95
  25.8 2.0 gather_fusion.2
  27.8 2.5 fusion.13
  30.4 1.6 copy-done.3
  31.9 2.5 copy.16
  34.4 4.1 %all-to-all-start = ((bf16[8,64,2048]{2,1,0:T(8,128)(2,1)}), bf16[8,64,2048]{2,1,0:T(8,128)(2,1)S(1)}, u32[]{:S(2)}, u32[]{:S(2)}) async-start(bf16[8,64,2048]{2,1,0:T(8,128)(2,1)} %bitcast.34), calls=%async_computation | async-start | bytes 4194304 | tf_op jit(solution)/shard_map/all_to_all | solution.py:18
  38.6 26.6 %all-to-all-done = bf16[8,64,2048]{2,1,0:T(8,128)(2,1)S(1)} async-done(((bf16[8,64,2048]{2,1,0:T(8,128)(2,1)}), bf16[8,64,2048]{2,1,0:T(8,128)(2,1)S(1)}, u32[]{:S(2)}, u32[]{:S(2)}) %all-to-all-start) | async-done | bytes 2097184 | tf_op jit(solution)/shard_map/all_to_all | solution.py:18
  65.2 3.0 gather_fusion.1
  68.2 20.5 %fusion = f32[336,8192]{1,0:T(8,128)} fusion(bf16[2048,8192]{1,0:T(8,128)(2,1)} %param.8, bf16[336,2048]{1,0:T(8,128)(2,1)} %gather_fusion.1, pred[336]{0:T(512)(128)(4,1)S(1)} %broadcast_compare_fusion), kind=kOutput, calls=%fused_computation.3 | convolution fusion | flops 11274977280 | bytes 45941072 | tf_op jit(solution)/shard_map/dot_general | solution.py:105
  88.7 1.1 convert_element_type.10
  89.9 0.1 broadcast_in_dim.21
  90.0 71.7 %all_to_all.39 = bf16[4,336,512]{2,1,0:T(8,128)(2,1)S(1)} all-to-all(bf16[4,336,512]{2,1,0:T(8,128)(2,1)S(1)} %broadcast_in_dim.21), channel_id=1, replica_groups=mesh['dp'=8,'tensor'=4] {'tensor'}, dimensions={0} | all-to-all | bytes 2752512 | tf_op jit(solution)/shard_map/all_to_all | solution.py:109
  161.7 1.1 copy.18
  162.8 1.3 reshape_reshape.3
  164.0 1.6 copy.19
  165.6 23.5 %all_to_all.40 = bf16[8,336,256]{2,1,0:T(8,128)(2,1)} all-to-all(bf16[8,336,256]{2,1,0:T(8,128)(2,1)S(1)} %copy.19), channel_id=1, replica_groups=mesh['dp'=8,'tensor'=4] {'dp'}, dimensions={0} | all-to-all | bytes 2752512 | tf_op jit(solution)/shard_map/all_to_all | solution.py:113
  189.1 105.9 %reduce-scatter.5.cloned.1.call-done = f32[336,2048]{1,0:T(8,128)} async-done(((f32[336,8192]{1,0:T(8,128)}), f32[336,2048]{1,0:T(8,128)}) %reduce-scatter.5.cloned.1.call-update) | async-done | bytes 2752528 | tf_op jit(solution)/shard_map/reduce_scatter | solution.py:115
  295.0 3.1 convert_element_type.11
  298.1 0.1 reduce_window_sum.14
  298.3 0.1 sub.63
  298.4 0.5 fusion.11
  298.9 0.5 multiply_minimum_fusion.win_ref
  299.4 71.8 %all-gather.2.cloned.1.call-done.grads_hbm = bf16[2688,2048]{1,0:T(8,128)(2,1)} async-done(((bf16[336,2048]{1,0:T(8,128)(2,1)}), bf16[2688,2048]{1,0:T(8,128)(2,1)}) %all-gather.2.cloned.1.call-update) | async-done | bytes 11010064 | tf_op jit(solution)/shard_map/all_gather | solution.py:118
  371.2 20.2 %shard_map.64 = f32[2048,256]{1,0:T(8,128)} custom-call(s32[128]{0:T(128)} %multiply_minimum_fusion.win_ref, s32[128]{0:T(128)} %copy-done.4, s32[128]{0:T(128)} %get-tuple-element.24.hi_ref, bf16[2688,2048]{1,0:T(8,128)(2,1)} %all-gather.2.cloned.1.call-done.grads_hbm, bf16[2688,256]{1,0:T(8,128)(2,1)} %bitcast.35), custom_call_target="tpu_custom_call" | custom-call | tf_op jit(solution)/shard_map/pallas_call | solution.py:126
  (30 shorter events, 0.4 us)
Async XLA Ops:
  6.5 21.3 %copy-start = (bf16[512,2048]{1,0:T(8,128)(2,1)S(1)}, bf16[512,2048]{1,0:T(8,128)(2,1)}, u32[]{:S(2)}) copy-start(bf16[512,2048]{1,0:T(8,128)(2,1)} %param.9) | copy-start | bytes 6291460
  6.5 7.4 %copy-start.5 = (s32[16]{0:T(128)S(1)}, s32[16]{0:T(128)}, u32[]{:S(2)}) copy-start(s32[16]{0:T(128)} %param.10) | copy-start | bytes 196
  6.5 7.4 %copy-start.2 = (s32[16]{0:T(128)S(1)}, s32[16]{0:T(128)}, u32[]{:S(2)}) copy-start(s32[16]{0:T(128)} %param.11) | copy-start | bytes 196
  8.7 17.1 %all-to-all-start.1 = ((bf16[8,64,512]{2,1,0:T(8,128)(2,1)}), bf16[8,64,512]{2,1,0:T(8,128)(2,1)S(1)}, u32[]{:S(2)}, u32[]{:S(2)}) async-start(bf16[8,64,512]{2,1,0:T(8,128)(2,1)} %bitcast.22), calls=%async_computation.1 | async-start | bytes 1048576 | tf_op jit(solution)/shard_map/all_to_all | solution.py:18
  13.9 74.8 %reduce-scatter.3.cloned.1.call-start = ((), (), s32[]{:S(2)}) async-start(), calls=%async_computation.6 | async-start | bytes 3440640 | tf_op jit(solution)/shard_map/reduce_scatter | solution.py:104
  30.3 1.6 copy-start.3
  34.4 30.8 %all-to-all-start = ((bf16[8,64,2048]{2,1,0:T(8,128)(2,1)}), bf16[8,64,2048]{2,1,0:T(8,128)(2,1)S(1)}, u32[]{:S(2)}, u32[]{:S(2)}) async-start(bf16[8,64,2048]{2,1,0:T(8,128)(2,1)} %bitcast.34), calls=%async_computation | async-start | bytes 4194304 | tf_op jit(solution)/shard_map/all_to_all | solution.py:18
  38.5 256.5 %reduce-scatter.5.cloned.1.call-start = ((), (), s32[]{:S(2)}) async-start(), calls=%async_computation.7 | async-start | bytes 13762560 | tf_op jit(solution)/shard_map/reduce_scatter | solution.py:115
  89.9 281.4 %all-gather.2.cloned.1.call-start = ((), (), s32[]{:S(2)}) async-start(), calls=%async_computation.8 | async-start | bytes 12386304 | tf_op jit(solution)/shard_map/all_gather | solution.py:118
  298.9 72.4 %copy-start.4 = (s32[128]{0:T(128)}, s32[128]{0:T(128)S(1)}, u32[]{:S(2)}) copy-start(s32[128]{0:T(128)S(1)} %get-tuple-element.25.lo_ref) | copy-start | bytes 1540
  371.2 20.2 %copy-start.1 = (bf16[512,2048]{1,0:T(8,128)(2,1)S(1)}, bf16[512,2048]{1,0:T(8,128)(2,1)}, u32[]{:S(2)}) copy-start(bf16[512,2048]{1,0:T(8,128)(2,1)} %param.9) | copy-start | bytes 6291460
Sparse Core Ops, SparseCore 0:
  30.5 55.9 reduce-scatter.2
  90.0 204.9 reduce-scatter.4
  298.2 72.9 all-gather.1

commit v10 on v9

--- a/solution.py
+++ b/solution.py
@@ -100,8 +100,13 @@
     acts_r = redistribute(acts, dp)
     acts_p = jnp.take(acts_r, src, axis=0, mode="clip")
 
-    act_part = jnp.dot(acts_p, basis_in, preferred_element_type=jnp.float32)
-    act_sum = lax.psum_scatter(act_part, "tensor", scatter_dimension=1, tiled=True).astype(jnp.bfloat16)
+    quarter = basis_in.shape[1] // tp
+    basis_cols = basis_in.reshape(basis_in.shape[0], tp, quarter).transpose(1, 0, 2).reshape(-1, quarter)
+    basis_q = lax.all_to_all(basis_cols, "tensor", 0, 0, tiled=True)
+    copies = jnp.broadcast_to(acts_p[None], (tp,) + acts_p.shape).reshape(-1, acts_p.shape[1])
+    acts_full = lax.all_to_all(copies, "tensor", 0, 0, tiled=True).reshape(tp, cap, acts_p.shape[1])
+    acts_full = acts_full.transpose(1, 0, 2).reshape(cap, -1)
+    act_sum = jnp.dot(acts_full, basis_q, preferred_element_type=jnp.float32).astype(jnp.bfloat16)
     grad_part = jnp.dot(grads_p, basis_out, preferred_element_type=jnp.float32)
     grad_part, act_sum = lax.optimization_barrier((grad_part, act_sum))
     quarter = act_sum.shape[1]

time: 399 us -> 455 us (1.14)
  waiting for transfers between devices: 204 us -> 247 us
  starting transfers between devices: 9.46 us -> 18.4 us
  local copies, waits for them, and re-layouts: 16.9 us -> 22.8 us
    all_to_all x0 -> x2, waiting for transfers between devices: none -> 46.9 us  [the longest x1 25.1 us: shards(): basis_q = lax.all_to_all(basis_cols, 'tensor', 0, 0, tiled=True)]
    all_to_all x0 -> x2, starting transfers between devices: none -> 9.37 us  [the longest x1 4.87 us: shards(): lax.all_to_all(copies, 'tensor', 0, 0, tiled=True)]
    all_to_all x2, waiting for transfers between devices: 26.6 us -> 19.9 us  [redistribute(): return lax.all_to_all(x, 'dp', 0, 0, tiled=True)]
  transfers between devices with their start and end apart: 5 -> 6, of which waited for: 3 -> 6; matrix products, arithmetic and copies ran while one was open for 11% -> 11% of each run, Pallas kernels for 0% -> 0%
where the time goes in v10:
time: 455 us
  waiting for transfers between devices  247 us (54%)
  blocking collectives  95.2 us (21%)
  local copies, waits for them, and re-layouts  22.8 us (5%)
  matrix products  22.7 us (5%)
  Pallas kernels  21.2 us (5%)
  starting transfers between devices  18.4 us (4%)
  other arithmetic  14.5 us (3%)
  between operations  13.6 us (3%)
    reduce_scatter x1, waiting for transfers between devices, shards(): lax.psum_scatter(grad_part, 'tensor', scatter_dimension=1, tiled=True)  108 us
    all_gather x1, waiting for transfers between devices, shards(): all_grads = lax.all_gather(rot_grads, 'dp', axis=0, tiled=True)  71.8 us
    all_to_all x1, blocking collectives, shards(): lax.all_to_all(sent, 'tensor', 0, 0, tiled=True).reshape(tp, cap, quarter)  71 us
    all_to_all x1, waiting for transfers between devices, shards(): basis_q = lax.all_to_all(basis_cols, 'tensor', 0, 0, tiled=True)  25.1 us
    all_to_all x1, blocking collectives, shards(): rot_acts = lax.all_to_all(act_whole, 'dp', 0, 0, tiled=True)  24.1 us
    all_to_all x1, waiting for transfers between devices, shards(): lax.all_to_all(copies, 'tensor', 0, 0, tiled=True)  21.8 us
    pallas_call x1, Pallas kernels, shards(): pl.pallas_call(kernel, out_shape=jax.ShapeDtypeStruct((out_rows, in_cols)...  21.2 us
    dot_general x1, matrix products, shards(): grad_part = jnp.dot(grads_p, basis_out, preferred_element_type=jnp.float32)  20.2 us
  transfers between devices with their start and end apart: 6, of which 6 were waited for; matrix products, arithmetic and copies ran while one was open for 11% of the time, Pallas kernels for 0%

profile of v10, /device:TPU:0, one launch (start us, length us, event | category | flops | bytes accessed | tf_op | source)
XLA Modules:
  0.0 455.2 jit_solution(17708584009780971077)
XLA Ops:
  6.5 2.1 copy.21
  8.7 5.2 %all-to-all-start.1 = ((bf16[8,64,512]{2,1,0:T(8,128)(2,1)}), bf16[8,64,512]{2,1,0:T(8,128)(2,1)S(1)}, u32[]{:S(2)}, u32[]{:S(2)}) async-start(bf16[8,64,512]{2,1,0:T(8,128)(2,1)} %bitcast.22), calls=%async_computation.1 | async-start | bytes 1048576 | tf_op jit(solution)/shard_map/all_to_all | solution.py:18
  13.9 2.5 copy.20
  16.4 7.2 %all-to-all-done.1 = bf16[8,64,512]{2,1,0:T(8,128)(2,1)S(1)} async-done(((bf16[8,64,512]{2,1,0:T(8,128)(2,1)}), bf16[8,64,512]{2,1,0:T(8,128)(2,1)S(1)}, u32[]{:S(2)}, u32[]{:S(2)}) %all-to-all-start.1) | async-done | bytes 524320 | tf_op jit(solution)/shard_map/all_to_all | solution.py:18
  23.6 3.7 all-to-all-start
  27.4 0.7 gather_fusion
  28.4 0.7 fusion.20
  29.1 4.3 fusion.16
  33.4 5.7 %select_select_fusion = s32[336]{0:T(512)S(1)} fusion(pred[336]{0:T(512)(128)(4,1)S(1)} %get-tuple-element.21, pred[336]{0:T(512)(128)(4,1)S(1)} %get-tuple-element.20, pred[336]{0:T(512)(128)(4,1)S(1)} %get-tuple-element.19, pred[336]{0:T(512)(128)(4,1)S(1)} %get-tuple-element.18, pred[336]{0:T(512)(128)(4,1)S(1)} %get-tuple-element.17, ...), kind=kLoop, calls=%fused_computation.44 | loop fusion | flops 3024 | bytes 5748 | tf_op jit(solution)/shard_map/gather | solution.py:95
  39.2 2.0 gather_fusion.2
  41.2 12.7 %all-to-all-done = bf16[8,64,2048]{2,1,0:T(8,128)(2,1)S(1)} async-done(((bf16[8,64,2048]{2,1,0:T(8,128)(2,1)}), bf16[8,64,2048]{2,1,0:T(8,128)(2,1)S(1)}, u32[]{:S(2)}, u32[]{:S(2)}) %all-to-all-start) | async-done | bytes 2097184 | tf_op jit(solution)/shard_map/all_to_all | solution.py:18
  53.9 1.2 broadcast_in_dim.23
  55.1 4.9 %all-to-all-start.2 = ((bf16[4,336,512]{2,1,0:T(8,128)(2,1)}), bf16[4,336,512]{2,1,0:T(8,128)(2,1)S(1)}, u32[]{:S(2)}, u32[]{:S(2)}) async-start(bf16[4,336,512]{2,1,0:T(8,128)(2,1)} %broadcast_in_dim.23), calls=%async_computation.2 | async-start | bytes 2752512 | tf_op jit(solution)/shard_map/all_to_all | solution.py:107
  59.9 3.9 copy.22
  63.9 4.2 copy.23
  68.0 21.8 %all-to-all-done.2 = bf16[4,336,512]{2,1,0:T(8,128)(2,1)S(1)} async-done(((bf16[4,336,512]{2,1,0:T(8,128)(2,1)}), bf16[4,336,512]{2,1,0:T(8,128)(2,1)S(1)}, u32[]{:S(2)}, u32[]{:S(2)}) %all-to-all-start.2) | async-done | bytes 1376288 | tf_op jit(solution)/shard_map/all_to_all | solution.py:107
  89.9 1.1 copy-done.3
  90.9 4.5 all-to-all-start.3
  95.5 2.4 gather_fusion.1
  98.0 20.2 %fusion.2 = f32[336,8192]{1,0:T(8,128)} fusion(bf16[2048,8192]{1,0:T(8,128)(2,1)} %param.8, bf16[336,2048]{1,0:T(8,128)(2,1)S(1)} %gather_fusion.1, pred[336]{0:T(512)(128)(4,1)S(1)} %broadcast_compare_fusion), kind=kOutput, calls=%fused_computation.5 | convolution fusion | flops 11274977280 | bytes 45941072 | tf_op jit(solution)/shard_map/dot_general | solution.py:110
  118.2 25.1 %all-to-all-done.3 = bf16[4,512,512]{2,1,0:T(8,128)(2,1)} async-done(((bf16[4,512,512]{2,1,0:T(8,128)(2,1)}), bf16[4,512,512]{2,1,0:T(8,128)(2,1)}, u32[]{:S(2)}, u32[]{:S(2)}) %all-to-all-start.3) | async-done | bytes 2097184 | tf_op jit(solution)/shard_map/all_to_all | solution.py:105
  143.3 2.5 fusion.8
  145.9 71.0 %all_to_all.51 = bf16[4,336,512]{2,1,0:T(8,128)(2,1)S(1)} all-to-all(bf16[4,336,512]{2,1,0:T(8,128)(2,1)S(1)} %broadcast_in_dim.24), channel_id=1, replica_groups=mesh['dp'=8,'tensor'=4] {'tensor'}, dimensions={0} | all-to-all | bytes 2752512 | tf_op jit(solution)/shard_map/all_to_all | solution.py:114
  217.0 1.1 copy.24
  218.0 0.4 reshape_reshape.3
  218.7 24.1 %all_to_all.52 = bf16[8,336,256]{2,1,0:T(8,128)(2,1)} all-to-all(bf16[8,336,256]{2,1,0:T(8,128)(2,1)S(1)} %copy.25), channel_id=1, replica_groups=mesh['dp'=8,'tensor'=4] {'dp'}, dimensions={0} | all-to-all | bytes 2752512 | tf_op jit(solution)/shard_map/all_to_all | solution.py:118
  242.8 108.1 %reduce-scatter.2.cloned.1.call-done = f32[336,2048]{1,0:T(8,128)} async-done(((f32[336,8192]{1,0:T(8,128)}), f32[336,2048]{1,0:T(8,128)}) %reduce-scatter.2.cloned.1.call-update) | async-done | bytes 2752528 | tf_op jit(solution)/shard_map/reduce_scatter | solution.py:120
  350.9 3.1 convert_element_type.11
  354.3 0.5 fusion.19
  354.8 0.5 multiply_minimum_fusion.win_ref
  355.3 71.8 %all-gather.2.cloned.1.call-done.grads_hbm = bf16[2688,2048]{1,0:T(8,128)(2,1)} async-done(((bf16[336,2048]{1,0:T(8,128)(2,1)}), bf16[2688,2048]{1,0:T(8,128)(2,1)}) %all-gather.2.cloned.1.call-update) | async-done | bytes 11010064 | tf_op jit(solution)/shard_map/all_gather | solution.py:123
  427.1 21.2 %shard_map.64 = f32[2048,256]{1,0:T(8,128)} custom-call(s32[128]{0:T(128)} %multiply_minimum_fusion.win_ref, s32[128]{0:T(128)} %copy-done.5, s32[128]{0:T(128)} %get-tuple-element.24.hi_ref, bf16[2688,2048]{1,0:T(8,128)(2,1)} %all-gather.2.cloned.1.call-done.grads_hbm, bf16[2688,256]{1,0:T(8,128)(2,1)} %bitcast.49), custom_call_target="tpu_custom_call" | custom-call | tf_op jit(solution)/shard_map/pallas_call | solution.py:131
  (35 shorter events, 1.3 us)
Async XLA Ops:
  6.5 20.8 %copy-start = (s32[16]{0:T(128)S(1)}, s32[16]{0:T(128)}, u32[]{:S(2)}) copy-start(s32[16]{0:T(128)} %param.11) | copy-start | bytes 196
  6.5 7.3 %copy-start.2 = (bf16[512,2048]{1,0:T(8,128)(2,1)S(1)}, bf16[512,2048]{1,0:T(8,128)(2,1)}, u32[]{:S(2)}) copy-start(bf16[512,2048]{1,0:T(8,128)(2,1)} %param.7) | copy-start | bytes 6291460
  8.7 14.9 %all-to-all-start.1 = ((bf16[8,64,512]{2,1,0:T(8,128)(2,1)}), bf16[8,64,512]{2,1,0:T(8,128)(2,1)S(1)}, u32[]{:S(2)}, u32[]{:S(2)}) async-start(bf16[8,64,512]{2,1,0:T(8,128)(2,1)} %bitcast.22), calls=%async_computation.1 | async-start | bytes 1048576 | tf_op jit(solution)/shard_map/all_to_all | solution.py:18
  23.6 3.8 copy-start.6
  23.6 30.3 %all-to-all-start = ((bf16[8,64,2048]{2,1,0:T(8,128)(2,1)}), bf16[8,64,2048]{2,1,0:T(8,128)(2,1)S(1)}, u32[]{:S(2)}, u32[]{:S(2)}) async-start(bf16[8,64,2048]{2,1,0:T(8,128)(2,1)} %bitcast.46), calls=%async_computation | async-start | bytes 4194304 | tf_op jit(solution)/shard_map/all_to_all | solution.py:18
  55.1 34.8 %all-to-all-start.2 = ((bf16[4,336,512]{2,1,0:T(8,128)(2,1)}), bf16[4,336,512]{2,1,0:T(8,128)(2,1)S(1)}, u32[]{:S(2)}, u32[]{:S(2)}) async-start(bf16[4,336,512]{2,1,0:T(8,128)(2,1)} %broadcast_in_dim.23), calls=%async_computation.2 | async-start | bytes 2752512 | tf_op jit(solution)/shard_map/all_to_all | solution.py:107
  89.9 1.1 copy-start.3
  90.9 52.3 %all-to-all-start.3 = ((bf16[4,512,512]{2,1,0:T(8,128)(2,1)}), bf16[4,512,512]{2,1,0:T(8,128)(2,1)}, u32[]{:S(2)}, u32[]{:S(2)}) async-start(bf16[4,512,512]{2,1,0:T(8,128)(2,1)} %bitcast.47), calls=%async_computation.3 | async-start | bytes 4194304 | tf_op jit(solution)/shard_map/all_to_all | solution.py:105
  95.4 255.5 %reduce-scatter.2.cloned.1.call-start = ((), (), s32[]{:S(2)}) async-start(), calls=%async_computation.7 | async-start | bytes 13762560 | tf_op jit(solution)/shard_map/reduce_scatter | solution.py:120
  98.0 45.3 %copy-start.4 = (bf16[4,336,512]{2,1,0:T(8,128)(2,1)S(1)}, bf16[4,336,512]{2,1,0:T(8,128)(2,1)}, u32[]{:S(2)}) copy-start(bf16[4,336,512]{2,1,0:T(8,128)(2,1)} %copy-done.3) | copy-start | bytes 4128772
  145.8 281.3 %all-gather.2.cloned.1.call-start = ((), (), s32[]{:S(2)}) async-start(), calls=%async_computation.8 | async-start | bytes 12386304 | tf_op jit(solution)/shard_map/all_gather | solution.py:123
  354.8 72.3 %copy-start.5 = (s32[128]{0:T(128)}, s32[128]{0:T(128)S(1)}, u32[]{:S(2)}) copy-start(s32[128]{0:T(128)S(1)} %get-tuple-element.25.lo_ref) | copy-start | bytes 1540
  427.1 21.3 %copy-start.1 = (s32[16]{0:T(128)S(1)}, s32[16]{0:T(128)}, u32[]{:S(2)}) copy-start(s32[16]{0:T(128)} %param.11) | copy-start | bytes 196
Sparse Core Ops, SparseCore 0:
  145.9 204.9 reduce-scatter.1
  354.1 72.9 all-gather.1

commit v11 on v9

--- a/solution.py
+++ b/solution.py
@@ -121,7 +121,7 @@
     lo = groups[None, :] * cap + starts
     win = jnp.minimum((lo // 16) * 16, dp * cap - span)
     out_rows, in_cols = all_grads.shape[1], rot_acts.shape[1]
-    pair = 2 if nseq % 2 == 0 else 1
+    pair = 4 if nseq % 4 == 0 else 1
     kernel = functools.partial(slot_squares, dp=dp, per=span, pair=pair, scale=1.0 / (nseq * LEN))
     return pl.pallas_call(
         kernel,

time: 399 us -> 399 us (level)
  no operation moved by 1% of the time
where the time goes in v11:
time: 399 us; the launch traced here: 398 us
  waiting for transfers between devices  204 us (51%)
  blocking collectives  95.2 us (24%)
  matrix products  23 us (6%)
  Pallas kernels  19.7 us (5%)
  local copies, waits for them, and re-layouts  16.9 us (4%)
  other arithmetic  15.7 us (4%)
  between operations  13.3 us (3%)
  starting transfers between devices  9.46 us (2%)
    reduce_scatter x1, waiting for transfers between devices, shards(): lax.psum_scatter(grad_part, 'tensor', scatter_dimension=1, tiled=True)  106 us
    all_gather x1, waiting for transfers between devices, shards(): all_grads = lax.all_gather(rot_grads, 'dp', axis=0, tiled=True)  71.8 us
    all_to_all x1, blocking collectives, shards(): lax.all_to_all(sent, 'tensor', 0, 0, tiled=True).reshape(tp, cap, quarter)  71.7 us
    all_to_all x2, waiting for transfers between devices, redistribute(): return lax.all_to_all(x, 'dp', 0, 0, tiled=True)  26.6 us
    all_to_all x1, blocking collectives, shards(): rot_acts = lax.all_to_all(act_whole, 'dp', 0, 0, tiled=True)  23.5 us
    dot_general x1, matrix products, shards(): grad_part = jnp.dot(grads_p, basis_out, preferred_element_type=jnp.float32)  20.5 us
    pallas_call x1, Pallas kernels, shards(): pl.pallas_call(kernel, out_shape=jax.ShapeDtypeStruct((out_rows, in_cols)...  19.7 us
    gather x3, other arithmetic, shards(): src = jnp.clip(slot_c * per + rows - my_starts[slot_c], 0, nseq * per - 1)  10 us
  transfers between devices with their start and end apart: 5, of which 3 were waited for; matrix products, arithmetic and copies ran while one was open for 11% of the time, Pallas kernels for 0%

profile of v11, /device:TPU:0, one launch (start us, length us, event | category | flops | bytes accessed | tf_op | source)
XLA Modules:
  0.0 397.5 jit_solution(10642039190331959521)
XLA Ops:
  6.5 2.1 copy.17
  8.7 5.2 %all-to-all-start.1 = ((bf16[8,64,512]{2,1,0:T(8,128)(2,1)}), bf16[8,64,512]{2,1,0:T(8,128)(2,1)S(1)}, u32[]{:S(2)}, u32[]{:S(2)}) async-start(bf16[8,64,512]{2,1,0:T(8,128)(2,1)} %bitcast.22), calls=%async_computation.1 | async-start | bytes 1048576 | tf_op jit(solution)/shard_map/all_to_all | solution.py:18
  14.0 0.7 gather_fusion
  14.6 0.1 fusion.5
  14.8 0.2 dynamic-slice_reduce_fusion
  14.9 0.1 convert_reduce_fusion
  15.1 0.6 fusion.12
  15.7 4.3 %fusion.8 = (s32[336]{0:T(512)S(1)}, s32[336,1]{0,1:T(1,128)S(1)}) fusion(s32[]{:T(128)} %bitcast.13, s32[]{:T(128)} %bitcast.14, s32[]{:T(128)} %bitcast.15, s32[]{:T(128)} %bitcast.16, s32[]{:T(128)} %bitcast.17, s32[]{:T(128)} %bitcast.19, s32[]{:T(128)} %bitcast.18, s32[336]{0:T(512)S(1)} %broadcast_minimum_fusion), kind=kLoop, calls=%fused_computation.43 | loop fusion | flops 5040 | bytes 4060 | tf_op jit(solution)/shard_map/gather | solution.py:95
  20.0 5.7 %select_select_fusion = s32[336]{0:T(512)S(1)} fusion(pred[336]{0:T(512)(128)(4,1)S(1)} %get-tuple-element.21, pred[336]{0:T(512)(128)(4,1)S(1)} %get-tuple-element.20, pred[336]{0:T(512)(128)(4,1)S(1)} %get-tuple-element.19, pred[336]{0:T(512)(128)(4,1)S(1)} %get-tuple-element.18, pred[336]{0:T(512)(128)(4,1)S(1)} %get-tuple-element.17, ...), kind=kLoop, calls=%fused_computation.40 | loop fusion | flops 3024 | bytes 5748 | tf_op jit(solution)/shard_map/gather | solution.py:95
  25.8 2.0 gather_fusion.2
  27.8 2.5 fusion.13
  30.4 1.6 copy-done.3
  31.9 2.5 copy.16
  34.4 4.1 %all-to-all-start = ((bf16[8,64,2048]{2,1,0:T(8,128)(2,1)}), bf16[8,64,2048]{2,1,0:T(8,128)(2,1)S(1)}, u32[]{:S(2)}, u32[]{:S(2)}) async-start(bf16[8,64,2048]{2,1,0:T(8,128)(2,1)} %bitcast.34), calls=%async_computation | async-start | bytes 4194304 | tf_op jit(solution)/shard_map/all_to_all | solution.py:18
  38.6 26.6 %all-to-all-done = bf16[8,64,2048]{2,1,0:T(8,128)(2,1)S(1)} async-done(((bf16[8,64,2048]{2,1,0:T(8,128)(2,1)}), bf16[8,64,2048]{2,1,0:T(8,128)(2,1)S(1)}, u32[]{:S(2)}, u32[]{:S(2)}) %all-to-all-start) | async-done | bytes 2097184 | tf_op jit(solution)/shard_map/all_to_all | solution.py:18
  65.2 3.0 gather_fusion.1
  68.2 20.5 %fusion = f32[336,8192]{1,0:T(8,128)} fusion(bf16[2048,8192]{1,0:T(8,128)(2,1)} %param.8, bf16[336,2048]{1,0:T(8,128)(2,1)} %gather_fusion.1, pred[336]{0:T(512)(128)(4,1)S(1)} %broadcast_compare_fusion), kind=kOutput, calls=%fused_computation.3 | convolution fusion | flops 11274977280 | bytes 45941072 | tf_op jit(solution)/shard_map/dot_general | solution.py:105
  88.7 1.1 convert_element_type.10
  89.9 0.1 broadcast_in_dim.21
  90.0 71.7 %all_to_all.39 = bf16[4,336,512]{2,1,0:T(8,128)(2,1)S(1)} all-to-all(bf16[4,336,512]{2,1,0:T(8,128)(2,1)S(1)} %broadcast_in_dim.21), channel_id=1, replica_groups=mesh['dp'=8,'tensor'=4] {'tensor'}, dimensions={0} | all-to-all | bytes 2752512 | tf_op jit(solution)/shard_map/all_to_all | solution.py:109
  161.7 1.1 copy.18
  162.8 1.3 reshape_reshape.3
  164.0 1.6 copy.19
  165.6 23.5 %all_to_all.40 = bf16[8,336,256]{2,1,0:T(8,128)(2,1)} all-to-all(bf16[8,336,256]{2,1,0:T(8,128)(2,1)S(1)} %copy.19), channel_id=1, replica_groups=mesh['dp'=8,'tensor'=4] {'dp'}, dimensions={0} | all-to-all | bytes 2752512 | tf_op jit(solution)/shard_map/all_to_all | solution.py:113
  189.1 105.9 %reduce-scatter.5.cloned.1.call-done = f32[336,2048]{1,0:T(8,128)} async-done(((f32[336,8192]{1,0:T(8,128)}), f32[336,2048]{1,0:T(8,128)}) %reduce-scatter.5.cloned.1.call-update) | async-done | bytes 2752528 | tf_op jit(solution)/shard_map/reduce_scatter | solution.py:115
  295.0 3.1 convert_element_type.11
  298.1 0.1 reduce_window_sum.14
  298.3 0.1 sub.63
  298.4 0.5 fusion.11
  298.9 0.5 multiply_minimum_fusion.win_ref
  299.4 71.8 %all-gather.2.cloned.1.call-done.grads_hbm = bf16[2688,2048]{1,0:T(8,128)(2,1)} async-done(((bf16[336,2048]{1,0:T(8,128)(2,1)}), bf16[2688,2048]{1,0:T(8,128)(2,1)}) %all-gather.2.cloned.1.call-update) | async-done | bytes 11010064 | tf_op jit(solution)/shard_map/all_gather | solution.py:118
  371.2 19.7 %shard_map.64 = f32[2048,256]{1,0:T(8,128)} custom-call(s32[128]{0:T(128)} %multiply_minimum_fusion.win_ref, s32[128]{0:T(128)} %copy-done.4, s32[128]{0:T(128)} %get-tuple-element.24.hi_ref, bf16[2688,2048]{1,0:T(8,128)(2,1)} %all-gather.2.cloned.1.call-done.grads_hbm, bf16[2688,256]{1,0:T(8,128)(2,1)} %bitcast.35), custom_call_target="tpu_custom_call" | custom-call | tf_op jit(solution)/shard_map/pallas_call | solution.py:126
  (30 shorter events, 0.4 us)
Async XLA Ops:
  6.5 21.3 %copy-start = (bf16[512,2048]{1,0:T(8,128)(2,1)S(1)}, bf16[512,2048]{1,0:T(8,128)(2,1)}, u32[]{:S(2)}) copy-start(bf16[512,2048]{1,0:T(8,128)(2,1)} %param.9) | copy-start | bytes 6291460
  6.5 7.4 %copy-start.5 = (s32[16]{0:T(128)S(1)}, s32[16]{0:T(128)}, u32[]{:S(2)}) copy-start(s32[16]{0:T(128)} %param.10) | copy-start | bytes 196
  6.5 7.4 %copy-start.2 = (s32[16]{0:T(128)S(1)}, s32[16]{0:T(128)}, u32[]{:S(2)}) copy-start(s32[16]{0:T(128)} %param.11) | copy-start | bytes 196
  8.7 17.1 %all-to-all-start.1 = ((bf16[8,64,512]{2,1,0:T(8,128)(2,1)}), bf16[8,64,512]{2,1,0:T(8,128)(2,1)S(1)}, u32[]{:S(2)}, u32[]{:S(2)}) async-start(bf16[8,64,512]{2,1,0:T(8,128)(2,1)} %bitcast.22), calls=%async_computation.1 | async-start | bytes 1048576 | tf_op jit(solution)/shard_map/all_to_all | solution.py:18
  13.9 74.8 %reduce-scatter.3.cloned.1.call-start = ((), (), s32[]{:S(2)}) async-start(), calls=%async_computation.6 | async-start | bytes 3440640 | tf_op jit(solution)/shard_map/reduce_scatter | solution.py:104
  30.3 1.6 copy-start.3
  34.4 30.8 %all-to-all-start = ((bf16[8,64,2048]{2,1,0:T(8,128)(2,1)}), bf16[8,64,2048]{2,1,0:T(8,128)(2,1)S(1)}, u32[]{:S(2)}, u32[]{:S(2)}) async-start(bf16[8,64,2048]{2,1,0:T(8,128)(2,1)} %bitcast.34), calls=%async_computation | async-start | bytes 4194304 | tf_op jit(solution)/shard_map/all_to_all | solution.py:18
  38.5 256.5 %reduce-scatter.5.cloned.1.call-start = ((), (), s32[]{:S(2)}) async-start(), calls=%async_computation.7 | async-start | bytes 13762560 | tf_op jit(solution)/shard_map/reduce_scatter | solution.py:115
  89.9 281.4 %all-gather.2.cloned.1.call-start = ((), (), s32[]{:S(2)}) async-start(), calls=%async_computation.8 | async-start | bytes 12386304 | tf_op jit(solution)/shard_map/all_gather | solution.py:118
  298.9 72.4 %copy-start.4 = (s32[128]{0:T(128)}, s32[128]{0:T(128)S(1)}, u32[]{:S(2)}) copy-start(s32[128]{0:T(128)S(1)} %get-tuple-element.25.lo_ref) | copy-start | bytes 1540
  371.2 19.7 %copy-start.1 = (bf16[512,2048]{1,0:T(8,128)(2,1)S(1)}, bf16[512,2048]{1,0:T(8,128)(2,1)}, u32[]{:S(2)}) copy-start(bf16[512,2048]{1,0:T(8,128)(2,1)} %param.9) | copy-start | bytes 6291460
Sparse Core Ops, SparseCore 0:
  30.5 55.9 reduce-scatter.2
  90.0 204.9 reduce-scatter.4
  298.2 72.9 all-gather.1

commit v12 on v11

--- a/solution.py
+++ b/solution.py
@@ -121,7 +121,7 @@
     lo = groups[None, :] * cap + starts
     win = jnp.minimum((lo // 16) * 16, dp * cap - span)
     out_rows, in_cols = all_grads.shape[1], rot_acts.shape[1]
-    pair = 4 if nseq % 4 == 0 else 1
+    pair = 8 if nseq % 8 == 0 else 1
     kernel = functools.partial(slot_squares, dp=dp, per=span, pair=pair, scale=1.0 / (nseq * LEN))
     return pl.pallas_call(
         kernel,

time: 399 us -> 402 us (level)
  no operation moved by 1% of the time
where the time goes in v12:
time: 402 us; the launch traced here: 401 us
  waiting for transfers between devices  204 us (51%)
  blocking collectives  95.2 us (24%)
  matrix products  23 us (6%)
  Pallas kernels  22.9 us (6%)
  local copies, waits for them, and re-layouts  16.9 us (4%)
  other arithmetic  15.7 us (4%)
  between operations  13.3 us (3%)
  starting transfers between devices  9.46 us (2%)
    reduce_scatter x1, waiting for transfers between devices, shards(): lax.psum_scatter(grad_part, 'tensor', scatter_dimension=1, tiled=True)  106 us
    all_gather x1, waiting for transfers between devices, shards(): all_grads = lax.all_gather(rot_grads, 'dp', axis=0, tiled=True)  71.8 us
    all_to_all x1, blocking collectives, shards(): lax.all_to_all(sent, 'tensor', 0, 0, tiled=True).reshape(tp, cap, quarter)  71.7 us
    all_to_all x2, waiting for transfers between devices, redistribute(): return lax.all_to_all(x, 'dp', 0, 0, tiled=True)  26.6 us
    all_to_all x1, blocking collectives, shards(): rot_acts = lax.all_to_all(act_whole, 'dp', 0, 0, tiled=True)  23.5 us
    pallas_call x1, Pallas kernels, shards(): pl.pallas_call(kernel, out_shape=jax.ShapeDtypeStruct((out_rows, in_cols)...  22.9 us
    dot_general x1, matrix products, shards(): grad_part = jnp.dot(grads_p, basis_out, preferred_element_type=jnp.float32)  20.5 us
    gather x3, other arithmetic, shards(): src = jnp.clip(slot_c * per + rows - my_starts[slot_c], 0, nseq * per - 1)  10 us
  transfers between devices with their start and end apart: 5, of which 3 were waited for; matrix products, arithmetic and copies ran while one was open for 11% of the time, Pallas kernels for 0%

profile of v12, /device:TPU:0, one launch (start us, length us, event | category | flops | bytes accessed | tf_op | source)
XLA Modules:
  0.0 400.7 jit_solution(10661706077092240425)
XLA Ops:
  6.5 2.1 copy.17
  8.7 5.2 %all-to-all-start.1 = ((bf16[8,64,512]{2,1,0:T(8,128)(2,1)}), bf16[8,64,512]{2,1,0:T(8,128)(2,1)S(1)}, u32[]{:S(2)}, u32[]{:S(2)}) async-start(bf16[8,64,512]{2,1,0:T(8,128)(2,1)} %bitcast.22), calls=%async_computation.1 | async-start | bytes 1048576 | tf_op jit(solution)/shard_map/all_to_all | solution.py:18
  14.0 0.7 gather_fusion
  14.6 0.1 fusion.5
  14.8 0.2 dynamic-slice_reduce_fusion
  14.9 0.1 convert_reduce_fusion
  15.1 0.6 fusion.12
  15.7 4.3 %fusion.8 = (s32[336]{0:T(512)S(1)}, s32[336,1]{0,1:T(1,128)S(1)}) fusion(s32[]{:T(128)} %bitcast.13, s32[]{:T(128)} %bitcast.14, s32[]{:T(128)} %bitcast.15, s32[]{:T(128)} %bitcast.16, s32[]{:T(128)} %bitcast.17, s32[]{:T(128)} %bitcast.19, s32[]{:T(128)} %bitcast.18, s32[336]{0:T(512)S(1)} %broadcast_minimum_fusion), kind=kLoop, calls=%fused_computation.43 | loop fusion | flops 5040 | bytes 4060 | tf_op jit(solution)/shard_map/gather | solution.py:95
  20.0 5.7 %select_select_fusion = s32[336]{0:T(512)S(1)} fusion(pred[336]{0:T(512)(128)(4,1)S(1)} %get-tuple-element.21, pred[336]{0:T(512)(128)(4,1)S(1)} %get-tuple-element.20, pred[336]{0:T(512)(128)(4,1)S(1)} %get-tuple-element.19, pred[336]{0:T(512)(128)(4,1)S(1)} %get-tuple-element.18, pred[336]{0:T(512)(128)(4,1)S(1)} %get-tuple-element.17, ...), kind=kLoop, calls=%fused_computation.40 | loop fusion | flops 3024 | bytes 5748 | tf_op jit(solution)/shard_map/gather | solution.py:95
  25.8 2.0 gather_fusion.2
  27.8 2.5 fusion.13
  30.4 1.6 copy-done.3
  31.9 2.5 copy.16
  34.4 4.1 %all-to-all-start = ((bf16[8,64,2048]{2,1,0:T(8,128)(2,1)}), bf16[8,64,2048]{2,1,0:T(8,128)(2,1)S(1)}, u32[]{:S(2)}, u32[]{:S(2)}) async-start(bf16[8,64,2048]{2,1,0:T(8,128)(2,1)} %bitcast.34), calls=%async_computation | async-start | bytes 4194304 | tf_op jit(solution)/shard_map/all_to_all | solution.py:18
  38.6 26.6 %all-to-all-done = bf16[8,64,2048]{2,1,0:T(8,128)(2,1)S(1)} async-done(((bf16[8,64,2048]{2,1,0:T(8,128)(2,1)}), bf16[8,64,2048]{2,1,0:T(8,128)(2,1)S(1)}, u32[]{:S(2)}, u32[]{:S(2)}) %all-to-all-start) | async-done | bytes 2097184 | tf_op jit(solution)/shard_map/all_to_all | solution.py:18
  65.2 3.0 gather_fusion.1
  68.2 20.5 %fusion = f32[336,8192]{1,0:T(8,128)} fusion(bf16[2048,8192]{1,0:T(8,128)(2,1)} %param.8, bf16[336,2048]{1,0:T(8,128)(2,1)} %gather_fusion.1, pred[336]{0:T(512)(128)(4,1)S(1)} %broadcast_compare_fusion), kind=kOutput, calls=%fused_computation.3 | convolution fusion | flops 11274977280 | bytes 45941072 | tf_op jit(solution)/shard_map/dot_general | solution.py:105
  88.7 1.1 convert_element_type.10
  89.9 0.1 broadcast_in_dim.21
  90.0 71.7 %all_to_all.39 = bf16[4,336,512]{2,1,0:T(8,128)(2,1)S(1)} all-to-all(bf16[4,336,512]{2,1,0:T(8,128)(2,1)S(1)} %broadcast_in_dim.21), channel_id=1, replica_groups=mesh['dp'=8,'tensor'=4] {'tensor'}, dimensions={0} | all-to-all | bytes 2752512 | tf_op jit(solution)/shard_map/all_to_all | solution.py:109
  161.7 1.1 copy.18
  162.8 1.3 reshape_reshape.3
  164.0 1.6 copy.19
  165.6 23.5 %all_to_all.40 = bf16[8,336,256]{2,1,0:T(8,128)(2,1)} all-to-all(bf16[8,336,256]{2,1,0:T(8,128)(2,1)S(1)} %copy.19), channel_id=1, replica_groups=mesh['dp'=8,'tensor'=4] {'dp'}, dimensions={0} | all-to-all | bytes 2752512 | tf_op jit(solution)/shard_map/all_to_all | solution.py:113
  189.1 105.9 %reduce-scatter.5.cloned.1.call-done = f32[336,2048]{1,0:T(8,128)} async-done(((f32[336,8192]{1,0:T(8,128)}), f32[336,2048]{1,0:T(8,128)}) %reduce-scatter.5.cloned.1.call-update) | async-done | bytes 2752528 | tf_op jit(solution)/shard_map/reduce_scatter | solution.py:115
  295.0 3.1 convert_element_type.11
  298.2 0.1 add.69
  298.3 0.1 sub.63
  298.4 0.5 fusion.11
  298.9 0.5 multiply_minimum_fusion.win_ref
  299.4 71.8 %all-gather.2.cloned.1.call-done.grads_hbm = bf16[2688,2048]{1,0:T(8,128)(2,1)} async-done(((bf16[336,2048]{1,0:T(8,128)(2,1)}), bf16[2688,2048]{1,0:T(8,128)(2,1)}) %all-gather.2.cloned.1.call-update) | async-done | bytes 11010064 | tf_op jit(solution)/shard_map/all_gather | solution.py:118
  371.2 22.9 %shard_map.64 = f32[2048,256]{1,0:T(8,128)} custom-call(s32[128]{0:T(128)} %multiply_minimum_fusion.win_ref, s32[128]{0:T(128)} %copy-done.4, s32[128]{0:T(128)} %get-tuple-element.24.hi_ref, bf16[2688,2048]{1,0:T(8,128)(2,1)} %all-gather.2.cloned.1.call-done.grads_hbm, bf16[2688,256]{1,0:T(8,128)(2,1)} %bitcast.35), custom_call_target="tpu_custom_call" | custom-call | tf_op jit(solution)/shard_map/pallas_call | solution.py:126
  (30 shorter events, 0.4 us)
Async XLA Ops:
  6.5 21.3 %copy-start = (bf16[512,2048]{1,0:T(8,128)(2,1)S(1)}, bf16[512,2048]{1,0:T(8,128)(2,1)}, u32[]{:S(2)}) copy-start(bf16[512,2048]{1,0:T(8,128)(2,1)} %param.9) | copy-start | bytes 6291460
  6.5 7.4 %copy-start.5 = (s32[16]{0:T(128)S(1)}, s32[16]{0:T(128)}, u32[]{:S(2)}) copy-start(s32[16]{0:T(128)} %param.10) | copy-start | bytes 196
  6.5 7.4 %copy-start.2 = (s32[16]{0:T(128)S(1)}, s32[16]{0:T(128)}, u32[]{:S(2)}) copy-start(s32[16]{0:T(128)} %param.11) | copy-start | bytes 196
  8.7 17.1 %all-to-all-start.1 = ((bf16[8,64,512]{2,1,0:T(8,128)(2,1)}), bf16[8,64,512]{2,1,0:T(8,128)(2,1)S(1)}, u32[]{:S(2)}, u32[]{:S(2)}) async-start(bf16[8,64,512]{2,1,0:T(8,128)(2,1)} %bitcast.22), calls=%async_computation.1 | async-start | bytes 1048576 | tf_op jit(solution)/shard_map/all_to_all | solution.py:18
  13.9 74.8 %reduce-scatter.3.cloned.1.call-start = ((), (), s32[]{:S(2)}) async-start(), calls=%async_computation.6 | async-start | bytes 3440640 | tf_op jit(solution)/shard_map/reduce_scatter | solution.py:104
  30.3 1.6 copy-start.3
  34.4 30.8 %all-to-all-start = ((bf16[8,64,2048]{2,1,0:T(8,128)(2,1)}), bf16[8,64,2048]{2,1,0:T(8,128)(2,1)S(1)}, u32[]{:S(2)}, u32[]{:S(2)}) async-start(bf16[8,64,2048]{2,1,0:T(8,128)(2,1)} %bitcast.34), calls=%async_computation | async-start | bytes 4194304 | tf_op jit(solution)/shard_map/all_to_all | solution.py:18
  38.5 256.5 %reduce-scatter.5.cloned.1.call-start = ((), (), s32[]{:S(2)}) async-start(), calls=%async_computation.7 | async-start | bytes 13762560 | tf_op jit(solution)/shard_map/reduce_scatter | solution.py:115
  89.9 281.4 %all-gather.2.cloned.1.call-start = ((), (), s32[]{:S(2)}) async-start(), calls=%async_computation.8 | async-start | bytes 12386304 | tf_op jit(solution)/shard_map/all_gather | solution.py:118
  298.9 72.4 %copy-start.4 = (s32[128]{0:T(128)}, s32[128]{0:T(128)S(1)}, u32[]{:S(2)}) copy-start(s32[128]{0:T(128)S(1)} %get-tuple-element.25.lo_ref) | copy-start | bytes 1540
  371.2 22.9 %copy-start.1 = (bf16[512,2048]{1,0:T(8,128)(2,1)S(1)}, bf16[512,2048]{1,0:T(8,128)(2,1)}, u32[]{:S(2)}) copy-start(bf16[512,2048]{1,0:T(8,128)(2,1)} %param.9) | copy-start | bytes 6291460
Sparse Core Ops, SparseCore 0:
  30.5 55.9 reduce-scatter.2
  90.0 204.9 reduce-scatter.4
  298.2 72.9 all-gather.1
